TPU v7x, 32 devices: a whole 2x2x4 slice. The times are simulated.
32 devices in a mesh: groups: 2 (over y), freq: 4 (over z), tile: 4 (over x, core).
Axes of the slice: x: 2, y: 2, z: 4, core: 2. Of those that a mesh axis runs over, the one named last changes fastest.
Arguments:
- traces: bfloat16 [640, 32, 16384], P('freq', 'groups', 'tile'), parts along dimension 1, may hold values from -6 to 6
- v_factors: bfloat16 [4, 2, 32, 64, 8, 256], P('freq', None, None, 'tile'), may hold values from -0.375 to 0.375
- u_factors: bfloat16 [4, 2, 32, 64, 8, 256], P('freq', None, 'tile'), may hold values from -0.25 to 0.25
- ranks: int32 [4, 32, 64], P('freq', None, 'tile'), may hold values from 1 to 8
Outputs:
- convolved: bfloat16 [640, 32, 8192], P('freq', 'groups', 'tile'), parts along dimension 1
There are 2 independent parts, one for each index of `groups`. A program takes and returns all parts, laid end to end along the dimension named above; an argument that names none is the same for every part. Nothing has to cross between parts.
All inputs are finite; a program needn't handle non-finite values.
Results may differ from a plain program's by a relative error of at most 0.0074.
Values may be sent and summed in bfloat16 or wider, within the bound.
No kernel may reach another device: no remote copies, remote signals or barrier semaphores. Data moves between devices by JAX's collectives and lax.ppermute only.
A program may use at most 192 MiB of HBM per device.

v0:
```python
import math

import jax
import jax.numpy as jnp
from jax import lax
from jax.sharding import PartitionSpec as P

NT = 640
F0 = 40


def twiddle(freq_ids, time_ids):
    turns = (F0 + freq_ids)[:, None] * time_ids[None, :] % NT
    angle = turns.astype(jnp.float32) * (2.0 * math.pi / NT)
    return (jnp.cos(angle).astype(jnp.bfloat16), jnp.sin(angle).astype(jnp.bfloat16))


def spread_over(weights, count):
    eye = jnp.eye(count, dtype=weights.dtype)
    rows, cols = weights.shape
    return (weights[:, None, :, None] * eye[None, :, None, :]).reshape(rows * count, cols * count)


def per_device(traces, v_factors, u_factors, ranks):
    time_count = traces.shape[0]
    virtual_sources = traces.shape[1]
    source_count = traces.shape[2]
    freq_local = v_factors.shape[0]
    freq_total = freq_local * lax.axis_size("freq")
    tile_width = v_factors.shape[5]
    rank_positions = v_factors.shape[4]
    rows_all = v_factors.shape[2]
    columns = v_factors.shape[3]
    time_ids = lax.axis_index("freq") * time_count + jnp.arange(time_count, dtype=jnp.int32)
    scale_time = 1.0 / math.sqrt(NT)
    freq_ids = jnp.arange(freq_total, dtype=jnp.int32)
    cosine, sine = twiddle(freq_ids, time_ids)

    forward = jnp.stack([cosine, -sine], 1).reshape(freq_total * 2, time_count)
    flat_traces = traces.reshape(time_count * virtual_sources, source_count)
    partial = jnp.dot(
        spread_over(forward, virtual_sources), flat_traces, preferred_element_type=jnp.float32
    ).reshape(freq_total, 2, virtual_sources, source_count)
    summed = lax.psum_scatter(partial, "freq", scatter_dimension=0, tiled=True)
    spectrum = (summed * scale_time).astype(jnp.bfloat16)[0]
    spectral_tiles = spectrum.reshape(2, virtual_sources, columns, tile_width)
    emitter_factors = v_factors[0]

    def source_product(left_operand_factors, right_operand_factors):
        return jnp.einsum(
            "ajrs,vjs->ajrv",
            left_operand_factors,
            right_operand_factors,
            preferred_element_type=jnp.float32,
        )

    real_coeff = source_product(emitter_factors[0], spectral_tiles[0]) - source_product(
        emitter_factors[1], spectral_tiles[1]
    )
    imag_coeff = source_product(emitter_factors[0], spectral_tiles[1]) + source_product(
        emitter_factors[1], spectral_tiles[0]
    )
    rank_mask = (
        jnp.arange(rank_positions, dtype=jnp.int32)[None, None, :, None]
        < ranks[0][:, :, None, None]
    )
    stacked = jnp.stack([real_coeff, imag_coeff])
    coefficients = jnp.where(rank_mask[None], stacked, jnp.float32(0.0)).astype(jnp.bfloat16)
    coefficients = coefficients.reshape(2, rows_all, columns, rank_positions * virtual_sources)
    arrived = lax.all_to_all(coefficients, "tile", split_axis=1, concat_axis=2, tiled=True)
    rows_local = arrived.shape[1]
    columns_all = arrived.shape[2]
    arrived = arrived.reshape(2, rows_local, columns_all, rank_positions, virtual_sources)
    receiver_factors = u_factors[0]

    def receiver_product(left_operand_factors, right_operand_factors):
        return jnp.einsum(
            "mdlh,mdlu->umh",
            left_operand_factors,
            right_operand_factors,
            preferred_element_type=jnp.float32,
        )

    real_recv = receiver_product(receiver_factors[0], arrived[0]) - receiver_product(
        receiver_factors[1], arrived[1]
    )
    imag_recv = receiver_product(receiver_factors[0], arrived[1]) + receiver_product(
        receiver_factors[1], arrived[0]
    )
    receivers = rows_local * tile_width
    received = (
        jnp.stack([real_recv, imag_recv])
        .reshape(1, 2, virtual_sources, receivers)
        .astype(jnp.bfloat16)
    )
    piece = lax.all_gather(received, "freq", axis=0, tiled=True)
    count = piece.shape[0]

    backward = jnp.stack([cosine.T, -sine.T], 2).reshape(time_count, count * 2)
    added = jnp.dot(
        spread_over(backward, virtual_sources),
        piece.reshape(count * 2 * virtual_sources, receivers),
        preferred_element_type=jnp.float32,
    )
    scale_freq = 1.0 / math.sqrt(freq_total)
    return (added * scale_freq).astype(jnp.bfloat16).reshape(time_count, virtual_sources, receivers)


def solution(mesh):
    placed = (
        P("freq", "groups", "tile"),
        P("freq", None, None, "tile", None, None),
        P("freq", None, "tile", None, None, None),
        P("freq", None, "tile"),
    )
    return jax.shard_map(
        per_device,
        mesh=mesh,
        in_specs=placed,
        out_specs=P("freq", "groups", "tile"),
        check_vma=False,
    )
```

profile of v0, /device:TPU:0, one launch (start us, length us, event | category | flops | bytes accessed | tf_op | source)
XLA Modules:
  0.0 121.3 jit_solution(4675950118513015756)
XLA Ops:
  6.5 0.1 fusion.41
  6.9 0.2 mul.161
  7.1 0.4 mul.162
  7.6 0.9 mul.165
  8.5 11.2 %fusion.20 = f32[4,2,16,4096]{3,2,1,0:T(8,128)} fusion(bf16[2560,4096,1,1]{1,0,3,2:T(8,128)(2,1)} %bitcast.115, bf16[16,2560]{1,0:T(8,128)(2,1)S(1)} %mul.165, bf16[4,2,2560]{2,1,0:T(2,128)(2,1)S(1)} %mul.162), kind=kOutput, calls=%fused_computation.26 | convolution fusion | flops 2684682240 | bytes 23191552 | tf_op jit(solution)/shard_map/dot_general | solution.py:41
  20.1 0.2 copy-done.4
  20.5 0.4 copy.99
  20.8 2.8 %broadcast_multiply_fusion = bf16[160,16,8,16]{3,2,1,0:T(8,128)(2,1)} fusion(bf16[16,16]{1,0:T(8,128)(2,1)S(1)} %fusion.29, bf16[160,8]{1,0:T(8,128)(2,1)S(1)} %copy.98), kind=kLoop, calls=%fused_computation.1 | loop fusion | flops 327680 | bytes 658432 | tf_op jit(solution)/shard_map/mul | solution.py:21
  23.6 6.8 %mul.154 = bf16[2560,128]{1,0:T(8,128)(2,1)} reshape(bf16[160,16,8,16]{3,2,1,0:T(8,128)(2,1)} %broadcast_multiply_fusion) | data formatting | bytes 1310720 | tf_op jit(solution)/shard_map/mul | solution.py:21
  30.4 3.9 %fusion.43 = (bf16[1,1,32,16,8,256]{5,4,3,2,1,0:T(8,128)(2,1)S(1)}, bf16[1,1,32,16,8,256]{5,4,3,2,1,0:T(8,128)(2,1)}) fusion(bf16[1,2,32,16,8,256]{5,4,3,2,1,0:T(8,128)(2,1)} %param.5), kind=kLoop, calls=%fused_computation.66 | loop fusion | bytes 8388608 | tf_op jit(solution)/shard_map/slice | solution.py:58
  34.3 32.1 %reduce-scatter.2.cloned.1.call-done = f32[1,2,16,4096]{3,2,1,0:T(8,128)} async-done(((f32[4,2,16,4096]{3,2,1,0:T(8,128)}), f32[1,2,16,4096]{3,2,1,0:T(8,128)}) %reduce-scatter.2.cloned.1.call-update) | async-done | bytes 524304 | tf_op jit(solution)/shard_map/reduce_scatter | solution.py:44
  66.4 1.1 multiply_convert_fusion.1
  67.6 3.2 %fusion = f32[16,16,32,8]{2,1,3,0:T(8,128)S(1)} fusion(bf16[1,1,32,16,8,256]{5,4,3,2,1,0:T(8,128)(2,1)} %get-tuple-element.8, bf16[16,16,256,1]{2,1,0,3:T(8,128)(2,1)S(1)} %bitcast.119), kind=kOutput, calls=%fused_computation.6 | convolution fusion | flops 33554432 | bytes 2490368 | tf_op jit(solution)/shard_map/ajrs,vjs->ajrv/dot_general | solution.py:50
  70.8 1.5 %fusion.1 = f32[16,16,32,8]{2,1,3,0:T(8,128)S(1)} fusion(bf16[1,1,32,16,8,256]{5,4,3,2,1,0:T(8,128)(2,1)S(1)} %copy-done, bf16[16,16,256,1]{2,1,0,3:T(8,128)(2,1)S(1)} %bitcast.121), kind=kOutput, calls=%fused_computation.7 | convolution fusion | flops 33554432 | bytes 2490368 | tf_op jit(solution)/shard_map/ajrs,vjs->ajrv/dot_general | solution.py:50
  72.4 1.5 %fusion.9 = bf16[16,16,32,8]{2,1,3,0:T(8,128)(2,1)S(1)} fusion(f32[16,16,32,8]{2,1,3,0:T(8,128)S(1)} %fusion, bf16[1,1,32,16,8,256]{5,4,3,2,1,0:T(8,128)(2,1)S(1)} %get-tuple-element.7, bf16[16,16,256,1]{2,1,0,3:T(8,128)(2,1)S(1)} %bitcast.122), kind=kOutput, calls=%fused_computation.15 | convolution fusion | flops 33685504 | bytes 2621440 | tf_op jit(solution)/shard_map/ajrs,vjs->ajrv/dot_general | solution.py:50
  73.9 1.5 %fusion.8 = bf16[16,16,32,8]{2,1,3,0:T(8,128)(2,1)S(1)} fusion(f32[16,16,32,8]{2,1,3,0:T(8,128)S(1)} %fusion.1, bf16[1,1,32,16,8,256]{5,4,3,2,1,0:T(8,128)(2,1)S(1)} %get-tuple-element.7, bf16[16,16,256,1]{2,1,0,3:T(8,128)(2,1)S(1)} %bitcast.120), kind=kOutput, calls=%fused_computation.14 | convolution fusion | flops 33685504 | bytes 2621440 | tf_op jit(solution)/shard_map/ajrs,vjs->ajrv/dot_general | solution.py:50
  75.4 0.2 copy.107
  75.6 0.2 copy.108
  75.9 0.8 fusion.22
  76.7 3.4 %all-to-all-start = ((bf16[2,32,16,128]{3,2,0,1:T(8,128)(2,1)}), bf16[2,32,16,128]{3,2,0,1:T(8,128)(2,1)S(1)}, u32[]{:S(2)}, u32[]{:S(2)}) async-start(bf16[2,32,16,128]{3,2,0,1:T(8,128)(2,1)} %fusion.22), calls=%async_computation.1 | async-start | bytes 524288 | tf_op jit(solution)/shard_map/all_to_all | solution.py:70
  80.1 3.9 %fusion.42 = (bf16[1,1,8,64,8,256]{5,4,3,2,1,0:T(8,128)(2,1)S(1)}, bf16[1,1,8,64,8,256]{5,4,3,2,1,0:T(8,128)(2,1)}) fusion(bf16[1,2,8,64,8,256]{5,4,3,2,1,0:T(8,128)(2,1)} %param.6), kind=kLoop, calls=%fused_computation.65 | loop fusion | bytes 8388608 | tf_op jit(solution)/shard_map/slice | solution.py:84
  83.9 2.1 %all-to-all-done = bf16[2,32,16,128]{3,2,0,1:T(8,128)(2,1)S(1)} async-done(((bf16[2,32,16,128]{3,2,0,1:T(8,128)(2,1)}), bf16[2,32,16,128]{3,2,0,1:T(8,128)(2,1)S(1)}, u32[]{:S(2)}, u32[]{:S(2)}) %all-to-all-start) | async-done | bytes 262176 | tf_op jit(solution)/shard_map/all_to_all | solution.py:70
  86.1 0.7 copy.138
  86.8 0.5 reshape.371
  87.3 0.7 copy.137
  88.0 1.2 %reshape.370 = bf16[8,64,8,16]{1,3,2,0:T(8,128)(2,1)} reshape(bf16[1,8,4,16,128]{3,2,4,1,0:T(4,128)(2,1)S(1)} %copy.137) | data formatting | bytes 262144 | tf_op jit(solution)/shard_map/squeeze | solution.py:84
  89.2 2.3 %fusion.11 = f32[8,16,256]{2,1,0:T(8,128)S(1)} fusion(bf16[8,64,8,16]{1,3,2,0:T(8,128)(2,1)} %reshape.370, bf16[1,1,8,64,8,256]{5,4,3,2,1,0:T(8,128)(2,1)} %get-tuple-element.6), kind=kOutput, calls=%fused_computation.17 | convolution fusion | flops 33554432 | bytes 2359296 | tf_op jit(solution)/shard_map/mdlh,mdlu->umh/dot_general | solution.py:77
  91.5 0.5 fusion.10
  92.0 0.5 fusion.18
  92.5 0.5 fusion.19
  93.1 15.7 %all_gather.3 = bf16[4,2,16,2048]{3,2,1,0:T(8,128)(2,1)S(1)} all-gather(bf16[1,2,16,2048]{3,2,1,0:T(8,128)(2,1)S(1)} %pad_maximum_fusion), channel_id=1, replica_groups=mesh['groups'=2,'freq'=4,'tile'=4] {'freq'}, dimensions={0}, use_global_device_ids=true | all-gather | bytes 655360 | tf_op jit(solution)/shard_map/all_gather | solution.py:96
  108.8 5.6 %multiply_convert_fusion = bf16[2560,2048]{1,0:T(8,128)(2,1)} fusion(bf16[2560,128]{1,0:T(8,128)(2,1)S(1)} %copy-done.1, bf16[128,2048]{1,0:T(8,128)(2,1)S(1)} %bitcast.116), kind=kOutput, calls=%fused_computation | convolution fusion | flops 1352663040 | bytes 11665408 | tf_op jit(solution)/shard_map/dot_general | solution.py:100
  (37 shorter events, 1.1 us)
Async XLA Ops:
  6.5 59.9 %reduce-scatter.2.cloned.1.call-start = ((), (), s32[]{:S(2)}) async-start(), calls=%async_computation.2 | async-start | bytes 2621440 | tf_op jit(solution)/shard_map/reduce_scatter | solution.py:44
  19.7 0.7 copy-start.4
  67.5 3.3 %copy-start = (bf16[1,1,32,16,8,256]{5,4,3,2,1,0:T(8,128)(2,1)S(1)}, bf16[1,1,32,16,8,256]{5,4,3,2,1,0:T(8,128)(2,1)}, u32[]{:S(2)}) copy-start(bf16[1,1,32,16,8,256]{5,4,3,2,1,0:T(8,128)(2,1)} %get-tuple-element.8) | copy-start | bytes 6291460
  76.7 9.4 %all-to-all-start = ((bf16[2,32,16,128]{3,2,0,1:T(8,128)(2,1)}), bf16[2,32,16,128]{3,2,0,1:T(8,128)(2,1)S(1)}, u32[]{:S(2)}, u32[]{:S(2)}) async-start(bf16[2,32,16,128]{3,2,0,1:T(8,128)(2,1)} %fusion.22), calls=%async_computation.1 | async-start | bytes 524288 | tf_op jit(solution)/shard_map/all_to_all | solution.py:70
  89.2 2.3 %copy-start.2 = (bf16[1,1,8,64,8,256]{5,4,3,2,1,0:T(8,128)(2,1)S(1)}, bf16[1,1,8,64,8,256]{5,4,3,2,1,0:T(8,128)(2,1)}, u32[]{:S(2)}) copy-start(bf16[1,1,8,64,8,256]{5,4,3,2,1,0:T(8,128)(2,1)} %get-tuple-element.6) | copy-start | bytes 6291460
  91.5 1.0 copy-start.3
  92.5 16.3 %copy-start.1 = (bf16[2560,128]{1,0:T(8,128)(2,1)S(1)}, bf16[2560,128]{1,0:T(8,128)(2,1)}, u32[]{:S(2)}) copy-start(bf16[2560,128]{1,0:T(8,128)(2,1)} %mul.154) | copy-start | bytes 1966084
Sparse Core Ops, SparseCore 0:
  19.8 46.5 reduce-scatter.1
where the time goes:
time: 122 us; the launch traced here: 121 us
  waiting for transfers between devices  34.3 us (28%)
  matrix products  28.3 us (23%)
  local copies, waits for them, and re-layouts  20.8 us (17%)
  blocking collectives  15.7 us (13%)
  between operations  13.6 us (11%)
  other arithmetic  5.24 us (4%)
  starting transfers between devices  3.41 us (3%)
    reduce_scatter x1, waiting for transfers between devices, per_device(): summed = lax.psum_scatter(partial, 'freq', scatter_dimension=0, tiled=True)  32.1 us
    all_gather x1, blocking collectives, per_device(): piece = lax.all_gather(received, 'freq', axis=0, tiled=True)  15.7 us
    dot_general x1, matrix products, per_device(): jnp.dot(spread_over(forward, virtual_sources), flat_traces, preferred_ele...  11.2 us
    mul x8, local copies, waits for them, and re-layouts, spread_over(): weights[:, None, :, None] * eye[None, :, None, :]  8.53 us
    dot_general x4, matrix products, source_product(): jnp.einsum('ajrs,vjs->ajrv', left_operand_factors, right_operand_factors,...  7.79 us
    dot_general x1, matrix products, per_device(): jnp.dot(spread_over(backward, virtual_sources), piece.reshape(count * 2 *...  5.6 us
    slice x1, local copies, waits for them, and re-layouts, per_device(): emitter_factors[1]  3.92 us
    slice x1, local copies, waits for them, and re-layouts, per_device(): receiver_factors[0]  3.86 us
  transfers between devices with their start and end apart: 2, of which 2 were waited for; matrix products, arithmetic and copies ran while one was open for 15% of the time, Pallas kernels for 0%

commit v1 on v0

--- a/solution.py
+++ b/solution.py
@@ -16,9 +16,23 @@
 
 
 def spread_over(weights, count):
-    eye = jnp.eye(count, dtype=weights.dtype)
     rows, cols = weights.shape
-    return (weights[:, None, :, None] * eye[None, :, None, :]).reshape(rows * count, cols * count)
+    kind = weights.dtype
+    repeat_rows = (
+        jnp.arange(rows * count, dtype=jnp.int32)[:, None] // count
+        == jnp.arange(rows, dtype=jnp.int32)[None, :]
+    ).astype(kind)
+    repeat_cols = (
+        jnp.arange(cols, dtype=jnp.int32)[:, None]
+        == jnp.arange(cols * count, dtype=jnp.int32)[None, :] // count
+    ).astype(kind)
+    tall = jnp.dot(repeat_rows, weights, preferred_element_type=jnp.float32).astype(kind)
+    wide = jnp.dot(tall, repeat_cols, preferred_element_type=jnp.float32)
+    same = (
+        jnp.arange(rows * count, dtype=jnp.int32)[:, None] % count
+        == jnp.arange(cols * count, dtype=jnp.int32)[None, :] % count
+    )
+    return jnp.where(same, wide, jnp.float32(0.0)).astype(kind)
 
 
 def per_device(traces, v_factors, u_factors, ranks):
@@ -40,9 +54,10 @@
     flat_traces = traces.reshape(time_count * virtual_sources, source_count)
     partial = jnp.dot(
         spread_over(forward, virtual_sources), flat_traces, preferred_element_type=jnp.float32
-    ).reshape(freq_total, 2, virtual_sources, source_count)
-    summed = lax.psum_scatter(partial, "freq", scatter_dimension=0, tiled=True)
-    spectrum = (summed * scale_time).astype(jnp.bfloat16)[0]
+    )
+    partial = (partial * scale_time).astype(jnp.bfloat16)
+    partial = partial.reshape(freq_total, 2, virtual_sources, source_count)
+    spectrum = lax.psum_scatter(partial, "freq", scatter_dimension=0, tiled=True)[0]
     spectral_tiles = spectrum.reshape(2, virtual_sources, columns, tile_width)
     emitter_factors = v_factors[0]
 

time: 122 us -> 103 us (0.84)
  local copies, waits for them, and re-layouts: 20.8 us -> 12 us
  waiting for transfers between devices: 34.3 us -> 26.4 us
  other arithmetic: 5.24 us -> 1.38 us
    reduce_scatter x1, waiting for transfers between devices: 32.1 us -> 22.6 us  [per_device(): lax.psum_scatter(partial, 'freq', scatter_dimension=0, tiled=True)[0]]
    mul x8 -> x0, local copies, waits for them, and re-layouts: 8.53 us -> none  [spread_over(): weights[:, None, :, None] * eye[None, :, None, :]]
    mul x1 -> x0, other arithmetic: 2.77 us -> none  [spread_over(): weights[:, None, :, None] * eye[None, :, None, :]]
    dot_general x0 -> x2, matrix products: none -> 2.25 us  [spread_over(): jnp.dot(repeat_rows, weights, preferred_element_type=jnp.float32)]
    slice x1, local copies, waits for them, and re-layouts: 3.86 us -> 1.68 us  [per_device(): receiver_factors[0]]
    all_to_all x1, waiting for transfers between devices: 2.14 us -> 3.81 us  [per_device(): lax.all_to_all(coefficients, 'tile', split_axis=1, concat_axis=2, tiled=T...]
    dot_general x1, matrix products: 11.2 us -> 9.82 us  [per_device(): jnp.dot(spread_over(forward, virtual_sources), flat_traces, preferred_ele...]
  transfers between devices with their start and end apart: 2 -> 2, of which waited for: 2 -> 2; matrix products, arithmetic and copies ran while one was open for 15% -> 9% of each run, Pallas kernels for 0% -> 0%
where the time goes in v1:
time: 103 us; the launch traced here: 102 us
  matrix products  29.4 us (29%)
  waiting for transfers between devices  26.4 us (26%)
  blocking collectives  15.9 us (15%)
  between operations  13.6 us (13%)
  local copies, waits for them, and re-layouts  12 us (12%)
  starting transfers between devices  3.59 us (3%)
  other arithmetic  1.38 us (1%)
    reduce_scatter x1, waiting for transfers between devices, per_device(): lax.psum_scatter(partial, 'freq', scatter_dimension=0, tiled=True)[0]  22.6 us
    all_gather x1, blocking collectives, per_device(): piece = lax.all_gather(received, 'freq', axis=0, tiled=True)  15.9 us
    dot_general x1, matrix products, per_device(): jnp.dot(spread_over(forward, virtual_sources), flat_traces, preferred_ele...  9.82 us
    dot_general x4, matrix products, source_product(): jnp.einsum('ajrs,vjs->ajrv', left_operand_factors, right_operand_factors,...  7.62 us
    dot_general x1, matrix products, per_device(): jnp.dot(spread_over(backward, virtual_sources), piece.reshape(count * 2 *...  6.01 us
    slice x1, local copies, waits for them, and re-layouts, per_device(): emitter_factors[1]  4.89 us
    all_to_all x1, waiting for transfers between devices, per_device(): lax.all_to_all(coefficients, 'tile', split_axis=1, concat_axis=2, tiled=T...  3.81 us
    dot_general x4, matrix products, receiver_product(): jnp.einsum('mdlh,mdlu->umh', left_operand_factors, right_operand_factors,...  3.72 us
  transfers between devices with their start and end apart: 2, of which 2 were waited for; matrix products, arithmetic and copies ran while one was open for 9% of the time, Pallas kernels for 0%

profile of v1, /device:TPU:0, one launch (start us, length us, event | category | flops | bytes accessed | tf_op | source)
XLA Modules:
  0.0 102.4 jit_solution(18074341768632488276)
XLA Ops:
  6.6 0.1 fusion.54
  6.7 0.1 cosine_convert_fusion
  6.9 0.2 convolution_convert_fusion.1
  7.2 9.8 %fusion = bf16[128,4096]{1,0:T(8,128)(2,1)} fusion(bf16[2560,4096]{1,0:T(8,128)(2,1)} %bitcast.113, bf16[128,160]{0,1:T(8,128)(2,1)S(1)} %convolution_convert_fusion.1, s32[2560]{0:T(1024)S(1)} %get-tuple-element.13, s32[2560]{0:T(1024)S(1)} %get-tuple-element.14, s32[128]{0:T(128)S(1)} %get-tuple-element.16), kind=kOutput, calls=%fused_computation.2 | convolution fusion | flops 2791653376 | bytes 22082048 | tf_op jit(solution)/shard_map/dot_general | solution.py:55
  17.0 0.1 fusion.53
  17.1 0.1 cosine_convert_fusion.1
  17.4 0.4 copy.90
  17.8 4.9 %fusion.60 = (bf16[1,1,32,16,8,256]{5,4,3,2,1,0:T(8,128)(2,1)}, bf16[1,1,32,16,8,256]{5,4,3,2,1,0:T(8,128)(2,1)}) fusion(bf16[1,2,32,16,8,256]{5,4,3,2,1,0:T(8,128)(2,1)} %param.5), kind=kLoop, calls=%fused_computation.97 | loop fusion | bytes 8388608 | tf_op jit(solution)/shard_map/slice | solution.py:73
  22.7 1.7 %fusion.59 = (bf16[1,1,8,64,8,256]{5,4,3,2,1,0:T(8,128)(2,1)S(1)}, bf16[1,1,8,64,8,256]{5,4,3,2,1,0:T(8,128)(2,1)}) fusion(bf16[1,2,8,64,8,256]{5,4,3,2,1,0:T(8,128)(2,1)S(1)} %copy-done.2), kind=kLoop, calls=%fused_computation.96 | loop fusion | bytes 8388608 | tf_op jit(solution)/shard_map/slice | solution.py:99
  24.4 22.6 %reduce-scatter.2.cloned.1.call-done = bf16[1,2,16,4096]{3,2,1,0:T(8,128)(2,1)} async-done(((bf16[4,2,16,4096]{3,2,1,0:T(8,128)(2,1)}), bf16[1,2,16,4096]{3,2,1,0:T(8,128)(2,1)}) %reduce-scatter.2.cloned.1.call-update) | async-done | bytes 262160 | tf_op jit(solution)/shard_map/reduce_scatter | solution.py:60
  47.0 1.1 %fusion.62 = (bf16[1,1,16,4096]{3,2,1,0:T(8,128)(2,1)S(1)}, bf16[1,1,16,4096]{3,2,1,0:T(8,128)(2,1)S(1)}) fusion(bf16[1,2,16,4096]{3,2,1,0:T(8,128)(2,1)} %reduce-scatter.2.cloned.1.call-done), kind=kLoop, calls=%fused_computation.99 | loop fusion | bytes 524288 | tf_op jit(solution)/shard_map/slice | solution.py:72
  48.2 3.1 %fusion.3 = f32[16,16,32,8]{2,1,3,0:T(8,128)S(1)} fusion(bf16[1,1,32,16,8,256]{5,4,3,2,1,0:T(8,128)(2,1)} %get-tuple-element.8, bf16[16,16,256,1]{2,1,0,3:T(8,128)(2,1)S(1)} %bitcast.118), kind=kOutput, calls=%fused_computation.13 | convolution fusion | flops 33554432 | bytes 2490368 | tf_op jit(solution)/shard_map/ajrs,vjs->ajrv/dot_general | solution.py:65
  51.3 1.5 %fusion.4 = f32[16,16,32,8]{2,1,3,0:T(8,128)S(1)} fusion(bf16[1,1,32,16,8,256]{5,4,3,2,1,0:T(8,128)(2,1)S(1)} %copy-done.1, bf16[16,16,256,1]{2,1,0,3:T(8,128)(2,1)S(1)} %bitcast.120), kind=kOutput, calls=%fused_computation.14 | convolution fusion | flops 33554432 | bytes 2490368 | tf_op jit(solution)/shard_map/ajrs,vjs->ajrv/dot_general | solution.py:65
  52.8 0.1 copy-done
  52.9 1.5 %fusion.12 = bf16[16,16,32,8]{2,1,3,0:T(8,128)(2,1)S(1)} fusion(f32[16,16,32,8]{2,1,3,0:T(8,128)S(1)} %fusion.3, bf16[1,1,32,16,8,256]{5,4,3,2,1,0:T(8,128)(2,1)S(1)} %copy-done, bf16[16,16,256,1]{2,1,0,3:T(8,128)(2,1)S(1)} %bitcast.121), kind=kOutput, calls=%fused_computation.23 | convolution fusion | flops 33685504 | bytes 2621440 | tf_op jit(solution)/shard_map/ajrs,vjs->ajrv/dot_general | solution.py:65
  54.4 1.5 %fusion.11 = bf16[16,16,32,8]{2,1,3,0:T(8,128)(2,1)S(1)} fusion(f32[16,16,32,8]{2,1,3,0:T(8,128)S(1)} %fusion.4, bf16[1,1,32,16,8,256]{5,4,3,2,1,0:T(8,128)(2,1)S(1)} %copy-done, bf16[16,16,256,1]{2,1,0,3:T(8,128)(2,1)S(1)} %bitcast.119), kind=kOutput, calls=%fused_computation.22 | convolution fusion | flops 33685504 | bytes 2621440 | tf_op jit(solution)/shard_map/ajrs,vjs->ajrv/dot_general | solution.py:65
  55.9 0.2 copy.98
  56.2 0.2 copy.99
  56.4 0.8 fusion.32
  57.2 3.6 %all-to-all-start = ((bf16[2,32,16,128]{3,2,0,1:T(8,128)(2,1)}), bf16[2,32,16,128]{3,2,0,1:T(8,128)(2,1)S(1)}, u32[]{:S(2)}, u32[]{:S(2)}) async-start(bf16[2,32,16,128]{3,2,0,1:T(8,128)(2,1)} %fusion.32), calls=%async_computation.1 | async-start | bytes 524288 | tf_op jit(solution)/shard_map/all_to_all | solution.py:85
  60.8 2.0 %convolution_convert_fusion = bf16[2560,8]{0,1:T(8,128)(2,1)} fusion(bf16[160,8]{0,1:T(8,128)(2,1)S(1)} %reshape.540, s32[2560]{0:T(1024)S(1)} %get-tuple-element.13), kind=kOutput, calls=%fused_computation.7 | convolution fusion | flops 6983680 | bytes 53760 | tf_op jit(solution)/shard_map/dot_general | solution.py:29
  62.8 3.8 %all-to-all-done = bf16[2,32,16,128]{3,2,0,1:T(8,128)(2,1)S(1)} async-done(((bf16[2,32,16,128]{3,2,0,1:T(8,128)(2,1)}), bf16[2,32,16,128]{3,2,0,1:T(8,128)(2,1)S(1)}, u32[]{:S(2)}, u32[]{:S(2)}) %all-to-all-start) | async-done | bytes 262176 | tf_op jit(solution)/shard_map/all_to_all | solution.py:85
  66.7 0.7 copy.128
  67.3 0.5 reshape.555
  67.8 0.7 copy.127
  68.5 1.2 %reshape.554 = bf16[8,64,8,16]{1,3,2,0:T(8,128)(2,1)} reshape(bf16[1,8,4,16,128]{3,2,4,1,0:T(4,128)(2,1)S(1)} %copy.127) | data formatting | bytes 262144 | tf_op jit(solution)/shard_map/squeeze | solution.py:99
  69.7 2.3 %fusion.15 = f32[8,16,256]{2,1,0:T(8,128)S(1)} fusion(bf16[8,64,8,16]{1,3,2,0:T(8,128)(2,1)} %reshape.554, bf16[1,1,8,64,8,256]{5,4,3,2,1,0:T(8,128)(2,1)} %get-tuple-element.6), kind=kOutput, calls=%fused_computation.26 | convolution fusion | flops 33554432 | bytes 2359296 | tf_op jit(solution)/shard_map/mdlh,mdlu->umh/dot_general | solution.py:92
  72.0 0.5 fusion.14
  72.5 0.5 fusion.22
  73.0 0.5 fusion.23
  73.7 15.9 %all_gather.3 = bf16[4,2,16,2048]{3,2,1,0:T(8,128)(2,1)S(1)} all-gather(bf16[1,2,16,2048]{3,2,1,0:T(8,128)(2,1)S(1)} %pad_maximum_fusion), channel_id=1, replica_groups=mesh['groups'=2,'freq'=4,'tile'=4] {'freq'}, dimensions={0}, use_global_device_ids=true | all-gather | bytes 655360 | tf_op jit(solution)/shard_map/all_gather | solution.py:111
  89.5 6.0 %multiply_convert_fusion = bf16[2560,2048]{1,0:T(8,128)(2,1)} fusion(bf16[128,2048]{1,0:T(8,128)(2,1)S(1)} %bitcast.117, bf16[2560,8]{0,1:T(8,128)(2,1)S(1)} %copy-done.5, s32[128]{0:T(128)S(1)} %get-tuple-element.16, s32[2560]{0:T(1024)S(1)} %get-tuple-element.14, s32[128]{0:T(128)S(1)} %copy-done.8), kind=kOutput, calls=%fused_computation | convolution fusion | flops 1358889984 | bytes 11062272 | tf_op jit(solution)/shard_map/dot_general | solution.py:115
  (40 shorter events, 0.5 us)
Async XLA Ops:
  6.5 40.5 %reduce-scatter.2.cloned.1.call-start = ((), (), s32[]{:S(2)}) async-start(), calls=%async_computation.2 | async-start | bytes 1310720 | tf_op jit(solution)/shard_map/reduce_scatter | solution.py:60
  6.5 10.4 %copy-start.7 = (s32[128]{0:T(128)}, s32[128]{0:T(128)S(1)}, u32[]{:S(2)}) copy-start(s32[128]{0:T(128)S(1)} %get-tuple-element.15) | copy-start | bytes 1540
  7.1 10.2 %copy-start.6 = (s32[1,32,16]{1,2,0:T(8,128)S(1)}, s32[1,32,16]{1,2,0:T(8,128)}, u32[]{:S(2)}) copy-start(s32[1,32,16]{1,2,0:T(8,128)} %param.7) | copy-start | bytes 6148
  17.8 4.9 %copy-start.2 = (bf16[1,2,8,64,8,256]{5,4,3,2,1,0:T(8,128)(2,1)S(1)}, bf16[1,2,8,64,8,256]{5,4,3,2,1,0:T(8,128)(2,1)}, u32[]{:S(2)}) copy-start(bf16[1,2,8,64,8,256]{5,4,3,2,1,0:T(8,128)(2,1)} %param.6) | copy-start | bytes 12582916
  47.0 4.3 %copy-start.1 = (bf16[1,1,32,16,8,256]{5,4,3,2,1,0:T(8,128)(2,1)S(1)}, bf16[1,1,32,16,8,256]{5,4,3,2,1,0:T(8,128)(2,1)}, u32[]{:S(2)}) copy-start(bf16[1,1,32,16,8,256]{5,4,3,2,1,0:T(8,128)(2,1)} %get-tuple-element.8) | copy-start | bytes 6291460
  51.3 1.6 %copy-start = (bf16[1,1,32,16,8,256]{5,4,3,2,1,0:T(8,128)(2,1)S(1)}, bf16[1,1,32,16,8,256]{5,4,3,2,1,0:T(8,128)(2,1)}, u32[]{:S(2)}) copy-start(bf16[1,1,32,16,8,256]{5,4,3,2,1,0:T(8,128)(2,1)} %get-tuple-element.7) | copy-start | bytes 6291460
  57.2 9.4 %all-to-all-start = ((bf16[2,32,16,128]{3,2,0,1:T(8,128)(2,1)}), bf16[2,32,16,128]{3,2,0,1:T(8,128)(2,1)S(1)}, u32[]{:S(2)}, u32[]{:S(2)}) async-start(bf16[2,32,16,128]{3,2,0,1:T(8,128)(2,1)} %fusion.32), calls=%async_computation.1 | async-start | bytes 524288 | tf_op jit(solution)/shard_map/all_to_all | solution.py:85
  69.7 2.3 %copy-start.3 = (bf16[1,1,8,64,8,256]{5,4,3,2,1,0:T(8,128)(2,1)S(1)}, bf16[1,1,8,64,8,256]{5,4,3,2,1,0:T(8,128)(2,1)}, u32[]{:S(2)}) copy-start(bf16[1,1,8,64,8,256]{5,4,3,2,1,0:T(8,128)(2,1)} %get-tuple-element.6) | copy-start | bytes 6291460
  72.0 1.0 copy-start.4
  73.0 16.6 %copy-start.5 = (bf16[2560,8]{0,1:T(8,128)(2,1)S(1)}, bf16[2560,8]{0,1:T(8,128)(2,1)}, u32[]{:S(2)}) copy-start(bf16[2560,8]{0,1:T(8,128)(2,1)} %convolution_convert_fusion) | copy-start | bytes 122884
  73.0 16.6 %copy-start.8 = (s32[128]{0:T(128)S(1)}, s32[128]{0:T(128)}, u32[]{:S(2)}) copy-start(s32[128]{0:T(128)} %copy-done.7) | copy-start | bytes 1540
Sparse Core Ops, SparseCore 0:
  17.1 29.8 reduce-scatter.1

commit v2 on v1

--- a/solution.py
+++ b/solution.py
@@ -35,6 +35,44 @@
     return jnp.where(same, wide, jnp.float32(0.0)).astype(kind)
 
 
+def line_reduce_scatter(partial, axis):
+    count = partial.shape[0]
+    own = lax.axis_index(axis)
+
+    def block(index):
+        return lax.dynamic_index_in_dim(partial, jnp.clip(index, 0, count - 1), 0, keepdims=False)
+
+    right = jnp.zeros_like(partial[0])
+    left = jnp.zeros_like(partial[0])
+    for step in range(1, count):
+        send_right = block(count - step + own) + right
+        send_left = block(own + step - count) + left
+        right = lax.ppermute(send_right, axis, [(p, p + 1) for p in range(step)])
+        left = lax.ppermute(send_left, axis, [(count - 1 - p, count - 2 - p) for p in range(step)])
+    return block(own) + right + left
+
+
+def line_all_gather(piece, axis, count):
+    own = lax.axis_index(axis)
+    slots = jnp.zeros((count,) + piece.shape, piece.dtype)
+    slots = lax.dynamic_update_index_in_dim(slots, piece, own, 0)
+    right = piece
+    left = piece
+    for step in range(1, count):
+        right = lax.ppermute(right, axis, [(p, p + 1) for p in range(step - 1, count - 1)])
+        left = lax.ppermute(left, axis, [(p + 1, p) for p in range(0, count - step)])
+        for arrived, origin, valid in (
+            (right, own - step, own >= step),
+            (left, own + step, own + step <= count - 1),
+        ):
+            index = jnp.clip(origin, 0, count - 1)
+            current = lax.dynamic_index_in_dim(slots, index, 0, keepdims=False)
+            slots = lax.dynamic_update_index_in_dim(
+                slots, jnp.where(valid, arrived, current), index, 0
+            )
+    return slots
+
+
 def per_device(traces, v_factors, u_factors, ranks):
     time_count = traces.shape[0]
     virtual_sources = traces.shape[1]
@@ -54,10 +92,9 @@
     flat_traces = traces.reshape(time_count * virtual_sources, source_count)
     partial = jnp.dot(
         spread_over(forward, virtual_sources), flat_traces, preferred_element_type=jnp.float32
-    )
-    partial = (partial * scale_time).astype(jnp.bfloat16)
-    partial = partial.reshape(freq_total, 2, virtual_sources, source_count)
-    spectrum = lax.psum_scatter(partial, "freq", scatter_dimension=0, tiled=True)[0]
+    ).reshape(freq_total, 2, virtual_sources, source_count)
+    summed = line_reduce_scatter(partial, "freq")
+    spectrum = (summed * scale_time).astype(jnp.bfloat16)
     spectral_tiles = spectrum.reshape(2, virtual_sources, columns, tile_width)
     emitter_factors = v_factors[0]
 
@@ -108,8 +145,8 @@
         .reshape(1, 2, virtual_sources, receivers)
         .astype(jnp.bfloat16)
     )
-    piece = lax.all_gather(received, "freq", axis=0, tiled=True)
-    count = piece.shape[0]
+    count = freq_total
+    piece = line_all_gather(received[0], "freq", count)
 
     backward = jnp.stack([cosine.T, -sine.T], 2).reshape(time_count, count * 2)
     added = jnp.dot(

time: 103 us -> 129 us (1.25)
  starting transfers between devices: 3.59 us -> 32.8 us
  waiting for transfers between devices: 26.4 us -> 49.7 us
  blocking collectives: 15.9 us -> 0 us
  between operations: 13.6 us -> 0.55 us
  other arithmetic: 1.38 us -> 5.1 us
  matrix products: 29.4 us -> 26.3 us
  local copies, waits for them, and re-layouts: 12 us -> 14.1 us
    ppermute x0 -> x12, waiting for transfers between devices: none -> 45.2 us  [the longest x3 22.2 us: line_reduce_scatter(): right = lax.ppermute(send_right, axis, [(p, p + 1) for p in range(step)])]
    ppermute x0 -> x12, starting transfers between devices: none -> 29.2 us  [the longest x3 16 us: line_reduce_scatter(): right = lax.ppermute(send_right, axis, [(p, p + 1) for p in range(step)])]
    reduce_scatter x1 -> x0, waiting for transfers between devices: 22.6 us -> none  [per_device(): lax.psum_scatter(partial, 'freq', scatter_dimension=0, tiled=True)[0]]
    all_gather x1 -> x0, blocking collectives: 15.9 us -> none  [per_device(): piece = lax.all_gather(received, 'freq', axis=0, tiled=True)]
    add x0 -> x3, other arithmetic: none -> 2.22 us  [the longest x2 2.17 us: line_reduce_scatter(): send_right = block(count - step + own) + right]
    slice x1, local copies, waits for them, and re-layouts: 1.68 us -> 3.9 us  [per_device(): receiver_factors[0]]
    dot_general x4, matrix products: 7.62 us -> 6.04 us  [source_product(): jnp.einsum('ajrs,vjs->ajrv', left_operand_factors, right_operand_factors,...]
    dot_general x1, matrix products: 9.82 us -> 8.52 us  [per_device(): jnp.dot(spread_over(forward, virtual_sources), flat_traces, preferred_ele...]
  transfers between devices with their start and end apart: 2 -> 13, of which waited for: 2 -> 8; matrix products, arithmetic and copies ran while one was open for 9% -> 9% of each run, Pallas kernels for 0% -> 0%
where the time goes in v2:
time: 129 us; the launch traced here: 128 us
  waiting for transfers between devices  49.7 us (39%)
  starting transfers between devices  32.8 us (25%)
  matrix products  26.3 us (20%)
  local copies, waits for them, and re-layouts  14.1 us (11%)
  other arithmetic  5.1 us (4%)
    ppermute x3, waiting for transfers between devices, line_reduce_scatter(): right = lax.ppermute(send_right, axis, [(p, p + 1) for p in range(step)])  22.2 us
    ppermute x3, starting transfers between devices, line_reduce_scatter(): right = lax.ppermute(send_right, axis, [(p, p + 1) for p in range(step)])  16 us
    ppermute x3, waiting for transfers between devices, line_all_gather(): lax.ppermute(left, axis, [(p + 1, p) for p in range(0, count - step)])  13.6 us
    dot_general x1, matrix products, per_device(): jnp.dot(spread_over(forward, virtual_sources), flat_traces, preferred_ele...  8.52 us
    ppermute x3, waiting for transfers between devices, line_reduce_scatter(): lax.ppermute(send_left, axis, [(count - 1 - p, count - 2 - p) for p in ra...  7.12 us
    dot_general x4, matrix products, source_product(): jnp.einsum('ajrs,vjs->ajrv', left_operand_factors, right_operand_factors,...  6.04 us
    dot_general x1, matrix products, per_device(): jnp.dot(spread_over(backward, virtual_sources), piece.reshape(count * 2 *...  6.02 us
    ppermute x3, starting transfers between devices, line_all_gather(): lax.ppermute(right, axis, [(p, p + 1) for p in range(step - 1, count - 1)])  5.88 us
  transfers between devices with their start and end apart: 13, of which 8 were waited for; matrix products, arithmetic and copies ran while one was open for 9% of the time, Pallas kernels for 0%

profile of v2, /device:TPU:0, one launch (start us, length us, event | category | flops | bytes accessed | tf_op | source)
XLA Modules:
  0.0 128.5 jit_solution(11753833605231947994)
XLA Ops:
  1.0 8.5 %fusion.61 = f32[4,2,16,4096]{3,2,1,0:T(8,128)S(1)} fusion(bf16[4,2,16,2560]{3,2,1,0:T(8,128)(2,1)S(1)} %bitcast.181, bf16[2560,4096,1,1]{1,0,3,2:T(8,128)(2,1)} %bitcast.171), kind=kOutput, calls=%fused_computation.124 | convolution fusion | flops 2684354560 | bytes 23724032 | tf_op jit(solution)/shard_map/dot_general | solution.py:93
  9.6 0.9 dynamic-slice_bitcast_fusion.1
  10.5 4.9 %collective-permute-start = (f32[2,16,4096]{2,1,0:T(8,128)S(1)}, f32[2,16,4096]{2,1,0:T(8,128)S(1)}, u32[]{:S(2)}, u32[]{:S(2)}) collective-permute-start(f32[2,16,4096]{2,1,0:T(8,128)S(1)} %get-tuple-element.11), channel_id=1, source_target_pairs={{0,4},{1,5},{2,6},{3,7},{16,20},{17,21},{18,22},{19,23}} | collective-permute-start | bytes 1572872 | tf_op jit(solution)/shard_map/ppermute | solution.py:50
  15.5 1.5 %collective-permute-start.3 = (f32[2,16,4096]{2,1,0:T(8,128)}, f32[2,16,4096]{2,1,0:T(8,128)}, u32[]{:S(2)}, u32[]{:S(2)}) collective-permute-start(f32[2,16,4096]{2,1,0:T(8,128)} %get-tuple-element.12), channel_id=1, source_target_pairs={{12,8},{13,9},{14,10},{15,11},{28,24},{29,25},{30,26},{31,27}} | collective-permute-start | bytes 1572872 | tf_op jit(solution)/shard_map/ppermute | solution.py:51
  16.9 9.7 %collective-permute-done = f32[2,16,4096]{2,1,0:T(8,128)S(1)} collective-permute-done((f32[2,16,4096]{2,1,0:T(8,128)S(1)}, f32[2,16,4096]{2,1,0:T(8,128)S(1)}, u32[]{:S(2)}, u32[]{:S(2)}) %collective-permute-start) | collective-permute-done | bytes 524320 | tf_op jit(solution)/shard_map/ppermute | solution.py:50
  26.7 5.2 %collective-permute-start.1 = (f32[2,16,4096]{2,1,0:T(8,128)S(1)}, f32[2,16,4096]{2,1,0:T(8,128)}, u32[]{:S(2)}, u32[]{:S(2)}) collective-permute-start(f32[2,16,4096]{2,1,0:T(8,128)S(1)} %bitcast_add_fusion.2), channel_id=1, source_target_pairs={{0,4},{4,8},{1,5},{5,9},{2,6},{6,10},{3,7},{7,11},{16,20},{20,24},... | collective-permute-start | bytes 1572872 | tf_op jit(solution)/shard_map/ppermute | solution.py:50
  32.0 9.3 %collective-permute-done.1 = f32[2,16,4096]{2,1,0:T(8,128)} collective-permute-done((f32[2,16,4096]{2,1,0:T(8,128)S(1)}, f32[2,16,4096]{2,1,0:T(8,128)}, u32[]{:S(2)}, u32[]{:S(2)}) %collective-permute-start.1) | collective-permute-done | bytes 524320 | tf_op jit(solution)/shard_map/ppermute | solution.py:50
  41.3 2.1 %bitcast_add_fusion.3 = (f32[2,16,4096]{2,1,0:T(8,128)}, f32[2,16,4096]{2,1,0:T(8,128)S(1)}) fusion(f32[2,16,4096]{2,1,0:T(8,128)} %collective-permute-done.1, f32[4,2,16,4096]{3,2,1,0:T(8,128)S(1)} %fusion.61, s32[]{:T(128)S(6)} %min.29, f32[2,16,4096]{2,1,0:T(8,128)} %collective-permute-done.3, s32[]{:T(128)S(6)} %min.33), kind=kLoop, calls=%fused_computation.43 | loop fusion | flops 262144 | bytes 3145736 | tf_op jit(solution)/shard_map/add | solution.py:48
  44.4 4.7 %fusion.58 = (bf16[1,1,32,16,8,256]{5,4,3,2,1,0:T(8,128)(2,1)}, bf16[1,1,32,16,8,256]{5,4,3,2,1,0:T(8,128)(2,1)}) fusion(bf16[1,2,32,16,8,256]{5,4,3,2,1,0:T(8,128)(2,1)} %param.5), kind=kLoop, calls=%fused_computation.121 | loop fusion | bytes 8388608 | tf_op jit(solution)/shard_map/slice | solution.py:110
  49.1 5.9 %collective-permute-start.2 = (f32[2,16,4096]{2,1,0:T(8,128)}, f32[2,16,4096]{2,1,0:T(8,128)}, u32[]{:S(2)}, u32[]{:S(2)}) collective-permute-start(f32[2,16,4096]{2,1,0:T(8,128)} %get-tuple-element.9), channel_id=1, source_target_pairs={{0,4},{4,8},{8,12},{1,5},{5,9},{9,13},{2,6},{6,10},{10,14},{3,7},{... | collective-permute-start | bytes 1572872 | tf_op jit(solution)/shard_map/ppermute | solution.py:50
  55.0 1.3 %collective-permute-start.5 = (f32[2,16,4096]{2,1,0:T(8,128)S(1)}, f32[2,16,4096]{2,1,0:T(8,128)S(1)}, u32[]{:S(2)}, u32[]{:S(2)}) collective-permute-start(f32[2,16,4096]{2,1,0:T(8,128)S(1)} %bitcast_add_fusion.1), channel_id=1, source_target_pairs={{12,8},{8,4},{4,0},{13,9},{9,5},{5,1},{14,10},{10,6},{6,2},{15,11}... | collective-permute-start | bytes 1572872 | tf_op jit(solution)/shard_map/ppermute | solution.py:51
  56.8 3.9 %fusion.57 = (bf16[1,1,8,64,8,256]{5,4,3,2,1,0:T(8,128)(2,1)S(1)}, bf16[1,1,8,64,8,256]{5,4,3,2,1,0:T(8,128)(2,1)}) fusion(bf16[1,2,8,64,8,256]{5,4,3,2,1,0:T(8,128)(2,1)} %param.6), kind=kLoop, calls=%fused_computation.120 | loop fusion | bytes 8388608 | tf_op jit(solution)/shard_map/slice | solution.py:136
  60.7 3.1 %collective-permute-done.2 = f32[2,16,4096]{2,1,0:T(8,128)} collective-permute-done((f32[2,16,4096]{2,1,0:T(8,128)}, f32[2,16,4096]{2,1,0:T(8,128)}, u32[]{:S(2)}, u32[]{:S(2)}) %collective-permute-start.2) | collective-permute-done | bytes 524320 | tf_op jit(solution)/shard_map/ppermute | solution.py:50
  63.9 7.1 %collective-permute-done.5 = f32[2,16,4096]{2,1,0:T(8,128)S(1)} collective-permute-done((f32[2,16,4096]{2,1,0:T(8,128)S(1)}, f32[2,16,4096]{2,1,0:T(8,128)S(1)}, u32[]{:S(2)}, u32[]{:S(2)}) %collective-permute-start.5) | collective-permute-done | bytes 524320 | tf_op jit(solution)/shard_map/ppermute | solution.py:51
  71.0 1.3 fusion.30
  72.4 1.5 %fusion.2 = f32[16,16,32,8]{2,1,3,0:T(8,128)S(1)} fusion(bf16[1,1,32,16,8,256]{5,4,3,2,1,0:T(8,128)(2,1)S(1)} %copy-done.1, bf16[16,16,256,1]{2,1,0,3:T(8,128)(2,1)S(1)} %bitcast.175), kind=kOutput, calls=%fused_computation.11 | convolution fusion | flops 33554432 | bytes 2490368 | tf_op jit(solution)/shard_map/ajrs,vjs->ajrv/dot_general | solution.py:102
  73.9 1.5 %fusion.3 = f32[16,16,32,8]{2,1,3,0:T(8,128)S(1)} fusion(bf16[1,1,32,16,8,256]{5,4,3,2,1,0:T(8,128)(2,1)S(1)} %copy-done.1, bf16[16,16,256,1]{2,1,0,3:T(8,128)(2,1)S(1)} %bitcast.177), kind=kOutput, calls=%fused_computation.12 | convolution fusion | flops 33554432 | bytes 2490368 | tf_op jit(solution)/shard_map/ajrs,vjs->ajrv/dot_general | solution.py:102
  75.5 1.5 %fusion.11 = bf16[16,16,32,8]{2,1,3,0:T(8,128)(2,1)S(1)} fusion(f32[16,16,32,8]{2,1,3,0:T(8,128)S(1)} %fusion.2, bf16[1,1,32,16,8,256]{5,4,3,2,1,0:T(8,128)(2,1)S(1)} %copy-done, bf16[16,16,256,1]{2,1,0,3:T(8,128)(2,1)S(1)} %bitcast.178), kind=kOutput, calls=%fused_computation.21 | convolution fusion | flops 33685504 | bytes 2621440 | tf_op jit(solution)/shard_map/ajrs,vjs->ajrv/dot_general | solution.py:102
  77.0 1.5 %fusion.10 = bf16[16,16,32,8]{2,1,3,0:T(8,128)(2,1)S(1)} fusion(f32[16,16,32,8]{2,1,3,0:T(8,128)S(1)} %fusion.3, bf16[1,1,32,16,8,256]{5,4,3,2,1,0:T(8,128)(2,1)S(1)} %copy-done, bf16[16,16,256,1]{2,1,0,3:T(8,128)(2,1)S(1)} %bitcast.176), kind=kOutput, calls=%fused_computation.20 | convolution fusion | flops 33685504 | bytes 2621440 | tf_op jit(solution)/shard_map/ajrs,vjs->ajrv/dot_general | solution.py:102
  79.8 3.6 %all-to-all-start = ((bf16[2,32,16,128]{3,2,0,1:T(8,128)(2,1)}), bf16[2,32,16,128]{3,2,0,1:T(8,128)(2,1)S(1)}, u32[]{:S(2)}, u32[]{:S(2)}) async-start(bf16[2,32,16,128]{3,2,0,1:T(8,128)(2,1)} %fusion.27), calls=%async_computation | async-start | bytes 524288 | tf_op jit(solution)/shard_map/all_to_all | solution.py:122
  83.3 1.4 %convolution_convert_fusion = bf16[2560,8]{0,1:T(8,128)(2,1)S(1)} fusion(bf16[160,8]{0,1:T(8,128)(2,1)S(1)} %reshape.546, s32[2560]{0:T(1024)S(1)} %get-tuple-element.19), kind=kOutput, calls=%fused_computation.5 | convolution fusion | flops 6983680 | bytes 53760 | tf_op jit(solution)/shard_map/dot_general | solution.py:29
  84.7 4.4 %all-to-all-done = bf16[2,32,16,128]{3,2,0,1:T(8,128)(2,1)S(1)} async-done(((bf16[2,32,16,128]{3,2,0,1:T(8,128)(2,1)}), bf16[2,32,16,128]{3,2,0,1:T(8,128)(2,1)S(1)}, u32[]{:S(2)}, u32[]{:S(2)}) %all-to-all-start) | async-done | bytes 262176 | tf_op jit(solution)/shard_map/all_to_all | solution.py:122
  89.9 1.2 reshape.561
  92.3 2.2 %fusion.14 = f32[8,16,256]{2,1,0:T(8,128)S(1)} fusion(bf16[8,64,8,16]{1,3,2,0:T(8,128)(2,1)S(1)} %reshape.560, bf16[1,1,8,64,8,256]{5,4,3,2,1,0:T(8,128)(2,1)} %get-tuple-element.6), kind=kOutput, calls=%fused_computation.24 | convolution fusion | flops 33554432 | bytes 2359296 | tf_op jit(solution)/shard_map/mdlh,mdlu->umh/dot_general | solution.py:129
  96.2 1.3 %collective-permute-start.7 = (bf16[2,16,2048]{2,1,0:T(8,128)(2,1)S(1)}, bf16[2,16,2048]{2,1,0:T(8,128)(2,1)S(1)}, u32[]{:S(2)}, u32[]{:S(2)}) collective-permute-start(bf16[2,16,2048]{2,1,0:T(8,128)(2,1)S(1)} %constant_dynamic-update-slice_fusion), channel_id=1, source_target_pairs={{4,0},{8,4},{12,8},{5,1},{9,5},{13,9},{6,2},{10,6},{14,10},{7,3},{... | collective-permute-start | bytes 393224 | tf_op jit(solution)/shard_map/ppermute | solution.py:63
  97.5 4.6 %collective-permute-start.6 = (bf16[2,16,2048]{2,1,0:T(8,128)(2,1)S(1)}, bf16[2,16,2048]{2,1,0:T(8,128)(2,1)S(1)}, u32[]{:S(2)}, u32[]{:S(2)}) collective-permute-start(bf16[2,16,2048]{2,1,0:T(8,128)(2,1)S(1)} %constant_dynamic-update-slice_fusion), channel_id=1, source_target_pairs={{0,4},{4,8},{8,12},{1,5},{5,9},{9,13},{2,6},{6,10},{10,14},{3,7},{... | collective-permute-start | bytes 393224 | tf_op jit(solution)/shard_map/ppermute | solution.py:62
  102.2 2.4 %collective-permute-done.6 = bf16[2,16,2048]{2,1,0:T(8,128)(2,1)S(1)} collective-permute-done((bf16[2,16,2048]{2,1,0:T(8,128)(2,1)S(1)}, bf16[2,16,2048]{2,1,0:T(8,128)(2,1)S(1)}, u32[]{:S(2)}, u32[]{:S(2)}) %collective-permute-start.6) | collective-permute-done | bytes 131104 | tf_op jit(solution)/shard_map/ppermute | solution.py:62
  105.3 1.3 %collective-permute-start.9 = (bf16[2,16,2048]{2,1,0:T(8,128)(2,1)S(1)}, bf16[2,16,2048]{2,1,0:T(8,128)(2,1)S(1)}, u32[]{:S(2)}, u32[]{:S(2)}) collective-permute-start(bf16[2,16,2048]{2,1,0:T(8,128)(2,1)S(1)} %collective-permute-done.7), channel_id=1, source_target_pairs={{4,0},{8,4},{5,1},{9,5},{6,2},{10,6},{7,3},{11,7},{20,16},{24,20},... | collective-permute-start | bytes 393224 | tf_op jit(solution)/shard_map/ppermute | solution.py:63
  107.4 8.1 %collective-permute-done.9 = bf16[2,16,2048]{2,1,0:T(8,128)(2,1)S(1)} collective-permute-done((bf16[2,16,2048]{2,1,0:T(8,128)(2,1)S(1)}, bf16[2,16,2048]{2,1,0:T(8,128)(2,1)S(1)}, u32[]{:S(2)}, u32[]{:S(2)}) %collective-permute-start.9) | collective-permute-done | bytes 131104 | tf_op jit(solution)/shard_map/ppermute | solution.py:63
  115.6 1.3 collective-permute-start.11
  117.0 5.4 %collective-permute-done.11 = bf16[2,16,2048]{2,1,0:T(8,128)(2,1)S(1)} collective-permute-done((bf16[2,16,2048]{2,1,0:T(8,128)(2,1)S(1)}, bf16[2,16,2048]{2,1,0:T(8,128)(2,1)S(1)}, u32[]{:S(2)}, u32[]{:S(2)}) %collective-permute-start.11) | collective-permute-done | bytes 131104 | tf_op jit(solution)/shard_map/ppermute | solution.py:63
  122.5 6.0 %multiply_convert_fusion = bf16[2560,2048]{1,0:T(8,128)(2,1)} fusion(bf16[128,2048]{1,0:T(8,128)(2,1)S(1)} %bitcast.172, bf16[2560,8]{0,1:T(8,128)(2,1)S(1)} %convolution_convert_fusion, s32[128]{0:T(128)S(1)} %get-tuple-element.18, s32[2560]{0:T(1024)S(1)} %get-tuple-element.20, s32[128]{0:T(128)S(1)} %get-tuple-element.17), kind=kOutput, calls=%fused_computation | convolution fusion | flops 1358889984 | bytes 11062272 | tf_op jit(solution)/shard_map/dot_general | solution.py:152
  (76 shorter events, 9.2 us)
Async XLA Ops:
  9.6 45.4 %copy-start.2 = (f32[4,2,16,4096]{3,2,1,0:T(8,128)}, f32[4,2,16,4096]{3,2,1,0:T(8,128)S(1)}, u32[]{:S(2)}) copy-start(f32[4,2,16,4096]{3,2,1,0:T(8,128)S(1)} %fusion.61) | copy-start | bytes 6291460
  10.5 16.1 %collective-permute-start = (f32[2,16,4096]{2,1,0:T(8,128)S(1)}, f32[2,16,4096]{2,1,0:T(8,128)S(1)}, u32[]{:S(2)}, u32[]{:S(2)}) collective-permute-start(f32[2,16,4096]{2,1,0:T(8,128)S(1)} %get-tuple-element.11), channel_id=1, source_target_pairs={{0,4},{1,5},{2,6},{3,7},{16,20},{17,21},{18,22},{19,23}} | collective-permute-start | bytes 1572872 | tf_op jit(solution)/shard_map/ppermute | solution.py:50
  15.5 16.5 %collective-permute-start.3 = (f32[2,16,4096]{2,1,0:T(8,128)}, f32[2,16,4096]{2,1,0:T(8,128)}, u32[]{:S(2)}, u32[]{:S(2)}) collective-permute-start(f32[2,16,4096]{2,1,0:T(8,128)} %get-tuple-element.12), channel_id=1, source_target_pairs={{12,8},{13,9},{14,10},{15,11},{28,24},{29,25},{30,26},{31,27}} | collective-permute-start | bytes 1572872 | tf_op jit(solution)/shard_map/ppermute | solution.py:51
  26.7 14.7 %collective-permute-start.1 = (f32[2,16,4096]{2,1,0:T(8,128)S(1)}, f32[2,16,4096]{2,1,0:T(8,128)}, u32[]{:S(2)}, u32[]{:S(2)}) collective-permute-start(f32[2,16,4096]{2,1,0:T(8,128)S(1)} %bitcast_add_fusion.2), channel_id=1, source_target_pairs={{0,4},{4,8},{1,5},{5,9},{2,6},{6,10},{3,7},{7,11},{16,20},{20,24},... | collective-permute-start | bytes 1572872 | tf_op jit(solution)/shard_map/ppermute | solution.py:50
  43.5 11.5 %collective-permute-start.4 = (f32[2,16,4096]{2,1,0:T(8,128)S(1)}, f32[2,16,4096]{2,1,0:T(8,128)S(1)}, u32[]{:S(2)}, u32[]{:S(2)}) collective-permute-start(f32[2,16,4096]{2,1,0:T(8,128)S(1)} %get-tuple-element.10), channel_id=1, source_target_pairs={{12,8},{8,4},{13,9},{9,5},{14,10},{10,6},{15,11},{11,7},{28,24},{2... | collective-permute-start | bytes 1572872 | tf_op jit(solution)/shard_map/ppermute | solution.py:51
  44.4 12.0 %copy-start.5 = (s32[1,32,16]{1,2,0:T(8,128)S(1)}, s32[1,32,16]{1,2,0:T(8,128)}, u32[]{:S(2)}) copy-start(s32[1,32,16]{1,2,0:T(8,128)} %param.7) | copy-start | bytes 6148
  49.1 14.8 %collective-permute-start.2 = (f32[2,16,4096]{2,1,0:T(8,128)}, f32[2,16,4096]{2,1,0:T(8,128)}, u32[]{:S(2)}, u32[]{:S(2)}) collective-permute-start(f32[2,16,4096]{2,1,0:T(8,128)} %get-tuple-element.9), channel_id=1, source_target_pairs={{0,4},{4,8},{8,12},{1,5},{5,9},{9,13},{2,6},{6,10},{10,14},{3,7},{... | collective-permute-start | bytes 1572872 | tf_op jit(solution)/shard_map/ppermute | solution.py:50
  55.0 15.9 %collective-permute-start.5 = (f32[2,16,4096]{2,1,0:T(8,128)S(1)}, f32[2,16,4096]{2,1,0:T(8,128)S(1)}, u32[]{:S(2)}, u32[]{:S(2)}) collective-permute-start(f32[2,16,4096]{2,1,0:T(8,128)S(1)} %bitcast_add_fusion.1), channel_id=1, source_target_pairs={{12,8},{8,4},{4,0},{13,9},{9,5},{5,1},{14,10},{10,6},{6,2},{15,11}... | collective-permute-start | bytes 1572872 | tf_op jit(solution)/shard_map/ppermute | solution.py:51
  60.7 11.6 %copy-start.1 = (bf16[1,1,32,16,8,256]{5,4,3,2,1,0:T(8,128)(2,1)S(1)}, bf16[1,1,32,16,8,256]{5,4,3,2,1,0:T(8,128)(2,1)}, u32[]{:S(2)}) copy-start(bf16[1,1,32,16,8,256]{5,4,3,2,1,0:T(8,128)(2,1)} %get-tuple-element.8) | copy-start | bytes 6291460
  73.9 1.6 %copy-start = (bf16[1,1,32,16,8,256]{5,4,3,2,1,0:T(8,128)(2,1)S(1)}, bf16[1,1,32,16,8,256]{5,4,3,2,1,0:T(8,128)(2,1)}, u32[]{:S(2)}) copy-start(bf16[1,1,32,16,8,256]{5,4,3,2,1,0:T(8,128)(2,1)} %get-tuple-element.7) | copy-start | bytes 6291460
  79.8 9.4 %all-to-all-start = ((bf16[2,32,16,128]{3,2,0,1:T(8,128)(2,1)}), bf16[2,32,16,128]{3,2,0,1:T(8,128)(2,1)S(1)}, u32[]{:S(2)}, u32[]{:S(2)}) async-start(bf16[2,32,16,128]{3,2,0,1:T(8,128)(2,1)} %fusion.27), calls=%async_computation | async-start | bytes 524288 | tf_op jit(solution)/shard_map/all_to_all | solution.py:122
  92.3 2.2 %copy-start.3 = (bf16[1,1,8,64,8,256]{5,4,3,2,1,0:T(8,128)(2,1)S(1)}, bf16[1,1,8,64,8,256]{5,4,3,2,1,0:T(8,128)(2,1)}, u32[]{:S(2)}) copy-start(bf16[1,1,8,64,8,256]{5,4,3,2,1,0:T(8,128)(2,1)} %get-tuple-element.6) | copy-start | bytes 6291460
  92.3 2.2 %copy-start.4 = (bf16[8,64,8,16]{1,3,2,0:T(8,128)(2,1)S(1)}, bf16[8,64,8,16]{1,3,2,0:T(8,128)(2,1)}, u32[]{:S(2)}) copy-start(bf16[8,64,8,16]{1,3,2,0:T(8,128)(2,1)} %reshape.561) | copy-start | bytes 393220
  96.2 9.1 %collective-permute-start.7 = (bf16[2,16,2048]{2,1,0:T(8,128)(2,1)S(1)}, bf16[2,16,2048]{2,1,0:T(8,128)(2,1)S(1)}, u32[]{:S(2)}, u32[]{:S(2)}) collective-permute-start(bf16[2,16,2048]{2,1,0:T(8,128)(2,1)S(1)} %constant_dynamic-update-slice_fusion), channel_id=1, source_target_pairs={{4,0},{8,4},{12,8},{5,1},{9,5},{13,9},{6,2},{10,6},{14,10},{7,3},{... | collective-permute-start | bytes 393224 | tf_op jit(solution)/shard_map/ppermute | solution.py:63
  97.5 7.1 %collective-permute-start.6 = (bf16[2,16,2048]{2,1,0:T(8,128)(2,1)S(1)}, bf16[2,16,2048]{2,1,0:T(8,128)(2,1)S(1)}, u32[]{:S(2)}, u32[]{:S(2)}) collective-permute-start(bf16[2,16,2048]{2,1,0:T(8,128)(2,1)S(1)} %constant_dynamic-update-slice_fusion), channel_id=1, source_target_pairs={{0,4},{4,8},{8,12},{1,5},{5,9},{9,13},{2,6},{6,10},{10,14},{3,7},{... | collective-permute-start | bytes 393224 | tf_op jit(solution)/shard_map/ppermute | solution.py:62
  104.6 2.1 %collective-permute-start.8 = (bf16[2,16,2048]{2,1,0:T(8,128)(2,1)S(1)}, bf16[2,16,2048]{2,1,0:T(8,128)(2,1)S(1)}, u32[]{:S(2)}, u32[]{:S(2)}) collective-permute-start(bf16[2,16,2048]{2,1,0:T(8,128)(2,1)S(1)} %collective-permute-done.6), channel_id=1, source_target_pairs={{4,8},{8,12},{5,9},{9,13},{6,10},{10,14},{7,11},{11,15},{20,24},{2... | collective-permute-start | bytes 393224 | tf_op jit(solution)/shard_map/ppermute | solution.py:62
  105.3 10.3 %collective-permute-start.9 = (bf16[2,16,2048]{2,1,0:T(8,128)(2,1)S(1)}, bf16[2,16,2048]{2,1,0:T(8,128)(2,1)S(1)}, u32[]{:S(2)}, u32[]{:S(2)}) collective-permute-start(bf16[2,16,2048]{2,1,0:T(8,128)(2,1)S(1)} %collective-permute-done.7), channel_id=1, source_target_pairs={{4,0},{8,4},{5,1},{9,5},{6,2},{10,6},{7,3},{11,7},{20,16},{24,20},... | collective-permute-start | bytes 393224 | tf_op jit(solution)/shard_map/ppermute | solution.py:63
  106.7 10.3 %collective-permute-start.10 = (bf16[2,16,2048]{2,1,0:T(8,128)(2,1)S(1)}, bf16[2,16,2048]{2,1,0:T(8,128)(2,1)S(1)}, u32[]{:S(2)}, u32[]{:S(2)}) collective-permute-start(bf16[2,16,2048]{2,1,0:T(8,128)(2,1)S(1)} %collective-permute-done.8), channel_id=1, source_target_pairs={{8,12},{9,13},{10,14},{11,15},{24,28},{25,29},{26,30},{27,31}} | collective-permute-start | bytes 393224 | tf_op jit(solution)/shard_map/ppermute | solution.py:62
  115.6 6.8 %collective-permute-start.11 = (bf16[2,16,2048]{2,1,0:T(8,128)(2,1)S(1)}, bf16[2,16,2048]{2,1,0:T(8,128)(2,1)S(1)}, u32[]{:S(2)}, u32[]{:S(2)}) collective-permute-start(bf16[2,16,2048]{2,1,0:T(8,128)(2,1)S(1)} %collective-permute-done.9), channel_id=1, source_target_pairs={{4,0},{5,1},{6,2},{7,3},{20,16},{21,17},{22,18},{23,19}} | collective-permute-start | bytes 393224 | tf_op jit(solution)/shard_map/ppermute | solution.py:63

commit v3 on v1

--- a/solution.py
+++ b/solution.py
@@ -7,6 +7,7 @@
 
 NT = 640
 F0 = 40
+CHUNKS = 2
 
 
 def twiddle(freq_ids, time_ids):
@@ -49,17 +50,18 @@
     scale_time = 1.0 / math.sqrt(NT)
     freq_ids = jnp.arange(freq_total, dtype=jnp.int32)
     cosine, sine = twiddle(freq_ids, time_ids)
+    chunks = CHUNKS if virtual_sources % CHUNKS == 0 else 1
+    width = virtual_sources // chunks
 
-    forward = jnp.stack([cosine, -sine], 1).reshape(freq_total * 2, time_count)
-    flat_traces = traces.reshape(time_count * virtual_sources, source_count)
-    partial = jnp.dot(
-        spread_over(forward, virtual_sources), flat_traces, preferred_element_type=jnp.float32
+    forward = spread_over(
+        jnp.stack([cosine, -sine], 1).reshape(freq_total * 2, time_count), width
     )
-    partial = (partial * scale_time).astype(jnp.bfloat16)
-    partial = partial.reshape(freq_total, 2, virtual_sources, source_count)
-    spectrum = lax.psum_scatter(partial, "freq", scatter_dimension=0, tiled=True)[0]
-    spectral_tiles = spectrum.reshape(2, virtual_sources, columns, tile_width)
     emitter_factors = v_factors[0]
+    receiver_factors = u_factors[0]
+    rank_mask = (
+        jnp.arange(rank_positions, dtype=jnp.int32)[None, None, :, None]
+        < ranks[0][:, :, None, None]
+    )
 
     def source_product(left_operand_factors, right_operand_factors):
         return jnp.einsum(
@@ -69,25 +71,6 @@
             preferred_element_type=jnp.float32,
         )
 
-    real_coeff = source_product(emitter_factors[0], spectral_tiles[0]) - source_product(
-        emitter_factors[1], spectral_tiles[1]
-    )
-    imag_coeff = source_product(emitter_factors[0], spectral_tiles[1]) + source_product(
-        emitter_factors[1], spectral_tiles[0]
-    )
-    rank_mask = (
-        jnp.arange(rank_positions, dtype=jnp.int32)[None, None, :, None]
-        < ranks[0][:, :, None, None]
-    )
-    stacked = jnp.stack([real_coeff, imag_coeff])
-    coefficients = jnp.where(rank_mask[None], stacked, jnp.float32(0.0)).astype(jnp.bfloat16)
-    coefficients = coefficients.reshape(2, rows_all, columns, rank_positions * virtual_sources)
-    arrived = lax.all_to_all(coefficients, "tile", split_axis=1, concat_axis=2, tiled=True)
-    rows_local = arrived.shape[1]
-    columns_all = arrived.shape[2]
-    arrived = arrived.reshape(2, rows_local, columns_all, rank_positions, virtual_sources)
-    receiver_factors = u_factors[0]
-
     def receiver_product(left_operand_factors, right_operand_factors):
         return jnp.einsum(
             "mdlh,mdlu->umh",
@@ -96,19 +79,49 @@
             preferred_element_type=jnp.float32,
         )
 
-    real_recv = receiver_product(receiver_factors[0], arrived[0]) - receiver_product(
-        receiver_factors[1], arrived[1]
-    )
-    imag_recv = receiver_product(receiver_factors[0], arrived[1]) + receiver_product(
-        receiver_factors[1], arrived[0]
-    )
-    receivers = rows_local * tile_width
-    received = (
-        jnp.stack([real_recv, imag_recv])
-        .reshape(1, 2, virtual_sources, receivers)
-        .astype(jnp.bfloat16)
-    )
-    piece = lax.all_gather(received, "freq", axis=0, tiled=True)
+    sums = []
+    for part in range(chunks):
+        flat_traces = traces[:, part * width:(part + 1) * width, :].reshape(
+            time_count * width, source_count
+        )
+        partial = jnp.dot(forward, flat_traces, preferred_element_type=jnp.float32).reshape(
+            freq_total, 2, width, source_count
+        )
+        sums.append(lax.psum_scatter(partial, "freq", scatter_dimension=0, tiled=True))
+    pieces = []
+    for part in range(chunks):
+        summed = sums[part]
+        if pieces:
+            summed, pieces[-1] = lax.optimization_barrier((summed, pieces[-1]))
+        spectrum = (summed * scale_time).astype(jnp.bfloat16)[0]
+        spectral_tiles = spectrum.reshape(2, width, columns, tile_width)
+        real_coeff = source_product(emitter_factors[0], spectral_tiles[0]) - source_product(
+            emitter_factors[1], spectral_tiles[1]
+        )
+        imag_coeff = source_product(emitter_factors[0], spectral_tiles[1]) + source_product(
+            emitter_factors[1], spectral_tiles[0]
+        )
+        stacked = jnp.stack([real_coeff, imag_coeff])
+        coefficients = jnp.where(rank_mask[None], stacked, jnp.float32(0.0)).astype(jnp.bfloat16)
+        coefficients = coefficients.reshape(2, rows_all, columns, rank_positions * width)
+        arrived = lax.all_to_all(coefficients, "tile", split_axis=1, concat_axis=2, tiled=True)
+        rows_local = arrived.shape[1]
+        columns_all = arrived.shape[2]
+        arrived = arrived.reshape(2, rows_local, columns_all, rank_positions, width)
+        real_recv = receiver_product(receiver_factors[0], arrived[0]) - receiver_product(
+            receiver_factors[1], arrived[1]
+        )
+        imag_recv = receiver_product(receiver_factors[0], arrived[1]) + receiver_product(
+            receiver_factors[1], arrived[0]
+        )
+        receivers = rows_local * tile_width
+        received = (
+            jnp.stack([real_recv, imag_recv])
+            .reshape(1, 2, width, receivers)
+            .astype(jnp.bfloat16)
+        )
+        pieces.append(lax.all_gather(received, "freq", axis=0, tiled=True))
+    piece = jnp.concatenate(pieces, axis=2)
     count = piece.shape[0]
 
     backward = jnp.stack([cosine.T, -sine.T], 2).reshape(time_count, count * 2)

time: 103 us -> 137 us (1.33)
  matrix products: 29.4 us -> 47.6 us
  blocking collectives: 15.9 us -> 28.8 us
  starting transfers between devices: 3.59 us -> 7.09 us
  waiting for transfers between devices: 26.4 us -> 23 us
  other arithmetic: 1.38 us -> 3.11 us
    all_gather x1 -> x2, blocking collectives: 15.9 us -> 28.8 us  [per_device(): pieces.append(lax.all_gather(received, 'freq', axis=0, tiled=True))]
    dot_general x4 -> x8, matrix products: 7.62 us -> 17.1 us  [source_product(): jnp.einsum('ajrs,vjs->ajrv', left_operand_factors, right_operand_factors,...]
    reduce_scatter x1 -> x2, waiting for transfers between devices: 22.6 us -> 14.2 us  [per_device(): lax.psum_scatter(partial, 'freq', scatter_dimension=0, tiled=True)]
    dot_general x4 -> x8, matrix products: 3.72 us -> 8.98 us  [receiver_product(): jnp.einsum('mdlh,mdlu->umh', left_operand_factors, right_operand_factors,...]
    all_to_all x1 -> x2, waiting for transfers between devices: 3.81 us -> 8.77 us  [per_device(): lax.all_to_all(coefficients, 'tile', split_axis=1, concat_axis=2, tiled=T...]
    dot_general x1 -> x3, matrix products: 9.82 us -> 14.2 us  [the longest x2 13.8 us: per_device(): jnp.dot(forward, flat_traces, preferred_element_type=jnp.float32)]
    all_to_all x1 -> x2, starting transfers between devices: 3.59 us -> 7.05 us  [per_device(): lax.all_to_all(coefficients, 'tile', split_axis=1, concat_axis=2, tiled=T...]
    unnamed x20 -> x18, local copies, waits for them, and re-layouts: 0.18 us -> 2.26 us
  transfers between devices with their start and end apart: 2 -> 4, of which waited for: 2 -> 3; matrix products, arithmetic and copies ran while one was open for 9% -> 24% of each run, Pallas kernels for 0% -> 0%
where the time goes in v3:
time: 137 us; the launch traced here: 136 us
  matrix products  47.6 us (35%)
  blocking collectives  28.8 us (21%)
  waiting for transfers between devices  23 us (17%)
  between operations  13.8 us (10%)
  local copies, waits for them, and re-layouts  12.6 us (9%)
  starting transfers between devices  7.09 us (5%)
  other arithmetic  3.11 us (2%)
    all_gather x2, blocking collectives, per_device(): pieces.append(lax.all_gather(received, 'freq', axis=0, tiled=True))  28.8 us
    dot_general x8, matrix products, source_product(): jnp.einsum('ajrs,vjs->ajrv', left_operand_factors, right_operand_factors,...  17.1 us
    reduce_scatter x2, waiting for transfers between devices, per_device(): lax.psum_scatter(partial, 'freq', scatter_dimension=0, tiled=True)  14.2 us
    dot_general x2, matrix products, per_device(): jnp.dot(forward, flat_traces, preferred_element_type=jnp.float32)  13.8 us
    dot_general x8, matrix products, receiver_product(): jnp.einsum('mdlh,mdlu->umh', left_operand_factors, right_operand_factors,...  8.98 us
    all_to_all x2, waiting for transfers between devices, per_device(): lax.all_to_all(coefficients, 'tile', split_axis=1, concat_axis=2, tiled=T...  8.77 us
    all_to_all x2, starting transfers between devices, per_device(): lax.all_to_all(coefficients, 'tile', split_axis=1, concat_axis=2, tiled=T...  7.05 us
    dot_general x1, matrix products, per_device(): jnp.dot(spread_over(backward, virtual_sources), piece.reshape(count * 2 *...  6.02 us
  transfers between devices with their start and end apart: 4, of which 3 were waited for; matrix products, arithmetic and copies ran while one was open for 24% of the time, Pallas kernels for 0%

profile of v3, /device:TPU:0, one launch (start us, length us, event | category | flops | bytes accessed | tf_op | source)
XLA Modules:
  0.0 136.0 jit_solution(8641000433981534925)
XLA Ops:
  7.3 6.9 %fusion = f32[4,2,8,4096]{3,2,1,0:T(8,128)} fusion(bf16[4,2,8,1280]{3,2,1,0:T(8,128)(2,1)S(1)} %bitcast.242, bf16[160,16,4096]{2,1,0:T(8,128)(2,1)} %param.4), kind=kOutput, calls=%fused_computation.1 | convolution fusion | flops 671088640 | bytes 11698176 | tf_op jit(solution)/shard_map/dot_general | solution.py:87
  14.3 6.9 %fusion.2 = f32[4,2,8,4096]{3,2,1,0:T(8,128)} fusion(bf16[4,2,8,1280]{3,2,1,0:T(8,128)(2,1)S(1)} %bitcast.243, bf16[160,16,4096]{2,1,0:T(8,128)(2,1)} %param.4), kind=kOutput, calls=%fused_computation.3 | convolution fusion | flops 671088640 | bytes 11698176 | tf_op jit(solution)/shard_map/dot_general | solution.py:87
  21.9 5.1 %fusion.83 = (bf16[1,1,32,16,8,256]{5,4,3,2,1,0:T(8,128)(2,1)}, bf16[1,1,32,16,8,256]{5,4,3,2,1,0:T(8,128)(2,1)}) fusion(bf16[1,2,32,16,8,256]{5,4,3,2,1,0:T(8,128)(2,1)} %param.5), kind=kLoop, calls=%fused_computation.135 | loop fusion | bytes 8388608 | tf_op jit(solution)/shard_map/slice | solution.py:99
  27.0 1.7 %fusion.82 = (bf16[1,1,8,64,8,256]{5,4,3,2,1,0:T(8,128)(2,1)S(1)}, bf16[1,1,8,64,8,256]{5,4,3,2,1,0:T(8,128)(2,1)}) fusion(bf16[1,2,8,64,8,256]{5,4,3,2,1,0:T(8,128)(2,1)S(1)} %copy-done.5), kind=kLoop, calls=%fused_computation.134 | loop fusion | bytes 8388608 | tf_op jit(solution)/shard_map/slice | solution.py:111
  28.6 1.4 %convolution_convert_fusion = bf16[2560,8]{0,1:T(8,128)(2,1)S(1)} fusion(bf16[160,8]{0,1:T(8,128)(2,1)S(1)} %reshape.600, s32[2560]{0:T(1024)S(1)} %add_select_fusion), kind=kOutput, calls=%fused_computation.9 | convolution fusion | flops 6983680 | bytes 53760 | tf_op jit(solution)/shard_map/dot_general | solution.py:30
  30.0 14.2 %reduce-scatter.5.cloned.1.call-done = f32[1,2,8,4096]{3,2,1,0:T(8,128)} async-done(((f32[4,2,8,4096]{3,2,1,0:T(8,128)}), f32[1,2,8,4096]{3,2,1,0:T(8,128)}) %reduce-scatter.5.cloned.1.call-update) | async-done | bytes 262160 | tf_op jit(solution)/shard_map/reduce_scatter | solution.py:90
  44.2 1.1 multiply_convert_fusion.2
  45.4 3.2 %fusion.10 = f32[16,8,32,8]{2,1,3,0:T(8,128)S(1)} fusion(bf16[8,16,256,1]{2,0,3,1:T(8,128)(2,1)S(1)} %bitcast.229, bf16[1,1,32,16,8,256]{5,4,3,2,1,0:T(8,128)(2,1)} %get-tuple-element.12), kind=kOutput, calls=%fused_computation.19 | convolution fusion | flops 16777216 | bytes 2293760 | tf_op jit(solution)/shard_map/ajrs,vjs->ajrv/dot_general | solution.py:67
  48.6 1.5 %fusion.11 = f32[16,8,32,8]{2,1,3,0:T(8,128)S(1)} fusion(bf16[8,16,256,1]{2,0,3,1:T(8,128)(2,1)S(1)} %bitcast.233, bf16[1,1,32,16,8,256]{5,4,3,2,1,0:T(8,128)(2,1)S(1)} %copy-done.3), kind=kOutput, calls=%fused_computation.20 | convolution fusion | flops 16777216 | bytes 2293760 | tf_op jit(solution)/shard_map/ajrs,vjs->ajrv/dot_general | solution.py:67
  50.1 1.5 %fusion.28 = bf16[1,32,16,64]{1,3,2,0:T(8,128)(2,1)S(1)} fusion(f32[16,8,32,8]{2,1,3,0:T(8,128)S(1)} %fusion.10, bf16[8,16,256,1]{2,0,3,1:T(8,128)(2,1)S(1)} %bitcast.234, bf16[1,1,32,16,8,256]{5,4,3,2,1,0:T(8,128)(2,1)S(1)} %copy-done.1), kind=kOutput, calls=%fused_computation.37 | convolution fusion | flops 16842752 | bytes 2359296 | tf_op jit(solution)/shard_map/ajrs,vjs->ajrv/dot_general | solution.py:67
  51.8 3.1 %fusion.26 = bf16[1,32,16,64]{1,3,2,0:T(8,128)(2,1)S(1)} fusion(f32[16,8,32,8]{2,1,3,0:T(8,128)S(1)} %fusion.11, bf16[8,16,256,1]{2,0,3,1:T(8,128)(2,1)S(1)} %bitcast.230, bf16[1,1,32,16,8,256]{5,4,3,2,1,0:T(8,128)(2,1)} %get-tuple-element.11), kind=kOutput, calls=%fused_computation.35 | convolution fusion | flops 16842752 | bytes 2359296 | tf_op jit(solution)/shard_map/ajrs,vjs->ajrv/dot_general | solution.py:67
  55.2 0.9 reshape.620
  56.1 3.5 %all-to-all-start = ((bf16[4,2,8192]{2,1,0:T(2,128)(2,1)}), bf16[4,2,8192]{2,1,0:T(2,128)(2,1)S(1)}, u32[]{:S(2)}, u32[]{:S(2)}) async-start(bf16[4,2,8192]{2,1,0:T(2,128)(2,1)} %reshape.620), calls=%async_computation.2 | async-start | bytes 262144 | tf_op jit(solution)/shard_map/all_to_all | solution.py:107
  59.6 4.4 %all-to-all-done = bf16[4,2,8192]{2,1,0:T(2,128)(2,1)S(1)} async-done(((bf16[4,2,8192]{2,1,0:T(2,128)(2,1)}), bf16[4,2,8192]{2,1,0:T(2,128)(2,1)S(1)}, u32[]{:S(2)}, u32[]{:S(2)}) %all-to-all-start) | async-done | bytes 131104 | tf_op jit(solution)/shard_map/all_to_all | solution.py:107
  65.5 2.2 %fusion.34 = f32[8,8,256]{2,1,0:T(8,128)S(1)} fusion(bf16[8,64,8,8]{1,3,2,0:T(8,128)(2,1)S(1)} %squeeze.28, bf16[1,1,8,64,8,256]{5,4,3,2,1,0:T(8,128)(2,1)} %get-tuple-element.10), kind=kOutput, calls=%fused_computation.43 | convolution fusion | flops 16777216 | bytes 2228224 | tf_op jit(solution)/shard_map/mdlh,mdlu->umh/dot_general | solution.py:75
  68.3 0.5 fusion.46
  68.8 0.5 fusion.45
  69.3 14.4 %all_gather.6 = bf16[4,2,8,2048]{3,2,1,0:T(8,128)(2,1)S(1)} all-gather(bf16[1,2,8,2048]{3,2,1,0:T(8,128)(2,1)S(1)} %pad_maximum_fusion.1), channel_id=1, replica_groups=mesh['groups'=2,'freq'=4,'tile'=4] {'freq'}, dimensions={0}, use_global_device_ids=true | all-gather | bytes 327680 | tf_op jit(solution)/shard_map/all_gather | solution.py:123
  83.8 1.1 multiply_convert_fusion.1
  84.9 3.2 %fusion.8 = f32[16,8,32,8]{2,1,3,0:T(8,128)S(1)} fusion(bf16[8,16,256,1]{2,0,3,1:T(8,128)(2,1)S(1)} %bitcast.231, bf16[1,1,32,16,8,256]{5,4,3,2,1,0:T(8,128)(2,1)} %get-tuple-element.12), kind=kOutput, calls=%fused_computation.17 | convolution fusion | flops 16777216 | bytes 2293760 | tf_op jit(solution)/shard_map/ajrs,vjs->ajrv/dot_general | solution.py:67
  88.1 1.5 %fusion.9 = f32[16,8,32,8]{2,1,3,0:T(8,128)S(1)} fusion(bf16[8,16,256,1]{2,0,3,1:T(8,128)(2,1)S(1)} %bitcast.235, bf16[1,1,32,16,8,256]{5,4,3,2,1,0:T(8,128)(2,1)S(1)} %copy-done.4), kind=kOutput, calls=%fused_computation.18 | convolution fusion | flops 16777216 | bytes 2293760 | tf_op jit(solution)/shard_map/ajrs,vjs->ajrv/dot_general | solution.py:67
  89.6 1.5 %fusion.32 = bf16[1,32,16,64]{1,3,2,0:T(8,128)(2,1)S(1)} fusion(f32[16,8,32,8]{2,1,3,0:T(8,128)S(1)} %fusion.8, bf16[8,16,256,1]{2,0,3,1:T(8,128)(2,1)S(1)} %bitcast.236, bf16[1,1,32,16,8,256]{5,4,3,2,1,0:T(8,128)(2,1)S(1)} %copy-done.2), kind=kOutput, calls=%fused_computation.41 | convolution fusion | flops 16842752 | bytes 2359296 | tf_op jit(solution)/shard_map/ajrs,vjs->ajrv/dot_general | solution.py:67
  91.2 1.5 %fusion.30 = bf16[1,32,16,64]{1,3,2,0:T(8,128)(2,1)S(1)} fusion(f32[16,8,32,8]{2,1,3,0:T(8,128)S(1)} %fusion.9, bf16[8,16,256,1]{2,0,3,1:T(8,128)(2,1)S(1)} %bitcast.232, bf16[1,1,32,16,8,256]{5,4,3,2,1,0:T(8,128)(2,1)S(1)} %copy-done.2), kind=kOutput, calls=%fused_computation.39 | convolution fusion | flops 16842752 | bytes 2359296 | tf_op jit(solution)/shard_map/ajrs,vjs->ajrv/dot_general | solution.py:67
  93.1 0.9 reshape.622
  94.0 3.5 %all-to-all-start.1 = ((bf16[4,2,8192]{2,1,0:T(2,128)(2,1)}), bf16[4,2,8192]{2,1,0:T(2,128)(2,1)S(1)}, u32[]{:S(2)}, u32[]{:S(2)}) async-start(bf16[4,2,8192]{2,1,0:T(2,128)(2,1)} %reshape.622), calls=%async_computation.3 | async-start | bytes 262144 | tf_op jit(solution)/shard_map/all_to_all | solution.py:107
  97.6 4.4 %all-to-all-done.1 = bf16[4,2,8192]{2,1,0:T(2,128)(2,1)S(1)} async-done(((bf16[4,2,8192]{2,1,0:T(2,128)(2,1)}), bf16[4,2,8192]{2,1,0:T(2,128)(2,1)S(1)}, u32[]{:S(2)}, u32[]{:S(2)}) %all-to-all-start.1) | async-done | bytes 131104 | tf_op jit(solution)/shard_map/all_to_all | solution.py:107
  102.8 2.1 %fusion.35 = f32[8,8,256]{2,1,0:T(8,128)S(1)} fusion(bf16[8,64,8,8]{1,3,2,0:T(8,128)(2,1)S(1)} %squeeze.69, bf16[1,1,8,64,8,256]{5,4,3,2,1,0:T(8,128)(2,1)} %get-tuple-element.10), kind=kOutput, calls=%fused_computation.44 | convolution fusion | flops 16777216 | bytes 2228224 | tf_op jit(solution)/shard_map/mdlh,mdlu->umh/dot_general | solution.py:75
  105.6 2.1 %fusion.36 = f32[8,8,256]{2,1,0:T(8,128)S(1)} fusion(bf16[8,64,8,8]{1,3,2,0:T(8,128)(2,1)S(1)} %squeeze.68, bf16[1,1,8,64,8,256]{5,4,3,2,1,0:T(8,128)(2,1)} %get-tuple-element.10), kind=kOutput, calls=%fused_computation.45 | convolution fusion | flops 16777216 | bytes 2228224 | tf_op jit(solution)/shard_map/mdlh,mdlu->umh/dot_general | solution.py:75
  107.7 0.5 fusion.47
  108.2 0.5 fusion.48
  108.7 14.4 %all_gather.7 = bf16[4,2,8,2048]{3,2,1,0:T(8,128)(2,1)S(1)} all-gather(bf16[1,2,8,2048]{3,2,1,0:T(8,128)(2,1)S(1)} %pad_maximum_fusion.2), channel_id=1, replica_groups=mesh['groups'=2,'freq'=4,'tile'=4] {'freq'}, dimensions={0}, use_global_device_ids=true | all-gather | bytes 327680 | tf_op jit(solution)/shard_map/all_gather | solution.py:123
  123.1 6.0 %multiply_convert_fusion = bf16[2560,2048]{1,0:T(8,128)(2,1)} fusion(bf16[128,2048]{1,0:T(8,128)(2,1)S(1)} %bitcast.224, bf16[2560,8]{0,1:T(8,128)(2,1)S(1)} %convolution_convert_fusion, s32[128]{0:T(128)S(1)} %get-tuple-element.26, s32[2560]{0:T(1024)S(1)} %add_select_fusion.1, s32[128]{0:T(128)S(1)} %get-tuple-element.25), kind=kOutput, calls=%fused_computation | convolution fusion | flops 1358889984 | bytes 11062272 | tf_op jit(solution)/shard_map/dot_general | solution.py:128
  (66 shorter events, 5.8 us)
Async XLA Ops:
  6.5 37.7 %reduce-scatter.5.cloned.1.call-start = ((), (), s32[]{:S(2)}) async-start(), calls=%async_computation.5 | async-start | bytes 1310720 | tf_op jit(solution)/shard_map/reduce_scatter | solution.py:90
  14.2 7.3 %copy-start.6 = (s32[1,32,16]{1,2,0:T(8,128)S(1)}, s32[1,32,16]{1,2,0:T(8,128)}, u32[]{:S(2)}) copy-start(s32[1,32,16]{1,2,0:T(8,128)} %param.7) | copy-start | bytes 6148
  14.2 69.5 %reduce-scatter.3.cloned.1.call-start = ((), (), s32[]{:S(2)}) async-start(), calls=%async_computation.4 | async-start | bytes 1310720 | tf_op jit(solution)/shard_map/reduce_scatter | solution.py:90
  21.9 5.1 %copy-start.5 = (bf16[1,2,8,64,8,256]{5,4,3,2,1,0:T(8,128)(2,1)S(1)}, bf16[1,2,8,64,8,256]{5,4,3,2,1,0:T(8,128)(2,1)}, u32[]{:S(2)}) copy-start(bf16[1,2,8,64,8,256]{5,4,3,2,1,0:T(8,128)(2,1)} %param.6) | copy-start | bytes 12582916
  44.2 4.4 %copy-start.3 = (bf16[1,1,32,16,8,256]{5,4,3,2,1,0:T(8,128)(2,1)S(1)}, bf16[1,1,32,16,8,256]{5,4,3,2,1,0:T(8,128)(2,1)}, u32[]{:S(2)}) copy-start(bf16[1,1,32,16,8,256]{5,4,3,2,1,0:T(8,128)(2,1)} %get-tuple-element.12) | copy-start | bytes 6291460
  45.3 4.7 %copy-start.1 = (bf16[1,1,32,16,8,256]{5,4,3,2,1,0:T(8,128)(2,1)S(1)}, bf16[1,1,32,16,8,256]{5,4,3,2,1,0:T(8,128)(2,1)}, u32[]{:S(2)}) copy-start(bf16[1,1,32,16,8,256]{5,4,3,2,1,0:T(8,128)(2,1)} %get-tuple-element.11) | copy-start | bytes 6291460
  56.1 7.9 %all-to-all-start = ((bf16[4,2,8192]{2,1,0:T(2,128)(2,1)}), bf16[4,2,8192]{2,1,0:T(2,128)(2,1)S(1)}, u32[]{:S(2)}, u32[]{:S(2)}) async-start(bf16[4,2,8192]{2,1,0:T(2,128)(2,1)} %reshape.620), calls=%async_computation.2 | async-start | bytes 262144 | tf_op jit(solution)/shard_map/all_to_all | solution.py:107
  65.5 2.3 %copy-start = (bf16[1,1,8,64,8,256]{5,4,3,2,1,0:T(8,128)(2,1)S(1)}, bf16[1,1,8,64,8,256]{5,4,3,2,1,0:T(8,128)(2,1)}, u32[]{:S(2)}) copy-start(bf16[1,1,8,64,8,256]{5,4,3,2,1,0:T(8,128)(2,1)} %get-tuple-element.10) | copy-start | bytes 6291460
  83.8 4.4 %copy-start.4 = (bf16[1,1,32,16,8,256]{5,4,3,2,1,0:T(8,128)(2,1)S(1)}, bf16[1,1,32,16,8,256]{5,4,3,2,1,0:T(8,128)(2,1)}, u32[]{:S(2)}) copy-start(bf16[1,1,32,16,8,256]{5,4,3,2,1,0:T(8,128)(2,1)} %get-tuple-element.12) | copy-start | bytes 6291460
  84.9 4.7 %copy-start.2 = (bf16[1,1,32,16,8,256]{5,4,3,2,1,0:T(8,128)(2,1)S(1)}, bf16[1,1,32,16,8,256]{5,4,3,2,1,0:T(8,128)(2,1)}, u32[]{:S(2)}) copy-start(bf16[1,1,32,16,8,256]{5,4,3,2,1,0:T(8,128)(2,1)} %get-tuple-element.11) | copy-start | bytes 6291460
  94.0 7.9 %all-to-all-start.1 = ((bf16[4,2,8192]{2,1,0:T(2,128)(2,1)}), bf16[4,2,8192]{2,1,0:T(2,128)(2,1)S(1)}, u32[]{:S(2)}, u32[]{:S(2)}) async-start(bf16[4,2,8192]{2,1,0:T(2,128)(2,1)} %reshape.622), calls=%async_computation.3 | async-start | bytes 262144 | tf_op jit(solution)/shard_map/all_to_all | solution.py:107
Sparse Core Ops, SparseCore 0:
  14.3 29.8 reduce-scatter.4
  46.6 25.7 reduce-scatter.2

commit v4 on v1

--- a/solution.py
+++ b/solution.py
@@ -54,32 +54,25 @@
     flat_traces = traces.reshape(time_count * virtual_sources, source_count)
     partial = jnp.dot(
         spread_over(forward, virtual_sources), flat_traces, preferred_element_type=jnp.float32
-    )
-    partial = (partial * scale_time).astype(jnp.bfloat16)
-    partial = partial.reshape(freq_total, 2, virtual_sources, source_count)
-    spectrum = lax.psum_scatter(partial, "freq", scatter_dimension=0, tiled=True)[0]
+    ).reshape(freq_total, 2, virtual_sources, source_count)
+    summed = lax.psum_scatter(partial, "freq", scatter_dimension=0, tiled=True)
+    spectrum = (summed * scale_time).astype(jnp.bfloat16)[0]
     spectral_tiles = spectrum.reshape(2, virtual_sources, columns, tile_width)
     emitter_factors = v_factors[0]
-
-    def source_product(left_operand_factors, right_operand_factors):
-        return jnp.einsum(
-            "ajrs,vjs->ajrv",
-            left_operand_factors,
-            right_operand_factors,
-            preferred_element_type=jnp.float32,
-        )
-
-    real_coeff = source_product(emitter_factors[0], spectral_tiles[0]) - source_product(
-        emitter_factors[1], spectral_tiles[1]
+    real_part, imag_part = spectral_tiles[0], spectral_tiles[1]
+    stacked_spectrum = jnp.stack(
+        [jnp.stack([real_part, -imag_part]), jnp.stack([imag_part, real_part])]
     )
-    imag_coeff = source_product(emitter_factors[0], spectral_tiles[1]) + source_product(
-        emitter_factors[1], spectral_tiles[0]
+    stacked = jnp.einsum(
+        "iajrs,oivjs->oajrv",
+        emitter_factors,
+        stacked_spectrum,
+        preferred_element_type=jnp.float32,
     )
     rank_mask = (
         jnp.arange(rank_positions, dtype=jnp.int32)[None, None, :, None]
         < ranks[0][:, :, None, None]
     )
-    stacked = jnp.stack([real_coeff, imag_coeff])
     coefficients = jnp.where(rank_mask[None], stacked, jnp.float32(0.0)).astype(jnp.bfloat16)
     coefficients = coefficients.reshape(2, rows_all, columns, rank_positions * virtual_sources)
     arrived = lax.all_to_all(coefficients, "tile", split_axis=1, concat_axis=2, tiled=True)
@@ -87,24 +80,18 @@
     columns_all = arrived.shape[2]
     arrived = arrived.reshape(2, rows_local, columns_all, rank_positions, virtual_sources)
     receiver_factors = u_factors[0]
-
-    def receiver_product(left_operand_factors, right_operand_factors):
-        return jnp.einsum(
-            "mdlh,mdlu->umh",
-            left_operand_factors,
-            right_operand_factors,
-            preferred_element_type=jnp.float32,
-        )
-
-    real_recv = receiver_product(receiver_factors[0], arrived[0]) - receiver_product(
-        receiver_factors[1], arrived[1]
-    )
-    imag_recv = receiver_product(receiver_factors[0], arrived[1]) + receiver_product(
-        receiver_factors[1], arrived[0]
+    real_arrived, imag_arrived = arrived[0], arrived[1]
+    stacked_arrived = jnp.stack(
+        [jnp.stack([real_arrived, -imag_arrived]), jnp.stack([imag_arrived, real_arrived])]
     )
     receivers = rows_local * tile_width
     received = (
-        jnp.stack([real_recv, imag_recv])
+        jnp.einsum(
+            "imdlh,oimdlu->oumh",
+            receiver_factors,
+            stacked_arrived,
+            preferred_element_type=jnp.float32,
+        )
         .reshape(1, 2, virtual_sources, receivers)
         .astype(jnp.bfloat16)
     )

time: 103 us -> 119 us (1.16)
  waiting for transfers between devices: 26.4 us -> 51 us
  local copies, waits for them, and re-layouts: 12 us -> 3.93 us
    reduce_scatter x1, waiting for transfers between devices: 22.6 us -> 46.4 us  [per_device(): summed = lax.psum_scatter(partial, 'freq', scatter_dimension=0, tiled=True)]
    slice x4 -> x5, local copies, waits for them, and re-layouts: 7.72 us -> 1.25 us  [the longest x3 1.19 us: per_device(): real_arrived, imag_arrived = (arrived[0], arrived[1])]
    squeeze x4 -> x2, local copies, waits for them, and re-layouts: 3.06 us -> 1.17 us  [per_device(): real_arrived, imag_arrived = (arrived[0], arrived[1])]
    dot_general x8 -> x3, matrix products: 11.3 us -> 9.57 us  [the longest x1 5.65 us: per_device(): jnp.einsum('iajrs,oivjs->oajrv', emitter_factors, stacked_spectrum, prefe...]
    dot_general x1, matrix products: 9.82 us -> 11.6 us  [per_device(): jnp.dot(spread_over(forward, virtual_sources), flat_traces, preferred_ele...]
    reshape x0 -> x1, local copies, waits for them, and re-layouts: none -> 1.25 us  [per_device(): coefficients.reshape(2, rows_all, columns, rank_positions * virtual_sources)]
  transfers between devices with their start and end apart: 2 -> 2, of which waited for: 2 -> 2; matrix products, arithmetic and copies ran while one was open for 9% -> 1% of each run, Pallas kernels for 0% -> 0%
where the time goes in v4:
time: 119 us; the launch traced here: 118 us
  waiting for transfers between devices  51 us (43%)
  matrix products  28.5 us (24%)
  blocking collectives  15.7 us (13%)
  between operations  13.6 us (11%)
  local copies, waits for them, and re-layouts  3.93 us (3%)
  starting transfers between devices  3.41 us (3%)
  other arithmetic  2.02 us (2%)
    reduce_scatter x1, waiting for transfers between devices, per_device(): summed = lax.psum_scatter(partial, 'freq', scatter_dimension=0, tiled=True)  46.4 us
    all_gather x1, blocking collectives, per_device(): piece = lax.all_gather(received, 'freq', axis=0, tiled=True)  15.7 us
    dot_general x1, matrix products, per_device(): jnp.dot(spread_over(forward, virtual_sources), flat_traces, preferred_ele...  11.6 us
    dot_general x1, matrix products, per_device(): jnp.dot(spread_over(backward, virtual_sources), piece.reshape(count * 2 *...  5.99 us
    dot_general x1, matrix products, per_device(): jnp.einsum('iajrs,oivjs->oajrv', emitter_factors, stacked_spectrum, prefe...  5.65 us
    all_to_all x1, waiting for transfers between devices, per_device(): lax.all_to_all(coefficients, 'tile', split_axis=1, concat_axis=2, tiled=T...  4.6 us
    all_to_all x1, starting transfers between devices, per_device(): lax.all_to_all(coefficients, 'tile', split_axis=1, concat_axis=2, tiled=T...  3.41 us
    dot_general x1, matrix products, per_device(): jnp.einsum('imdlh,oimdlu->oumh', receiver_factors, stacked_arrived, prefe...  3.25 us
  transfers between devices with their start and end apart: 2, of which 2 were waited for; matrix products, arithmetic and copies ran while one was open for 1% of the time, Pallas kernels for 0%

profile of v4, /device:TPU:0, one launch (start us, length us, event | category | flops | bytes accessed | tf_op | source)
XLA Modules:
  0.0 118.2 jit_solution(5242468722377841497)
XLA Ops:
  6.5 0.0 reduce-scatter.2.cloned.1.call-start
  6.5 0.1 fusion.46
  6.7 0.1 cosine_convert_fusion
  6.9 0.7 fusion.5
  7.6 0.0 copy-start
  7.6 11.6 %fusion.54 = f32[4,2,16,4096]{3,2,1,0:T(8,128)} fusion(bf16[4,2,16,2560]{3,2,1,0:T(8,128)(2,1)S(1)} %bitcast.77, bf16[2560,4096,1,1]{1,0,3,2:T(8,128)(2,1)} %bitcast.73), kind=kOutput, calls=%fused_computation.84 | convolution fusion | flops 2684354560 | bytes 23724032 | tf_op jit(solution)/shard_map/dot_general | solution.py:55
  19.2 0.0 reduce-scatter.2.cloned.1.call-update
  19.2 0.1 fusion.45
  19.3 0.1 cosine_convert_fusion.1
  19.5 0.0 copy-done
  19.5 46.4 %reduce-scatter.2.cloned.1.call-done = f32[1,2,16,4096]{3,2,1,0:T(8,128)} async-done(((f32[4,2,16,4096]{3,2,1,0:T(8,128)}), f32[1,2,16,4096]{3,2,1,0:T(8,128)}) %reduce-scatter.2.cloned.1.call-update) | async-done | bytes 524304 | tf_op jit(solution)/shard_map/reduce_scatter | solution.py:58
  65.9 1.1 multiply_convert_fusion.1
  67.1 0.1 copy_negate_fusion
  67.2 5.7 %fusion.6 = bf16[2,32,16,8,16]{1,4,3,0,2:T(8,128)(2,1)S(1)} fusion(bf16[2,32,16,8,256,1]{4,3,2,1,0,5:T(8,128)(2,1)} %bitcast.83, pred[32,16,8]{0,2,1:T(8,128)(4,1)S(1)} %iota_compare_fusion.5, bf16[1,2,16,16,256]{4,2,1,0,3:T(8,128)(2,1)S(1)} %get-tuple-element.12, bf16[1,2,16,16,256]{4,2,1,0,3:T(8,128)(2,1)S(1)} %get-tuple-element.11), kind=kOutput, calls=%fused_computation.12 | convolution fusion | flops 135528448 | bytes 4984832 | tf_op jit(solution)/shard_map/iajrs,oivjs->oajrv/dot_general | solution.py:66
  72.9 1.2 %copy.65 = bf16[2,32,16,128]{3,2,0,1:T(8,128)(2,1)} copy(bf16[2,32,16,128]{1,3,0,2:T(8,128)(2,1)S(1)} %bitcast.75) | data formatting | bytes 524288 | tf_op jit(solution)/shard_map/reshape | solution.py:77
  74.1 3.4 %all-to-all-start = ((bf16[2,32,16,128]{3,2,0,1:T(8,128)(2,1)}), bf16[2,32,16,128]{3,2,0,1:T(8,128)(2,1)S(1)}, u32[]{:S(2)}, u32[]{:S(2)}) async-start(bf16[2,32,16,128]{3,2,0,1:T(8,128)(2,1)} %copy.65), calls=%async_computation.1 | async-start | bytes 524288 | tf_op jit(solution)/shard_map/all_to_all | solution.py:78
  77.6 1.4 %convolution_convert_fusion = bf16[2560,8]{0,1:T(8,128)(2,1)S(1)} fusion(bf16[160,8]{0,1:T(8,128)(2,1)S(1)} %reshape.520, s32[2560]{0:T(1024)S(1)} %get-tuple-element.15), kind=kOutput, calls=%fused_computation.9 | convolution fusion | flops 6983680 | bytes 53760 | tf_op jit(solution)/shard_map/dot_general | solution.py:29
  79.0 4.6 %all-to-all-done = bf16[2,32,16,128]{3,2,0,1:T(8,128)(2,1)S(1)} async-done(((bf16[2,32,16,128]{3,2,0,1:T(8,128)(2,1)}), bf16[2,32,16,128]{3,2,0,1:T(8,128)(2,1)S(1)}, u32[]{:S(2)}, u32[]{:S(2)}) %all-to-all-start) | async-done | bytes 262176 | tf_op jit(solution)/shard_map/all_to_all | solution.py:78
  83.6 0.6 copy.86
  84.3 0.5 reshape.533
  84.8 0.1 neg.43
  84.9 0.6 copy.85
  85.5 0.5 reshape.532
  86.0 0.2 maximum_bitcast_fusion.2
  86.3 3.2 %fusion.16 = bf16[2,16,8,256]{3,1,0,2:T(8,128)(2,1)S(1)} fusion(bf16[2,8,64,8,256,1]{4,3,2,1,0,5:T(8,128)(2,1)} %bitcast.84, bf16[1,2,8,64,8,16]{3,5,4,1,0,2:T(8,128)(2,1)S(1)} %get-tuple-element.6, bf16[1,2,8,64,8,16]{3,5,4,1,0,2:T(8,128)(2,1)S(1)} %get-tuple-element.5), kind=kOutput, calls=%fused_computation.17 | convolution fusion | flops 134545408 | bytes 4849664 | tf_op jit(solution)/shard_map/imdlh,oimdlu->oumh/dot_general | solution.py:89
  89.5 0.1 copy.74
  89.6 0.1 convert_element_type.125
  89.7 15.7 %all_gather.3 = bf16[4,2,16,2048]{3,2,1,0:T(8,128)(2,1)S(1)} all-gather(bf16[1,2,16,2048]{3,2,1,0:T(8,128)(2,1)S(1)} %convert_element_type.125), channel_id=1, replica_groups=mesh['groups'=2,'freq'=4,'tile'=4] {'freq'}, dimensions={0}, use_global_device_ids=true | all-gather | bytes 655360 | tf_op jit(solution)/shard_map/all_gather | solution.py:98
  105.4 6.0 %multiply_convert_fusion = bf16[2560,2048]{1,0:T(8,128)(2,1)} fusion(bf16[128,2048]{1,0:T(8,128)(2,1)S(1)} %bitcast.74, bf16[2560,8]{0,1:T(8,128)(2,1)S(1)} %convolution_convert_fusion, s32[128]{0:T(128)S(1)} %get-tuple-element.18, s32[2560]{0:T(1024)S(1)} %get-tuple-element.16, s32[128]{0:T(128)S(1)} %get-tuple-element.17), kind=kOutput, calls=%fused_computation | convolution fusion | flops 1358889984 | bytes 11062272 | tf_op jit(solution)/shard_map/dot_general | solution.py:102
  (18 shorter events, 0.3 us)
Async XLA Ops:
  6.5 59.4 %reduce-scatter.2.cloned.1.call-start = ((), (), s32[]{:S(2)}) async-start(), calls=%async_computation.2 | async-start | bytes 2621440 | tf_op jit(solution)/shard_map/reduce_scatter | solution.py:58
  7.6 11.9 %copy-start = (s32[1,32,16]{1,2,0:T(8,128)S(1)}, s32[1,32,16]{1,2,0:T(8,128)}, u32[]{:S(2)}) copy-start(s32[1,32,16]{1,2,0:T(8,128)} %param.7) | copy-start | bytes 6148
  74.1 9.4 %all-to-all-start = ((bf16[2,32,16,128]{3,2,0,1:T(8,128)(2,1)}), bf16[2,32,16,128]{3,2,0,1:T(8,128)(2,1)S(1)}, u32[]{:S(2)}, u32[]{:S(2)}) async-start(bf16[2,32,16,128]{3,2,0,1:T(8,128)(2,1)} %copy.65), calls=%async_computation.1 | async-start | bytes 524288 | tf_op jit(solution)/shard_map/all_to_all | solution.py:78
Sparse Core Ops, SparseCore 0:
  19.3 46.5 reduce-scatter.1

commit v5 on v4

--- a/solution.py
+++ b/solution.py
@@ -55,7 +55,10 @@
     partial = jnp.dot(
         spread_over(forward, virtual_sources), flat_traces, preferred_element_type=jnp.float32
     ).reshape(freq_total, 2, virtual_sources, source_count)
-    summed = lax.psum_scatter(partial, "freq", scatter_dimension=0, tiled=True)
+    gathered = lax.all_to_all(partial, "freq", split_axis=0, concat_axis=0, tiled=True)
+    summed = gathered.reshape(
+        lax.axis_size("freq"), freq_local, 2, virtual_sources, source_count
+    ).sum(axis=0)
     spectrum = (summed * scale_time).astype(jnp.bfloat16)[0]
     spectral_tiles = spectrum.reshape(2, virtual_sources, columns, tile_width)
     emitter_factors = v_factors[0]

time: 119 us -> 112 us (0.941)
  between operations: 13.6 us -> 0.22 us
  starting transfers between devices: 3.41 us -> 9.86 us
  waiting for transfers between devices: 51 us -> 52.5 us
    all_to_all x0 -> x1, waiting for transfers between devices: none -> 47.9 us  [per_device(): lax.all_to_all(partial, 'freq', split_axis=0, concat_axis=0, tiled=True)]
    reduce_scatter x1 -> x0, waiting for transfers between devices: 46.4 us -> none  [per_device(): summed = lax.psum_scatter(partial, 'freq', scatter_dimension=0, tiled=True)]
    all_to_all x0 -> x1, starting transfers between devices: none -> 6.45 us  [per_device(): lax.all_to_all(partial, 'freq', split_axis=0, concat_axis=0, tiled=True)]
  transfers between devices with their start and end apart: 2 -> 2, of which waited for: 2 -> 2; matrix products, arithmetic and copies ran while one was open for 1% -> 2% of each run, Pallas kernels for 0% -> 0%
where the time goes in v5:
time: 112 us
  waiting for transfers between devices  52.5 us (47%)
  matrix products  28.6 us (26%)
  blocking collectives  15.6 us (14%)
  starting transfers between devices  9.86 us (9%)
  local copies, waits for them, and re-layouts  3.94 us (4%)
  other arithmetic  1.14 us (1%)
    all_to_all x1, waiting for transfers between devices, per_device(): lax.all_to_all(partial, 'freq', split_axis=0, concat_axis=0, tiled=True)  47.9 us
    all_gather x1, blocking collectives, per_device(): piece = lax.all_gather(received, 'freq', axis=0, tiled=True)  15.6 us
    dot_general x1, matrix products, per_device(): jnp.dot(spread_over(forward, virtual_sources), flat_traces, preferred_ele...  11.6 us
    all_to_all x1, starting transfers between devices, per_device(): lax.all_to_all(partial, 'freq', split_axis=0, concat_axis=0, tiled=True)  6.45 us
    dot_general x1, matrix products, per_device(): jnp.dot(spread_over(backward, virtual_sources), piece.reshape(count * 2 *...  5.99 us
    dot_general x1, matrix products, per_device(): jnp.einsum('iajrs,oivjs->oajrv', emitter_factors, stacked_spectrum, prefe...  5.68 us
    all_to_all x1, waiting for transfers between devices, per_device(): lax.all_to_all(coefficients, 'tile', split_axis=1, concat_axis=2, tiled=T...  4.6 us
    all_to_all x1, starting transfers between devices, per_device(): lax.all_to_all(coefficients, 'tile', split_axis=1, concat_axis=2, tiled=T...  3.41 us
  transfers between devices with their start and end apart: 2, of which 2 were waited for; matrix products, arithmetic and copies ran while one was open for 2% of the time, Pallas kernels for 0%

profile of v5, /device:TPU:0, one launch (start us, length us, event | category | flops | bytes accessed | tf_op | source)
XLA Modules:
  0.0 111.8 jit_solution(1231623408836468820)
XLA Ops:
  0.0 0.1 fusion.47
  0.1 0.1 cosine_convert_fusion
  0.3 0.7 fusion.5
  1.0 11.6 %fusion.55 = f32[4,2,16,4096]{3,2,1,0:T(8,128)} fusion(bf16[4,2,16,2560]{3,2,1,0:T(8,128)(2,1)S(1)} %bitcast.79, bf16[2560,4096,1,1]{1,0,3,2:T(8,128)(2,1)} %bitcast.75), kind=kOutput, calls=%fused_computation.85 | convolution fusion | flops 2684354560 | bytes 23724032 | tf_op jit(solution)/shard_map/dot_general | solution.py:55
  12.6 0.0 copy-start
  12.6 6.5 %all-to-all-start = ((f32[4,2,16,4096]{3,2,1,0:T(8,128)}), f32[4,2,16,4096]{3,2,1,0:T(8,128)S(1)}, u32[]{:S(2)}, u32[]{:S(2)}) async-start(f32[4,2,16,4096]{3,2,1,0:T(8,128)} %fusion.55), calls=%async_computation | async-start | bytes 4194304 | tf_op jit(solution)/shard_map/all_to_all | solution.py:58
  19.0 0.1 fusion.46
  19.2 0.1 cosine_convert_fusion.1
  19.4 0.0 copy-done
  19.4 47.9 %all-to-all-done = f32[4,2,16,4096]{3,2,1,0:T(8,128)S(1)} async-done(((f32[4,2,16,4096]{3,2,1,0:T(8,128)}), f32[4,2,16,4096]{3,2,1,0:T(8,128)S(1)}, u32[]{:S(2)}, u32[]{:S(2)}) %all-to-all-start) | async-done | bytes 2097184 | tf_op jit(solution)/shard_map/all_to_all | solution.py:58
  67.2 0.2 reduce_sum.9
  67.6 0.1 copy_negate_fusion
  67.7 5.7 %fusion.6 = bf16[2,32,16,8,16]{1,4,3,0,2:T(8,128)(2,1)S(1)} fusion(bf16[2,32,16,8,256,1]{4,3,2,1,0,5:T(8,128)(2,1)} %bitcast.85, pred[32,16,8]{0,2,1:T(8,128)(4,1)S(1)} %iota_compare_fusion.5, bf16[1,2,16,16,256]{4,2,1,0,3:T(8,128)(2,1)S(1)} %get-tuple-element.12, bf16[1,2,16,16,256]{4,2,1,0,3:T(8,128)(2,1)S(1)} %get-tuple-element.11), kind=kOutput, calls=%fused_computation.12 | convolution fusion | flops 135528448 | bytes 4984832 | tf_op jit(solution)/shard_map/iajrs,oivjs->oajrv/dot_general | solution.py:69
  73.4 1.2 %copy.62 = bf16[2,32,16,128]{3,2,0,1:T(8,128)(2,1)} copy(bf16[2,32,16,128]{1,3,0,2:T(8,128)(2,1)S(1)} %bitcast.77) | data formatting | bytes 524288 | tf_op jit(solution)/shard_map/reshape | solution.py:80
  74.6 3.4 %all-to-all-start.1 = ((bf16[2,32,16,128]{3,2,0,1:T(8,128)(2,1)}), bf16[2,32,16,128]{3,2,0,1:T(8,128)(2,1)S(1)}, u32[]{:S(2)}, u32[]{:S(2)}) async-start(bf16[2,32,16,128]{3,2,0,1:T(8,128)(2,1)} %copy.62), calls=%async_computation.1 | async-start | bytes 524288 | tf_op jit(solution)/shard_map/all_to_all | solution.py:81
  78.1 1.4 %convolution_convert_fusion = bf16[2560,8]{0,1:T(8,128)(2,1)S(1)} fusion(bf16[160,8]{0,1:T(8,128)(2,1)S(1)} %reshape.537, s32[2560]{0:T(1024)S(1)} %get-tuple-element.15), kind=kOutput, calls=%fused_computation.9 | convolution fusion | flops 6983680 | bytes 53760 | tf_op jit(solution)/shard_map/dot_general | solution.py:29
  79.5 4.6 %all-to-all-done.1 = bf16[2,32,16,128]{3,2,0,1:T(8,128)(2,1)S(1)} async-done(((bf16[2,32,16,128]{3,2,0,1:T(8,128)(2,1)}), bf16[2,32,16,128]{3,2,0,1:T(8,128)(2,1)S(1)}, u32[]{:S(2)}, u32[]{:S(2)}) %all-to-all-start.1) | async-done | bytes 262176 | tf_op jit(solution)/shard_map/all_to_all | solution.py:81
  84.1 0.7 copy.83
  84.8 0.5 reshape.550
  85.3 0.1 neg.43
  85.4 0.7 copy.82
  86.0 0.5 reshape.549
  86.5 0.2 maximum_bitcast_fusion.2
  86.8 3.2 %fusion.16 = bf16[2,16,8,256]{3,1,0,2:T(8,128)(2,1)S(1)} fusion(bf16[2,8,64,8,256,1]{4,3,2,1,0,5:T(8,128)(2,1)} %bitcast.86, bf16[1,2,8,64,8,16]{3,5,4,1,0,2:T(8,128)(2,1)S(1)} %get-tuple-element.6, bf16[1,2,8,64,8,16]{3,5,4,1,0,2:T(8,128)(2,1)S(1)} %get-tuple-element.5), kind=kOutput, calls=%fused_computation.17 | convolution fusion | flops 134545408 | bytes 4849664 | tf_op jit(solution)/shard_map/imdlh,oimdlu->oumh/dot_general | solution.py:92
  90.0 0.1 copy.71
  90.1 0.1 convert_element_type.137
  90.2 15.6 %all_gather.3 = bf16[4,2,16,2048]{3,2,1,0:T(8,128)(2,1)S(1)} all-gather(bf16[1,2,16,2048]{3,2,1,0:T(8,128)(2,1)S(1)} %convert_element_type.137), channel_id=1, replica_groups=mesh['groups'=2,'freq'=4,'tile'=4] {'freq'}, dimensions={0}, use_global_device_ids=true | all-gather | bytes 655360 | tf_op jit(solution)/shard_map/all_gather | solution.py:101
  105.8 6.0 %multiply_convert_fusion = bf16[2560,2048]{1,0:T(8,128)(2,1)} fusion(bf16[128,2048]{1,0:T(8,128)(2,1)S(1)} %bitcast.76, bf16[2560,8]{0,1:T(8,128)(2,1)S(1)} %convolution_convert_fusion, s32[128]{0:T(128)S(1)} %get-tuple-element.18, s32[2560]{0:T(1024)S(1)} %get-tuple-element.16, s32[128]{0:T(128)S(1)} %get-tuple-element.17), kind=kOutput, calls=%fused_computation | convolution fusion | flops 1358889984 | bytes 11062272 | tf_op jit(solution)/shard_map/dot_general | solution.py:105
  (19 shorter events, 0.3 us)
Async XLA Ops:
  12.6 6.8 %copy-start = (s32[1,32,16]{1,2,0:T(8,128)S(1)}, s32[1,32,16]{1,2,0:T(8,128)}, u32[]{:S(2)}) copy-start(s32[1,32,16]{1,2,0:T(8,128)} %param.7) | copy-start | bytes 6148
  12.6 54.7 %all-to-all-start = ((f32[4,2,16,4096]{3,2,1,0:T(8,128)}), f32[4,2,16,4096]{3,2,1,0:T(8,128)S(1)}, u32[]{:S(2)}, u32[]{:S(2)}) async-start(f32[4,2,16,4096]{3,2,1,0:T(8,128)} %fusion.55), calls=%async_computation | async-start | bytes 4194304 | tf_op jit(solution)/shard_map/all_to_all | solution.py:58
  74.6 9.4 %all-to-all-start.1 = ((bf16[2,32,16,128]{3,2,0,1:T(8,128)(2,1)}), bf16[2,32,16,128]{3,2,0,1:T(8,128)(2,1)S(1)}, u32[]{:S(2)}, u32[]{:S(2)}) async-start(bf16[2,32,16,128]{3,2,0,1:T(8,128)(2,1)} %copy.62), calls=%async_computation.1 | async-start | bytes 524288 | tf_op jit(solution)/shard_map/all_to_all | solution.py:81

commit v6 on v5

--- a/solution.py
+++ b/solution.py
@@ -56,18 +56,27 @@
         spread_over(forward, virtual_sources), flat_traces, preferred_element_type=jnp.float32
     ).reshape(freq_total, 2, virtual_sources, source_count)
     gathered = lax.all_to_all(partial, "freq", split_axis=0, concat_axis=0, tiled=True)
+    tile_count = lax.axis_size("tile")
+    rows_local = rows_all // tile_count
+    emitter_factors = jnp.transpose(v_factors[0], (2, 1, 3, 0, 4))
+    receiver_factors = jnp.transpose(
+        u_factors[0].reshape(2, rows_local, tile_count, columns, rank_positions, tile_width),
+        (1, 2, 0, 3, 4, 5),
+    )
+    gathered, emitter_factors, receiver_factors = lax.optimization_barrier(
+        (gathered, emitter_factors, receiver_factors)
+    )
     summed = gathered.reshape(
         lax.axis_size("freq"), freq_local, 2, virtual_sources, source_count
     ).sum(axis=0)
     spectrum = (summed * scale_time).astype(jnp.bfloat16)[0]
     spectral_tiles = spectrum.reshape(2, virtual_sources, columns, tile_width)
-    emitter_factors = v_factors[0]
     real_part, imag_part = spectral_tiles[0], spectral_tiles[1]
     stacked_spectrum = jnp.stack(
         [jnp.stack([real_part, -imag_part]), jnp.stack([imag_part, real_part])]
     )
     stacked = jnp.einsum(
-        "iajrs,oivjs->oajrv",
+        "jaris,oivjs->aojrv",
         emitter_factors,
         stacked_spectrum,
         preferred_element_type=jnp.float32,
@@ -76,21 +85,22 @@
         jnp.arange(rank_positions, dtype=jnp.int32)[None, None, :, None]
         < ranks[0][:, :, None, None]
     )
-    coefficients = jnp.where(rank_mask[None], stacked, jnp.float32(0.0)).astype(jnp.bfloat16)
-    coefficients = coefficients.reshape(2, rows_all, columns, rank_positions * virtual_sources)
-    arrived = lax.all_to_all(coefficients, "tile", split_axis=1, concat_axis=2, tiled=True)
-    rows_local = arrived.shape[1]
-    columns_all = arrived.shape[2]
-    arrived = arrived.reshape(2, rows_local, columns_all, rank_positions, virtual_sources)
-    receiver_factors = u_factors[0]
-    real_arrived, imag_arrived = arrived[0], arrived[1]
+    coefficients = jnp.where(rank_mask[:, None], stacked, jnp.float32(0.0)).astype(jnp.bfloat16)
+    coefficients = coefficients.reshape(
+        tile_count, rows_local, 2, columns, rank_positions * virtual_sources
+    )
+    arrived = lax.all_to_all(coefficients, "tile", split_axis=0, concat_axis=0, tiled=True)
+    arrived = arrived.reshape(
+        tile_count, rows_local, 2, columns, rank_positions, virtual_sources
+    )
+    real_arrived, imag_arrived = arrived[:, :, 0], arrived[:, :, 1]
     stacked_arrived = jnp.stack(
         [jnp.stack([real_arrived, -imag_arrived]), jnp.stack([imag_arrived, real_arrived])]
     )
     receivers = rows_local * tile_width
     received = (
         jnp.einsum(
-            "imdlh,oimdlu->oumh",
+            "apijrb,oipajrv->ovab",
             receiver_factors,
             stacked_arrived,
             preferred_element_type=jnp.float32,

time: 112 us -> 115 us (1.027)
  local copies, waits for them, and re-layouts: 3.94 us -> 14.1 us
  waiting for transfers between devices: 52.5 us -> 46.6 us
  matrix products: 28.6 us -> 26.3 us
    all_to_all x1, waiting for transfers between devices: 47.9 us -> 42.2 us  [per_device(): lax.all_to_all(partial, 'freq', split_axis=0, concat_axis=0, tiled=True)]
    another operation x0 -> x1, local copies, waits for them, and re-layouts: none -> 5.64 us  [per_device(): u_factors[0]]
    convert_element_type x2 -> x3, local copies, waits for them, and re-layouts: 0.14 us -> 3.63 us  [the longest x1 3.52 us: per_device(): jnp.where(rank_mask[:, None], stacked, jnp.float32(0.0))]
    dot_general x2, matrix products: 8.93 us -> 7.06 us  [the longest x1 5.65 us: per_device(): jnp.einsum('jaris,oivjs->aojrv', emitter_factors, stacked_spectrum, prefe...]
    unnamed x4 -> x6, local copies, waits for them, and re-layouts: 0.05 us -> 1.29 us
    slice x3 -> x0, local copies, waits for them, and re-layouts: 1.19 us -> none  [per_device(): real_arrived, imag_arrived = (arrived[0], arrived[1])]
  transfers between devices with their start and end apart: 2 -> 2, of which waited for: 2 -> 2; matrix products, arithmetic and copies ran while one was open for 2% -> 6% of each run, Pallas kernels for 0% -> 0%
where the time goes in v6:
time: 115 us
  waiting for transfers between devices  46.6 us (41%)
  matrix products  26.3 us (23%)
  blocking collectives  15.6 us (14%)
  local copies, waits for them, and re-layouts  14.1 us (12%)
  starting transfers between devices  9.9 us (9%)
  other arithmetic  1.94 us (2%)
    all_to_all x1, waiting for transfers between devices, per_device(): lax.all_to_all(partial, 'freq', split_axis=0, concat_axis=0, tiled=True)  42.2 us
    all_gather x1, blocking collectives, per_device(): piece = lax.all_gather(received, 'freq', axis=0, tiled=True)  15.6 us
    dot_general x1, matrix products, per_device(): jnp.dot(spread_over(forward, virtual_sources), flat_traces, preferred_ele...  11.2 us
    all_to_all x1, starting transfers between devices, per_device(): lax.all_to_all(partial, 'freq', split_axis=0, concat_axis=0, tiled=True)  6.32 us
    dot_general x1, matrix products, per_device(): jnp.dot(spread_over(backward, virtual_sources), piece.reshape(count * 2 *...  5.99 us
    dot_general x1, matrix products, per_device(): jnp.einsum('jaris,oivjs->aojrv', emitter_factors, stacked_spectrum, prefe...  5.65 us
    another operation x1, local copies, waits for them, and re-layouts, per_device(): u_factors[0]  5.64 us
    all_to_all x1, waiting for transfers between devices, per_device(): lax.all_to_all(coefficients, 'tile', split_axis=0, concat_axis=0, tiled=T...  4.42 us
  transfers between devices with their start and end apart: 2, of which 2 were waited for; matrix products, arithmetic and copies ran while one was open for 6% of the time, Pallas kernels for 0%

profile of v6, /device:TPU:0, one launch (start us, length us, event | category | flops | bytes accessed | tf_op | source)
XLA Modules:
  0.0 114.8 jit_solution(518281071137488428)
XLA Ops:
  0.0 0.1 fusion.37
  0.1 0.1 cosine_convert_fusion
  0.4 0.7 fusion.6
  1.0 11.2 %fusion.44 = f32[4,2,16,4096]{3,2,1,0:T(8,128)} fusion(bf16[4,2,16,2560]{3,2,1,0:T(8,128)(2,1)S(1)} %bitcast.89, bf16[2560,4096,1,1]{1,0,3,2:T(8,128)(2,1)} %bitcast.83), kind=kOutput, calls=%fused_computation.85 | convolution fusion | flops 2684354560 | bytes 23724032 | tf_op jit(solution)/shard_map/dot_general | solution.py:55
  12.2 6.3 %all-to-all-start = ((f32[4,2,16,4096]{3,2,1,0:T(8,128)}), f32[4,2,16,4096]{3,2,1,0:T(8,128)S(1)}, u32[]{:S(2)}, u32[]{:S(2)}) async-start(f32[4,2,16,4096]{3,2,1,0:T(8,128)} %fusion.44), calls=%async_computation | async-start | bytes 4194304 | tf_op jit(solution)/shard_map/all_to_all | solution.py:58
  18.5 0.0 copy-start.1
  18.5 5.6 %copy.76 = bf16[2,8,4,16,8,256]{5,3,4,2,1,0:T(8,128)(2,1)} copy(bf16[2,8,4,16,8,256]{5,4,3,2,1,0:T(8,128)(2,1)} %bitcast.86) | data formatting | bytes 8388608 | tf_op jit(solution)/shard_map/reshape;squeeze | solution.py:63
  24.2 0.1 fusion.36
  24.3 0.1 cosine_convert_fusion.1
  24.5 0.0 copy-done.1
  24.5 42.2 %all-to-all-done = f32[4,2,16,4096]{3,2,1,0:T(8,128)S(1)} async-done(((f32[4,2,16,4096]{3,2,1,0:T(8,128)}), f32[4,2,16,4096]{3,2,1,0:T(8,128)S(1)}, u32[]{:S(2)}, u32[]{:S(2)}) %all-to-all-start) | async-done | bytes 2097184 | tf_op jit(solution)/shard_map/all_to_all | solution.py:58
  66.7 0.1 reduce_sum.9
  67.0 0.1 copy_negate_fusion
  67.2 5.7 %fusion.7 = bf16[32,2,16,8,16]{0,4,3,1,2:T(8,128)(2,1)S(1)} fusion(bf16[16,32,8,2,256,1]{4,2,0,1,3,5:T(8,128)(2,1)} %bitcast.96, pred[32,16,8]{0,2,1:T(8,128)(4,1)S(1)} %iota_compare_fusion.5, bf16[1,2,16,16,256]{4,2,1,0,3:T(8,128)(2,1)S(1)} %get-tuple-element.18, bf16[1,2,16,16,256]{4,2,1,0,3:T(8,128)(2,1)S(1)} %get-tuple-element.17), kind=kOutput, calls=%fused_computation.17 | convolution fusion | flops 135528448 | bytes 4984832 | tf_op jit(solution)/shard_map/jaris,oivjs->aojrv/dot_general | solution.py:78
  72.8 3.5 %copy.49 = bf16[32,2,16,8,16]{4,3,2,1,0:T(8,128)(2,1)S(1)} copy(bf16[32,2,16,8,16]{0,4,3,1,2:T(8,128)(2,1)S(1)} %fusion.7) | data formatting | bytes 524288 | tf_op jit(solution)/shard_map/convert_element_type | solution.py:88
  76.4 2.1 %reshape.538 = bf16[4,8,2,16,128]{4,3,2,1,0:T(8,128)(2,1)} reshape(bf16[32,2,16,8,16]{4,3,2,1,0:T(8,128)(2,1)S(1)} %copy.49) | data formatting | bytes 524288 | tf_op jit(solution)/shard_map/reshape | solution.py:89
  78.4 3.6 %all-to-all-start.1 = ((bf16[4,8,2,16,128]{4,3,2,1,0:T(8,128)(2,1)}), bf16[4,8,2,16,128]{4,3,2,1,0:T(8,128)(2,1)S(1)}, u32[]{:S(2)}, u32[]{:S(2)}) async-start(bf16[4,8,2,16,128]{4,3,2,1,0:T(8,128)(2,1)} %reshape.538), calls=%async_computation.1 | async-start | bytes 524288 | tf_op jit(solution)/shard_map/all_to_all | solution.py:92
  82.0 1.4 %convolution_convert_fusion = bf16[2560,8]{0,1:T(8,128)(2,1)S(1)} fusion(bf16[160,8]{0,1:T(8,128)(2,1)S(1)} %reshape.535, s32[2560]{0:T(1024)S(1)} %get-tuple-element.21), kind=kOutput, calls=%fused_computation.12 | convolution fusion | flops 6983680 | bytes 53760 | tf_op jit(solution)/shard_map/dot_general | solution.py:29
  83.4 4.4 %all-to-all-done.1 = bf16[4,8,2,16,128]{4,3,2,1,0:T(8,128)(2,1)S(1)} async-done(((bf16[4,8,2,16,128]{4,3,2,1,0:T(8,128)(2,1)}), bf16[4,8,2,16,128]{4,3,2,1,0:T(8,128)(2,1)S(1)}, u32[]{:S(2)}, u32[]{:S(2)}) %all-to-all-start.1) | async-done | bytes 262176 | tf_op jit(solution)/shard_map/all_to_all | solution.py:92
  87.9 1.0 copy.50
  88.9 0.1 fusion.42
  89.0 0.4 slice_bitcast_fusion
  89.4 0.0 copy-start
  89.4 0.9 maximum_bitcast_fusion
  90.4 1.2 %copy-done = bf16[2,8,4,16,8,256]{5,3,4,2,1,0:T(8,128)(2,1)S(1)} copy-done((bf16[2,8,4,16,8,256]{5,3,4,2,1,0:T(8,128)(2,1)S(1)}, bf16[2,8,4,16,8,256]{5,3,4,2,1,0:T(8,128)(2,1)}, u32[]{:S(2)}) %copy-start) | copy-done | bytes 4194328
  91.6 1.4 %fusion = bf16[8,2,16,256,1,1,1]{3,2,6,5,1,0,4:T(8,128)(2,1)S(1)} fusion(bf16[8,4,2,16,8,256]{5,3,4,1,0,2:T(8,128)(2,1)S(1)} %bitcast.87, bf16[1,2,4,8,16,8,16]{4,6,5,2,3,0,1:T(8,128)(2,1)S(1)} %get-tuple-element.14, bf16[1,2,4,8,16,8,16]{4,6,5,2,3,0,1:T(8,128)(2,1)S(1)} %get-tuple-element.13), kind=kOutput, calls=%fused_computation.2 | convolution fusion | flops 134479872 | bytes 4849664 | tf_op jit(solution)/shard_map/apijrb,oipajrv->ovab/dot_general | solution.py:102
  93.1 0.1 convert_element_type.137
  93.1 15.6 %all_gather.3 = bf16[4,2,16,2048]{3,2,1,0:T(8,128)(2,1)S(1)} all-gather(bf16[1,2,16,2048]{3,2,1,0:T(8,128)(2,1)S(1)} %convert_element_type.137), channel_id=1, replica_groups=mesh['groups'=2,'freq'=4,'tile'=4] {'freq'}, dimensions={0}, use_global_device_ids=true | all-gather | bytes 655360 | tf_op jit(solution)/shard_map/all_gather | solution.py:111
  108.8 6.0 %multiply_convert_fusion = bf16[2560,2048]{1,0:T(8,128)(2,1)} fusion(bf16[128,2048]{1,0:T(8,128)(2,1)S(1)} %bitcast.88, bf16[2560,8]{0,1:T(8,128)(2,1)S(1)} %convolution_convert_fusion, s32[128]{0:T(128)S(1)} %get-tuple-element.24, s32[2560]{0:T(1024)S(1)} %get-tuple-element.22, s32[128]{0:T(128)S(1)} %get-tuple-element.23), kind=kOutput, calls=%fused_computation | convolution fusion | flops 1358889984 | bytes 11062272 | tf_op jit(solution)/shard_map/dot_general | solution.py:115
  (19 shorter events, 0.4 us)
Async XLA Ops:
  12.2 54.5 %all-to-all-start = ((f32[4,2,16,4096]{3,2,1,0:T(8,128)}), f32[4,2,16,4096]{3,2,1,0:T(8,128)S(1)}, u32[]{:S(2)}, u32[]{:S(2)}) async-start(f32[4,2,16,4096]{3,2,1,0:T(8,128)} %fusion.44), calls=%async_computation | async-start | bytes 4194304 | tf_op jit(solution)/shard_map/all_to_all | solution.py:58
  18.5 6.0 %copy-start.1 = (s32[1,32,16]{1,2,0:T(8,128)S(1)}, s32[1,32,16]{1,2,0:T(8,128)}, u32[]{:S(2)}) copy-start(s32[1,32,16]{1,2,0:T(8,128)} %param.7) | copy-start | bytes 6148
  78.4 9.4 %all-to-all-start.1 = ((bf16[4,8,2,16,128]{4,3,2,1,0:T(8,128)(2,1)}), bf16[4,8,2,16,128]{4,3,2,1,0:T(8,128)(2,1)S(1)}, u32[]{:S(2)}, u32[]{:S(2)}) async-start(bf16[4,8,2,16,128]{4,3,2,1,0:T(8,128)(2,1)} %reshape.538), calls=%async_computation.1 | async-start | bytes 524288 | tf_op jit(solution)/shard_map/all_to_all | solution.py:92
  89.4 2.2 %copy-start = (bf16[2,8,4,16,8,256]{5,3,4,2,1,0:T(8,128)(2,1)S(1)}, bf16[2,8,4,16,8,256]{5,3,4,2,1,0:T(8,128)(2,1)}, u32[]{:S(2)}) copy-start(bf16[2,8,4,16,8,256]{5,3,4,2,1,0:T(8,128)(2,1)} %copy.76) | copy-start | bytes 12582916

commit v7 on v5

--- a/solution.py
+++ b/solution.py
@@ -1,8 +1,11 @@
 import math
+
+import functools
 
 import jax
 import jax.numpy as jnp
 from jax import lax
+from jax.experimental import pallas as pl
 from jax.sharding import PartitionSpec as P
 
 NT = 640
@@ -35,6 +38,39 @@
     return jnp.where(same, wide, jnp.float32(0.0)).astype(kind)
 
 
+def source_kernel(v_ref, x_ref, o_ref, *, group, tile_width, lhs_rows):
+    for column in range(group):
+        real_f = v_ref[0, :, column].astype(jnp.float32).reshape(lhs_rows, tile_width)
+        imag_f = v_ref[1, :, column].astype(jnp.float32).reshape(lhs_rows, tile_width)
+        lanes = slice(column * tile_width, (column + 1) * tile_width)
+        real_x = x_ref[0, :, lanes].astype(jnp.float32)
+        imag_x = x_ref[1, :, lanes].astype(jnp.float32)
+        lhs = jnp.concatenate([real_f, imag_f], axis=1).astype(jnp.bfloat16)
+        rhs = jnp.concatenate(
+            [jnp.concatenate([real_x, -imag_x], axis=1), jnp.concatenate([imag_x, real_x], axis=1)],
+            axis=0,
+        ).astype(jnp.bfloat16)
+        o_ref[column] = lax.dot_general(
+            lhs, rhs, (((1,), (1,)), ((), ())), preferred_element_type=jnp.float32
+        )
+
+def source_side(factors, spectrum, interpret=False):
+    _, rows, columns, ranks, tile_width = factors.shape
+    virtual = spectrum.shape[1]
+    group = 4 if columns % 4 == 0 else 1
+    return pl.pallas_call(
+        functools.partial(source_kernel, group=group, tile_width=tile_width, lhs_rows=rows * ranks),
+        grid=(columns // group,),
+        in_specs=[
+            pl.BlockSpec((2, rows, group, ranks, tile_width), lambda g: (0, 0, g, 0, 0)),
+            pl.BlockSpec((2, virtual, group * tile_width), lambda g: (0, 0, g)),
+        ],
+        out_specs=pl.BlockSpec((group, rows * ranks, 2 * virtual), lambda g: (g, 0, 0)),
+        out_shape=jax.ShapeDtypeStruct((columns, rows * ranks, 2 * virtual), jnp.float32),
+        interpret=interpret,
+    )(factors, spectrum)
+
+
 def per_device(traces, v_factors, u_factors, ranks):
     time_count = traces.shape[0]
     virtual_sources = traces.shape[1]
@@ -60,23 +96,18 @@
         lax.axis_size("freq"), freq_local, 2, virtual_sources, source_count
     ).sum(axis=0)
     spectrum = (summed * scale_time).astype(jnp.bfloat16)[0]
-    spectral_tiles = spectrum.reshape(2, virtual_sources, columns, tile_width)
-    emitter_factors = v_factors[0]
-    real_part, imag_part = spectral_tiles[0], spectral_tiles[1]
-    stacked_spectrum = jnp.stack(
-        [jnp.stack([real_part, -imag_part]), jnp.stack([imag_part, real_part])]
-    )
-    stacked = jnp.einsum(
-        "iajrs,oivjs->oajrv",
-        emitter_factors,
-        stacked_spectrum,
-        preferred_element_type=jnp.float32,
+    raw = source_side(v_factors[0], spectrum).reshape(
+        columns, rows_all, rank_positions, 2, virtual_sources
     )
     rank_mask = (
-        jnp.arange(rank_positions, dtype=jnp.int32)[None, None, :, None]
-        < ranks[0][:, :, None, None]
+        jnp.arange(rank_positions, dtype=jnp.int32)[None, None, :]
+        < jnp.transpose(ranks[0])[:, :, None]
     )
-    coefficients = jnp.where(rank_mask[None], stacked, jnp.float32(0.0)).astype(jnp.bfloat16)
+    coefficients = (
+        jnp.where(rank_mask[:, :, :, None, None], raw, jnp.float32(0.0))
+        .astype(jnp.bfloat16)
+        .transpose(3, 1, 0, 2, 4)
+    )
     coefficients = coefficients.reshape(2, rows_all, columns, rank_positions * virtual_sources)
     arrived = lax.all_to_all(coefficients, "tile", split_axis=1, concat_axis=2, tiled=True)
     rows_local = arrived.shape[1]

time: 112 us -> 128 us (1.14)
  local copies, waits for them, and re-layouts: 3.94 us -> 12.9 us
  other arithmetic: 1.14 us -> 8.27 us
  matrix products: 28.6 us -> 22.9 us
  Pallas kernels: 0 us -> 4.96 us
    transpose x0 -> x1, other arithmetic: none -> 6.4 us  [per_device(): coefficients = jnp.where(rank_mask[:, :, :, None, None], raw, jnp.float32...]
    dot_general x1 -> x0, matrix products: 5.68 us -> none  [per_device(): jnp.einsum('iajrs,oivjs->oajrv', emitter_factors, stacked_spectrum, prefe...]
    transpose x0 -> x1, local copies, waits for them, and re-layouts: none -> 5.09 us  [per_device(): coefficients = jnp.where(rank_mask[:, :, :, None, None], raw, jnp.float32...]
    pallas_call x0 -> x1, Pallas kernels: none -> 4.96 us  [source_side(): pl.pallas_call(functools.partial(source_kernel, group=group, tile_width=t...]
    reshape x0 -> x1, local copies, waits for them, and re-layouts: none -> 4.02 us  [per_device(): source_side(v_factors[0], spectrum)]
  transfers between devices with their start and end apart: 2 -> 2, of which waited for: 2 -> 2; matrix products, arithmetic and copies ran while one was open for 2% -> 1% of each run, Pallas kernels for 0% -> 0%
where the time goes in v7:
time: 128 us; the launch traced here: 127 us
  waiting for transfers between devices  52.3 us (41%)
  matrix products  22.9 us (18%)
  blocking collectives  15.6 us (12%)
  local copies, waits for them, and re-layouts  12.9 us (10%)
  starting transfers between devices  9.86 us (8%)
  other arithmetic  8.27 us (6%)
  Pallas kernels  4.96 us (4%)
    all_to_all x1, waiting for transfers between devices, per_device(): lax.all_to_all(partial, 'freq', split_axis=0, concat_axis=0, tiled=True)  47.7 us
    all_gather x1, blocking collectives, per_device(): piece = lax.all_gather(received, 'freq', axis=0, tiled=True)  15.6 us
    dot_general x1, matrix products, per_device(): jnp.dot(spread_over(forward, virtual_sources), flat_traces, preferred_ele...  11.6 us
    all_to_all x1, starting transfers between devices, per_device(): lax.all_to_all(partial, 'freq', split_axis=0, concat_axis=0, tiled=True)  6.45 us
    transpose x1, other arithmetic, per_device(): coefficients = jnp.where(rank_mask[:, :, :, None, None], raw, jnp.float32...  6.4 us
    dot_general x1, matrix products, per_device(): jnp.dot(spread_over(backward, virtual_sources), piece.reshape(count * 2 *...  5.99 us
    transpose x1, local copies, waits for them, and re-layouts, per_device(): coefficients = jnp.where(rank_mask[:, :, :, None, None], raw, jnp.float32...  5.09 us
    pallas_call x1, Pallas kernels, source_side(): pl.pallas_call(functools.partial(source_kernel, group=group, tile_width=t...  4.96 us
  transfers between devices with their start and end apart: 2, of which 2 were waited for; matrix products, arithmetic and copies ran while one was open for 1% of the time, Pallas kernels for 0%

profile of v7, /device:TPU:0, one launch (start us, length us, event | category | flops | bytes accessed | tf_op | source)
XLA Modules:
  0.0 127.0 jit_solution(13974309075410926423)
XLA Ops:
  0.0 0.1 fusion.40
  0.1 0.1 cosine_convert_fusion
  0.3 0.7 fusion.3
  1.0 11.6 %fusion.46 = f32[4,2,16,4096]{3,2,1,0:T(8,128)} fusion(bf16[4,2,16,2560]{3,2,1,0:T(8,128)(2,1)S(1)} %bitcast.54, bf16[2560,4096,1,1]{1,0,3,2:T(8,128)(2,1)} %bitcast.49), kind=kOutput, calls=%fused_computation.74 | convolution fusion | flops 2684354560 | bytes 23724032 | tf_op jit(solution)/shard_map/dot_general | solution.py:91
  12.6 0.0 copy-start
  12.6 6.5 %all-to-all-start = ((f32[4,2,16,4096]{3,2,1,0:T(8,128)}), f32[4,2,16,4096]{3,2,1,0:T(8,128)S(1)}, u32[]{:S(2)}, u32[]{:S(2)}) async-start(f32[4,2,16,4096]{3,2,1,0:T(8,128)} %fusion.46), calls=%async_computation | async-start | bytes 4194304 | tf_op jit(solution)/shard_map/all_to_all | solution.py:94
  19.0 0.1 fusion.39
  19.2 0.1 cosine_convert_fusion.1
  19.4 0.0 copy-done
  19.4 0.1 iota_compare_fusion.4
  19.5 47.7 %all-to-all-done = f32[4,2,16,4096]{3,2,1,0:T(8,128)S(1)} async-done(((f32[4,2,16,4096]{3,2,1,0:T(8,128)}), f32[4,2,16,4096]{3,2,1,0:T(8,128)S(1)}, u32[]{:S(2)}, u32[]{:S(2)}) %all-to-all-start) | async-done | bytes 2097184 | tf_op jit(solution)/shard_map/all_to_all | solution.py:94
  67.2 0.2 reduce_sum.9
  67.4 0.7 multiply_convert_fusion.1.x_ref
  68.2 5.0 %shard_map.46 = f32[16,256,32]{2,1,0:T(8,128)} custom-call(bf16[2,32,16,8,256]{4,3,2,1,0:T(8,128)(2,1)} %bitcast.51, bf16[2,16,4096]{2,1,0:T(8,128)(2,1)} %multiply_convert_fusion.1.x_ref), custom_call_target="tpu_custom_call" | custom-call | tf_op jit(solution)/shard_map/pallas_call | solution.py:61
  73.1 4.0 %reshape.517 = bf16[16,32,8,2,16]{4,3,2,1,0:T(2,128)(2,1)S(1)} reshape(f32[16,256,32]{2,1,0:T(8,128)} %shard_map.46) | data formatting | bytes 786432 | tf_op jit(solution)/shard_map/reshape | solution.py:99
  77.1 6.4 %fusion.4 = bf16[2,32,16,8,16]{4,0,3,1,2:T(2,128)(2,1)} fusion(bf16[16,32,8,2,16]{4,3,2,1,0:T(2,128)(2,1)S(1)} %reshape.517, pred[16,32,8]{2,1,0:T(8,128)(4,1)S(1)} %iota_compare_fusion.4), kind=kLoop, calls=%fused_computation.10 | loop fusion | flops 131072 | bytes 528384 | tf_op jit(solution)/shard_map/transpose | solution.py:109
  83.5 5.1 %copy.42 = bf16[2,32,16,8,16]{1,4,3,2,0:T(8,128)(2,1)S(1)} copy(bf16[2,32,16,8,16]{4,0,3,1,2:T(2,128)(2,1)} %fusion.4) | data formatting | bytes 524288 | tf_op jit(solution)/shard_map/transpose | solution.py:109
  88.6 1.2 copy.43
  89.9 3.4 %all-to-all-start.1 = ((bf16[2,32,16,128]{3,2,0,1:T(8,128)(2,1)}), bf16[2,32,16,128]{3,2,0,1:T(8,128)(2,1)S(1)}, u32[]{:S(2)}, u32[]{:S(2)}) async-start(bf16[2,32,16,128]{3,2,0,1:T(8,128)(2,1)} %copy.43), calls=%async_computation.1 | async-start | bytes 524288 | tf_op jit(solution)/shard_map/all_to_all | solution.py:112
  93.3 1.4 %convolution_convert_fusion = bf16[2560,8]{0,1:T(8,128)(2,1)S(1)} fusion(bf16[160,8]{0,1:T(8,128)(2,1)S(1)} %reshape.514, s32[2560]{0:T(1024)S(1)} %get-tuple-element.9), kind=kOutput, calls=%fused_computation.8 | convolution fusion | flops 6983680 | bytes 53760 | tf_op jit(solution)/shard_map/dot_general | solution.py:32
  94.7 4.6 %all-to-all-done.1 = bf16[2,32,16,128]{3,2,0,1:T(8,128)(2,1)S(1)} async-done(((bf16[2,32,16,128]{3,2,0,1:T(8,128)(2,1)}), bf16[2,32,16,128]{3,2,0,1:T(8,128)(2,1)S(1)}, u32[]{:S(2)}, u32[]{:S(2)}) %all-to-all-start.1) | async-done | bytes 262176 | tf_op jit(solution)/shard_map/all_to_all | solution.py:112
  99.3 0.6 copy.59
  100.0 0.5 reshape.525
  100.5 0.1 neg.32
  100.6 0.6 copy.58
  101.2 0.5 reshape.524
  101.8 0.2 maximum_bitcast_fusion
  102.0 3.2 %fusion.12 = bf16[2,16,8,256]{3,1,0,2:T(8,128)(2,1)S(1)} fusion(bf16[2,8,64,8,256,1]{4,3,2,1,0,5:T(8,128)(2,1)} %bitcast.56, bf16[1,2,8,64,8,16]{3,5,4,1,0,2:T(8,128)(2,1)S(1)} %get-tuple-element.6, bf16[1,2,8,64,8,16]{3,5,4,1,0,2:T(8,128)(2,1)S(1)} %get-tuple-element.5), kind=kOutput, calls=%fused_computation.15 | convolution fusion | flops 134545408 | bytes 4849664 | tf_op jit(solution)/shard_map/imdlh,oimdlu->oumh/dot_general | solution.py:123
  105.3 0.1 copy.52
  105.3 0.1 convert_element_type.128
  105.4 15.6 %all_gather.3 = bf16[4,2,16,2048]{3,2,1,0:T(8,128)(2,1)S(1)} all-gather(bf16[1,2,16,2048]{3,2,1,0:T(8,128)(2,1)S(1)} %convert_element_type.128), channel_id=1, replica_groups=mesh['groups'=2,'freq'=4,'tile'=4] {'freq'}, dimensions={0}, use_global_device_ids=true | all-gather | bytes 655360 | tf_op jit(solution)/shard_map/all_gather | solution.py:132
  121.0 6.0 %multiply_convert_fusion = bf16[2560,2048]{1,0:T(8,128)(2,1)} fusion(bf16[128,2048]{1,0:T(8,128)(2,1)S(1)} %bitcast.52, bf16[2560,8]{0,1:T(8,128)(2,1)S(1)} %convolution_convert_fusion, s32[128]{0:T(128)S(1)} %get-tuple-element.12, s32[2560]{0:T(1024)S(1)} %get-tuple-element.10, s32[128]{0:T(128)S(1)} %get-tuple-element.11), kind=kOutput, calls=%fused_computation | convolution fusion | flops 1358889984 | bytes 11062272 | tf_op jit(solution)/shard_map/dot_general | solution.py:136
  (12 shorter events, 0.1 us)
Async XLA Ops:
  12.6 6.8 %copy-start = (s32[1,32,16]{1,2,0:T(8,128)S(1)}, s32[1,32,16]{1,2,0:T(8,128)}, u32[]{:S(2)}) copy-start(s32[1,32,16]{1,2,0:T(8,128)} %param.7) | copy-start | bytes 6148
  12.6 54.7 %all-to-all-start = ((f32[4,2,16,4096]{3,2,1,0:T(8,128)}), f32[4,2,16,4096]{3,2,1,0:T(8,128)S(1)}, u32[]{:S(2)}, u32[]{:S(2)}) async-start(f32[4,2,16,4096]{3,2,1,0:T(8,128)} %fusion.46), calls=%async_computation | async-start | bytes 4194304 | tf_op jit(solution)/shard_map/all_to_all | solution.py:94
  89.9 9.4 %all-to-all-start.1 = ((bf16[2,32,16,128]{3,2,0,1:T(8,128)(2,1)}), bf16[2,32,16,128]{3,2,0,1:T(8,128)(2,1)S(1)}, u32[]{:S(2)}, u32[]{:S(2)}) async-start(bf16[2,32,16,128]{3,2,0,1:T(8,128)(2,1)} %copy.43), calls=%async_computation.1 | async-start | bytes 524288 | tf_op jit(solution)/shard_map/all_to_all | solution.py:112

commit v8 on v5

--- a/solution.py
+++ b/solution.py
@@ -98,8 +98,8 @@
         .reshape(1, 2, virtual_sources, receivers)
         .astype(jnp.bfloat16)
     )
-    piece = lax.all_gather(received, "freq", axis=0, tiled=True)
-    count = piece.shape[0]
+    count = freq_total
+    piece = lax.all_gather(received.reshape(-1), "freq", axis=0, tiled=True)
 
     backward = jnp.stack([cosine.T, -sine.T], 2).reshape(time_count, count * 2)
     added = jnp.dot(

time: 112 us -> 113 us (level)
  no operation moved by 1% of the time
where the time goes in v8:
time: 113 us; the launch traced here: 112 us
  waiting for transfers between devices  52.5 us (46%)
  matrix products  28.6 us (25%)
  blocking collectives  15.6 us (14%)
  starting transfers between devices  9.86 us (9%)
  local copies, waits for them, and re-layouts  4.2 us (4%)
  other arithmetic  1.14 us (1%)
    all_to_all x1, waiting for transfers between devices, per_device(): lax.all_to_all(partial, 'freq', split_axis=0, concat_axis=0, tiled=True)  47.9 us
    all_gather x1, blocking collectives, per_device(): piece = lax.all_gather(received.reshape(-1), 'freq', axis=0, tiled=True)  15.6 us
    dot_general x1, matrix products, per_device(): jnp.dot(spread_over(forward, virtual_sources), flat_traces, preferred_ele...  11.6 us
    all_to_all x1, starting transfers between devices, per_device(): lax.all_to_all(partial, 'freq', split_axis=0, concat_axis=0, tiled=True)  6.45 us
    dot_general x1, matrix products, per_device(): jnp.dot(spread_over(backward, virtual_sources), piece.reshape(count * 2 *...  6.02 us
    dot_general x1, matrix products, per_device(): jnp.einsum('iajrs,oivjs->oajrv', emitter_factors, stacked_spectrum, prefe...  5.68 us
    all_to_all x1, waiting for transfers between devices, per_device(): lax.all_to_all(coefficients, 'tile', split_axis=1, concat_axis=2, tiled=T...  4.6 us
    all_to_all x1, starting transfers between devices, per_device(): lax.all_to_all(coefficients, 'tile', split_axis=1, concat_axis=2, tiled=T...  3.41 us
  transfers between devices with their start and end apart: 2, of which 2 were waited for; matrix products, arithmetic and copies ran while one was open for 2% of the time, Pallas kernels for 0%

profile of v8, /device:TPU:0, one launch (start us, length us, event | category | flops | bytes accessed | tf_op | source)
XLA Modules:
  0.0 112.1 jit_solution(15181462430112609816)
XLA Ops:
  0.0 0.1 fusion.47
  0.1 0.1 cosine_convert_fusion
  0.3 0.7 fusion.5
  1.0 11.6 %fusion.55 = f32[4,2,16,4096]{3,2,1,0:T(8,128)} fusion(bf16[4,2,16,2560]{3,2,1,0:T(8,128)(2,1)S(1)} %bitcast.77, bf16[2560,4096,1,1]{1,0,3,2:T(8,128)(2,1)} %bitcast.74), kind=kOutput, calls=%fused_computation.85 | convolution fusion | flops 2684354560 | bytes 23724032 | tf_op jit(solution)/shard_map/dot_general | solution.py:55
  12.6 0.0 copy-start
  12.6 6.5 %all-to-all-start = ((f32[4,2,16,4096]{3,2,1,0:T(8,128)}), f32[4,2,16,4096]{3,2,1,0:T(8,128)S(1)}, u32[]{:S(2)}, u32[]{:S(2)}) async-start(f32[4,2,16,4096]{3,2,1,0:T(8,128)} %fusion.55), calls=%async_computation | async-start | bytes 4194304 | tf_op jit(solution)/shard_map/all_to_all | solution.py:58
  19.0 0.1 fusion.46
  19.2 0.1 cosine_convert_fusion.1
  19.4 0.0 copy-done
  19.4 47.9 %all-to-all-done = f32[4,2,16,4096]{3,2,1,0:T(8,128)S(1)} async-done(((f32[4,2,16,4096]{3,2,1,0:T(8,128)}), f32[4,2,16,4096]{3,2,1,0:T(8,128)S(1)}, u32[]{:S(2)}, u32[]{:S(2)}) %all-to-all-start) | async-done | bytes 2097184 | tf_op jit(solution)/shard_map/all_to_all | solution.py:58
  67.2 0.2 reduce_sum.9
  67.6 0.1 copy_negate_fusion
  67.7 5.7 %fusion.6 = bf16[2,32,16,8,16]{1,4,3,0,2:T(8,128)(2,1)S(1)} fusion(bf16[2,32,16,8,256,1]{4,3,2,1,0,5:T(8,128)(2,1)} %bitcast.85, pred[32,16,8]{0,2,1:T(8,128)(4,1)S(1)} %iota_compare_fusion.5, bf16[1,2,16,16,256]{4,2,1,0,3:T(8,128)(2,1)S(1)} %get-tuple-element.12, bf16[1,2,16,16,256]{4,2,1,0,3:T(8,128)(2,1)S(1)} %get-tuple-element.11), kind=kOutput, calls=%fused_computation.12 | convolution fusion | flops 135528448 | bytes 4984832 | tf_op jit(solution)/shard_map/iajrs,oivjs->oajrv/dot_general | solution.py:69
  73.4 1.2 %copy.62 = bf16[2,32,16,128]{3,2,0,1:T(8,128)(2,1)} copy(bf16[2,32,16,128]{1,3,0,2:T(8,128)(2,1)S(1)} %bitcast.75) | data formatting | bytes 524288 | tf_op jit(solution)/shard_map/reshape | solution.py:80
  74.6 3.4 %all-to-all-start.1 = ((bf16[2,32,16,128]{3,2,0,1:T(8,128)(2,1)}), bf16[2,32,16,128]{3,2,0,1:T(8,128)(2,1)S(1)}, u32[]{:S(2)}, u32[]{:S(2)}) async-start(bf16[2,32,16,128]{3,2,0,1:T(8,128)(2,1)} %copy.62), calls=%async_computation.1 | async-start | bytes 524288 | tf_op jit(solution)/shard_map/all_to_all | solution.py:81
  78.1 1.4 %convolution_convert_fusion = bf16[2560,8]{0,1:T(8,128)(2,1)S(1)} fusion(bf16[160,8]{0,1:T(8,128)(2,1)S(1)} %reshape.530, s32[2560]{0:T(1024)S(1)} %get-tuple-element.15), kind=kOutput, calls=%fused_computation.9 | convolution fusion | flops 6983680 | bytes 53760 | tf_op jit(solution)/shard_map/dot_general | solution.py:29
  79.5 4.6 %all-to-all-done.1 = bf16[2,32,16,128]{3,2,0,1:T(8,128)(2,1)S(1)} async-done(((bf16[2,32,16,128]{3,2,0,1:T(8,128)(2,1)}), bf16[2,32,16,128]{3,2,0,1:T(8,128)(2,1)S(1)}, u32[]{:S(2)}, u32[]{:S(2)}) %all-to-all-start.1) | async-done | bytes 262176 | tf_op jit(solution)/shard_map/all_to_all | solution.py:81
  84.1 0.7 copy.83
  84.8 0.5 reshape.543
  85.3 0.1 neg.43
  85.4 0.7 copy.82
  86.0 0.5 reshape.542
  86.5 0.2 maximum_bitcast_fusion.2
  86.8 3.2 %fusion.16 = bf16[2,16,8,256]{3,1,0,2:T(8,128)(2,1)S(1)} fusion(bf16[2,8,64,8,256,1]{4,3,2,1,0,5:T(8,128)(2,1)} %bitcast.86, bf16[1,2,8,64,8,16]{3,5,4,1,0,2:T(8,128)(2,1)S(1)} %get-tuple-element.6, bf16[1,2,8,64,8,16]{3,5,4,1,0,2:T(8,128)(2,1)S(1)} %get-tuple-element.5), kind=kOutput, calls=%fused_computation.17 | convolution fusion | flops 134545408 | bytes 4849664 | tf_op jit(solution)/shard_map/imdlh,oimdlu->oumh/dot_general | solution.py:92
  90.0 0.1 copy.71
  90.1 0.1 copy.88
  90.2 15.6 %all_gather.3 = bf16[262144]{0:T(1024)(128)(2,1)S(1)} all-gather(bf16[65536]{0:T(1024)(128)(2,1)S(1)} %bitcast.79), channel_id=1, replica_groups=mesh['groups'=2,'freq'=4,'tile'=4] {'freq'}, dimensions={0}, use_global_device_ids=true | all-gather | bytes 655360 | tf_op jit(solution)/shard_map/all_gather | solution.py:102
  105.8 0.2 reshape.534
  106.1 6.0 %multiply_convert_fusion = bf16[2560,2048]{1,0:T(8,128)(2,1)} fusion(bf16[128,2048]{1,0:T(8,128)(2,1)S(1)} %reshape.534, bf16[2560,8]{0,1:T(8,128)(2,1)S(1)} %convolution_convert_fusion, s32[128]{0:T(128)S(1)} %get-tuple-element.18, s32[2560]{0:T(1024)S(1)} %get-tuple-element.16, s32[128]{0:T(128)S(1)} %get-tuple-element.17), kind=kOutput, calls=%fused_computation | convolution fusion | flops 1358889984 | bytes 11062272 | tf_op jit(solution)/shard_map/dot_general | solution.py:105
  (19 shorter events, 0.3 us)
Async XLA Ops:
  12.6 6.8 %copy-start = (s32[1,32,16]{1,2,0:T(8,128)S(1)}, s32[1,32,16]{1,2,0:T(8,128)}, u32[]{:S(2)}) copy-start(s32[1,32,16]{1,2,0:T(8,128)} %param.7) | copy-start | bytes 6148
  12.6 54.7 %all-to-all-start = ((f32[4,2,16,4096]{3,2,1,0:T(8,128)}), f32[4,2,16,4096]{3,2,1,0:T(8,128)S(1)}, u32[]{:S(2)}, u32[]{:S(2)}) async-start(f32[4,2,16,4096]{3,2,1,0:T(8,128)} %fusion.55), calls=%async_computation | async-start | bytes 4194304 | tf_op jit(solution)/shard_map/all_to_all | solution.py:58
  74.6 9.4 %all-to-all-start.1 = ((bf16[2,32,16,128]{3,2,0,1:T(8,128)(2,1)}), bf16[2,32,16,128]{3,2,0,1:T(8,128)(2,1)S(1)}, u32[]{:S(2)}, u32[]{:S(2)}) async-start(bf16[2,32,16,128]{3,2,0,1:T(8,128)(2,1)} %copy.62), calls=%async_computation.1 | async-start | bytes 524288 | tf_op jit(solution)/shard_map/all_to_all | solution.py:81

commit v9 on v5

--- a/solution.py
+++ b/solution.py
@@ -56,6 +56,9 @@
         spread_over(forward, virtual_sources), flat_traces, preferred_element_type=jnp.float32
     ).reshape(freq_total, 2, virtual_sources, source_count)
     gathered = lax.all_to_all(partial, "freq", split_axis=0, concat_axis=0, tiled=True)
+    real_u, imag_u = u_factors[0, 0], u_factors[0, 1]
+    receiver_factors = jnp.stack([jnp.stack([real_u, -imag_u]), jnp.stack([imag_u, real_u])])
+    gathered, receiver_factors = lax.optimization_barrier((gathered, receiver_factors))
     summed = gathered.reshape(
         lax.axis_size("freq"), freq_local, 2, virtual_sources, source_count
     ).sum(axis=0)
@@ -82,17 +85,12 @@
     rows_local = arrived.shape[1]
     columns_all = arrived.shape[2]
     arrived = arrived.reshape(2, rows_local, columns_all, rank_positions, virtual_sources)
-    receiver_factors = u_factors[0]
-    real_arrived, imag_arrived = arrived[0], arrived[1]
-    stacked_arrived = jnp.stack(
-        [jnp.stack([real_arrived, -imag_arrived]), jnp.stack([imag_arrived, real_arrived])]
-    )
     receivers = rows_local * tile_width
     received = (
         jnp.einsum(
-            "imdlh,oimdlu->oumh",
+            "oimdlh,imdlu->oumh",
             receiver_factors,
-            stacked_arrived,
+            arrived,
             preferred_element_type=jnp.float32,
         )
         .reshape(1, 2, virtual_sources, receivers)

time: 112 us -> 112 us (level)
  waiting for transfers between devices: 52.5 us -> 40.4 us
  other arithmetic: 1.14 us -> 11.4 us
    all_to_all x1, waiting for transfers between devices: 47.9 us -> 36 us  [per_device(): lax.all_to_all(partial, 'freq', split_axis=0, concat_axis=0, tiled=True)]
    another operation x1 -> x2, other arithmetic: 0.21 us -> 8.67 us  [per_device(): jnp.stack([jnp.stack([real_u, -imag_u]), jnp.stack([imag_u, real_u])])]
    neg x1, other arithmetic: 0.06 us -> 1.88 us  [per_device(): -imag_u]
    reshape x0 -> x2, local copies, waits for them, and re-layouts: none -> 1.59 us  [per_device(): arrived.reshape(2, rows_local, columns_all, rank_positions, virtual_sources)]
    dot_general x1, matrix products: 3.25 us -> 4.61 us  [per_device(): jnp.einsum('oimdlh,imdlu->oumh', receiver_factors, arrived, preferred_ele...]
    slice x3 -> x0, local copies, waits for them, and re-layouts: 1.19 us -> none  [per_device(): real_arrived, imag_arrived = (arrived[0], arrived[1])]
  transfers between devices with their start and end apart: 2 -> 2, of which waited for: 2 -> 2; matrix products, arithmetic and copies ran while one was open for 2% -> 11% of each run, Pallas kernels for 0% -> 0%
where the time goes in v9:
time: 112 us
  waiting for transfers between devices  40.4 us (36%)
  matrix products  29.5 us (26%)
  blocking collectives  15.6 us (14%)
  other arithmetic  11.4 us (10%)
  starting transfers between devices  10 us (9%)
  local copies, waits for them, and re-layouts  4.42 us (4%)
    all_to_all x1, waiting for transfers between devices, per_device(): lax.all_to_all(partial, 'freq', split_axis=0, concat_axis=0, tiled=True)  36 us
    all_gather x1, blocking collectives, per_device(): piece = lax.all_gather(received, 'freq', axis=0, tiled=True)  15.6 us
    dot_general x1, matrix products, per_device(): jnp.dot(spread_over(forward, virtual_sources), flat_traces, preferred_ele...  11.2 us
    another operation x2, other arithmetic, per_device(): jnp.stack([jnp.stack([real_u, -imag_u]), jnp.stack([imag_u, real_u])])  8.67 us
    all_to_all x1, starting transfers between devices, per_device(): lax.all_to_all(partial, 'freq', split_axis=0, concat_axis=0, tiled=True)  6.45 us
    dot_general x1, matrix products, per_device(): jnp.dot(spread_over(backward, virtual_sources), piece.reshape(count * 2 *...  5.99 us
    dot_general x1, matrix products, per_device(): jnp.einsum('iajrs,oivjs->oajrv', emitter_factors, stacked_spectrum, prefe...  5.65 us
    dot_general x1, matrix products, per_device(): jnp.einsum('oimdlh,imdlu->oumh', receiver_factors, arrived, preferred_ele...  4.61 us
  transfers between devices with their start and end apart: 2, of which 2 were waited for; matrix products, arithmetic and copies ran while one was open for 11% of the time, Pallas kernels for 0%

profile of v9, /device:TPU:0, one launch (start us, length us, event | category | flops | bytes accessed | tf_op | source)
XLA Modules:
  0.0 111.6 jit_solution(5483583334155219792)
XLA Ops:
  0.0 0.1 cosine_convert_fusion
  0.1 0.1 fusion.51
  0.4 0.7 fusion.5
  1.0 11.2 %fusion.58 = f32[4,2,16,4096]{3,2,1,0:T(8,128)} fusion(bf16[4,2,16,2560]{3,2,1,0:T(8,128)(2,1)S(1)} %bitcast.89, bf16[2560,4096,1,1]{1,0,3,2:T(8,128)(2,1)} %bitcast.85), kind=kOutput, calls=%fused_computation.85 | convolution fusion | flops 2684354560 | bytes 23724032 | tf_op jit(solution)/shard_map/dot_general | solution.py:55
  12.2 0.0 copy-start.1
  12.2 6.5 %all-to-all-start = ((f32[4,2,16,4096]{3,2,1,0:T(8,128)}), f32[4,2,16,4096]{3,2,1,0:T(8,128)S(1)}, u32[]{:S(2)}, u32[]{:S(2)}) async-start(f32[4,2,16,4096]{3,2,1,0:T(8,128)} %fusion.58), calls=%async_computation | async-start | bytes 4194304 | tf_op jit(solution)/shard_map/all_to_all | solution.py:58
  18.7 0.1 cosine_convert_fusion.1
  18.8 0.1 fusion.50
  19.0 0.0 copy-start
  19.0 0.0 copy-done.1
  19.0 1.9 %fusion.56 = bf16[1,8,64,8,256]{4,3,2,1,0:T(8,128)(2,1)S(1)} fusion(bf16[1,2,8,64,8,256]{5,4,3,2,1,0:T(8,128)(2,1)} %param.6), kind=kLoop, calls=%fused_computation.83 | loop fusion | flops 1048576 | bytes 4194304 | tf_op jit(solution)/shard_map/neg | solution.py:60
  20.9 0.9 copy-done
  21.8 0.4 slice_bitcast_fusion
  22.2 2.3 %maximum_bitcast_fusion = (bf16[1,2,8,64,8,256]{5,4,3,2,1,0:T(8,128)(2,1)S(1)}, bf16[1,2,8,64,8,256]{5,4,3,2,1,0:T(8,128)(2,1)}) fusion(bf16[1,8,64,8,256]{4,3,2,1,0:T(8,128)(2,1)S(1)} %fusion.56, bf16[1,8,64,8,256]{4,3,2,1,0:T(8,128)(2,1)S(1)} %get-tuple-element.10, bf16[1,8,64,8,256]{4,3,2,1,0:T(8,128)(2,1)S(1)} %get-tuple-element.9), kind=kLoop, calls=%fused_computation.4 | loop fusion | flops 4194304 | bytes 14680064 | tf_op jit(solution)/shard_map/stack | solution.py:60
  24.5 6.3 %pad_maximum_fusion = bf16[2,2,8,64,8,256]{5,4,3,2,1,0:T(8,128)(2,1)} fusion(bf16[1,2,8,64,8,256]{5,4,3,2,1,0:T(8,128)(2,1)} %get-tuple-element.12, bf16[1,2,8,64,8,256]{5,4,3,2,1,0:T(8,128)(2,1)S(1)} %get-tuple-element.11), kind=kLoop, calls=%fused_computation.1 | loop fusion | flops 4194304 | bytes 16777216 | tf_op jit(solution)/shard_map/stack | solution.py:60
  30.9 36.0 %all-to-all-done = f32[4,2,16,4096]{3,2,1,0:T(8,128)S(1)} async-done(((f32[4,2,16,4096]{3,2,1,0:T(8,128)}), f32[4,2,16,4096]{3,2,1,0:T(8,128)S(1)}, u32[]{:S(2)}, u32[]{:S(2)}) %all-to-all-start) | async-done | bytes 2097184 | tf_op jit(solution)/shard_map/all_to_all | solution.py:58
  66.9 0.2 reduce_sum.9
  67.1 0.1 copy_negate_fusion
  67.3 5.7 %fusion.6 = bf16[2,32,16,8,16]{1,4,3,0,2:T(8,128)(2,1)S(1)} fusion(bf16[2,32,16,8,256,1]{4,3,2,1,0,5:T(8,128)(2,1)} %bitcast.95, pred[32,16,8]{0,2,1:T(8,128)(4,1)S(1)} %iota_compare_fusion.5, bf16[1,2,16,16,256]{4,2,1,0,3:T(8,128)(2,1)S(1)} %get-tuple-element.16, bf16[1,2,16,16,256]{4,2,1,0,3:T(8,128)(2,1)S(1)} %get-tuple-element.15), kind=kOutput, calls=%fused_computation.15 | convolution fusion | flops 135528448 | bytes 4984832 | tf_op jit(solution)/shard_map/iajrs,oivjs->oajrv/dot_general | solution.py:72
  73.0 1.2 %copy.49 = bf16[2,32,16,128]{3,2,0,1:T(8,128)(2,1)} copy(bf16[2,32,16,128]{1,3,0,2:T(8,128)(2,1)S(1)} %bitcast.87) | data formatting | bytes 524288 | tf_op jit(solution)/shard_map/reshape | solution.py:83
  74.2 3.6 %all-to-all-start.1 = ((bf16[2,32,16,128]{3,2,0,1:T(8,128)(2,1)}), bf16[2,32,16,128]{3,2,0,1:T(8,128)(2,1)S(1)}, u32[]{:S(2)}, u32[]{:S(2)}) async-start(bf16[2,32,16,128]{3,2,0,1:T(8,128)(2,1)} %copy.49), calls=%async_computation.1 | async-start | bytes 524288 | tf_op jit(solution)/shard_map/all_to_all | solution.py:84
  77.8 1.4 %convolution_convert_fusion = bf16[2560,8]{0,1:T(8,128)(2,1)S(1)} fusion(bf16[160,8]{0,1:T(8,128)(2,1)S(1)} %reshape.536, s32[2560]{0:T(1024)S(1)} %get-tuple-element.19), kind=kOutput, calls=%fused_computation.12 | convolution fusion | flops 6983680 | bytes 53760 | tf_op jit(solution)/shard_map/dot_general | solution.py:29
  79.2 4.4 %all-to-all-done.1 = bf16[2,32,16,128]{3,2,0,1:T(8,128)(2,1)S(1)} async-done(((bf16[2,32,16,128]{3,2,0,1:T(8,128)(2,1)}), bf16[2,32,16,128]{3,2,0,1:T(8,128)(2,1)S(1)}, u32[]{:S(2)}, u32[]{:S(2)}) %all-to-all-start.1) | async-done | bytes 262176 | tf_op jit(solution)/shard_map/all_to_all | solution.py:84
  83.6 0.2 copy.64
  83.9 1.4 %reshape.547 = bf16[2,8,64,8,16,1]{4,3,0,2,1,5:T(8,128)(2,1)S(1)} reshape(bf16[2,8,4,16,128]{4,0,3,2,1:T(2,128)(2,1)S(1)} %copy.64) | data formatting | bytes 524288 | tf_op jit(solution)/shard_map/reshape | solution.py:87
  85.2 4.6 %fusion.21 = bf16[2,16,8,256]{3,1,0,2:T(8,128)(2,1)S(1)} fusion(bf16[2,2,8,64,8,256]{5,4,3,2,1,0:T(8,128)(2,1)} %pad_maximum_fusion, bf16[2,8,64,8,16,1]{4,3,0,2,1,5:T(8,128)(2,1)S(1)} %reshape.547), kind=kOutput, calls=%fused_computation.23 | convolution fusion | flops 134283264 | bytes 8781824 | tf_op jit(solution)/shard_map/oimdlh,imdlu->oumh/dot_general | solution.py:90
  89.8 0.1 copy.54
  89.9 0.1 convert_element_type.137
  90.0 15.6 %all_gather.3 = bf16[4,2,16,2048]{3,2,1,0:T(8,128)(2,1)S(1)} all-gather(bf16[1,2,16,2048]{3,2,1,0:T(8,128)(2,1)S(1)} %convert_element_type.137), channel_id=1, replica_groups=mesh['groups'=2,'freq'=4,'tile'=4] {'freq'}, dimensions={0}, use_global_device_ids=true | all-gather | bytes 655360 | tf_op jit(solution)/shard_map/all_gather | solution.py:99
  105.6 6.0 %multiply_convert_fusion = bf16[2560,2048]{1,0:T(8,128)(2,1)} fusion(bf16[128,2048]{1,0:T(8,128)(2,1)S(1)} %bitcast.86, bf16[2560,8]{0,1:T(8,128)(2,1)S(1)} %convolution_convert_fusion, s32[128]{0:T(128)S(1)} %get-tuple-element.22, s32[2560]{0:T(1024)S(1)} %get-tuple-element.20, s32[128]{0:T(128)S(1)} %get-tuple-element.21), kind=kOutput, calls=%fused_computation | convolution fusion | flops 1358889984 | bytes 11062272 | tf_op jit(solution)/shard_map/dot_general | solution.py:103
  (17 shorter events, 0.3 us)
Async XLA Ops:
  12.2 6.8 %copy-start.1 = (s32[1,32,16]{1,2,0:T(8,128)S(1)}, s32[1,32,16]{1,2,0:T(8,128)}, u32[]{:S(2)}) copy-start(s32[1,32,16]{1,2,0:T(8,128)} %param.7) | copy-start | bytes 6148
  12.2 54.6 %all-to-all-start = ((f32[4,2,16,4096]{3,2,1,0:T(8,128)}), f32[4,2,16,4096]{3,2,1,0:T(8,128)S(1)}, u32[]{:S(2)}, u32[]{:S(2)}) async-start(f32[4,2,16,4096]{3,2,1,0:T(8,128)} %fusion.58), calls=%async_computation | async-start | bytes 4194304 | tf_op jit(solution)/shard_map/all_to_all | solution.py:58
  19.0 2.8 %copy-start = (bf16[1,2,8,64,8,256]{5,4,3,2,1,0:T(8,128)(2,1)S(1)}, bf16[1,2,8,64,8,256]{5,4,3,2,1,0:T(8,128)(2,1)}, u32[]{:S(2)}) copy-start(bf16[1,2,8,64,8,256]{5,4,3,2,1,0:T(8,128)(2,1)} %param.6) | copy-start | bytes 12582916
  74.2 9.4 %all-to-all-start.1 = ((bf16[2,32,16,128]{3,2,0,1:T(8,128)(2,1)}), bf16[2,32,16,128]{3,2,0,1:T(8,128)(2,1)S(1)}, u32[]{:S(2)}, u32[]{:S(2)}) async-start(bf16[2,32,16,128]{3,2,0,1:T(8,128)(2,1)} %copy.49), calls=%async_computation.1 | async-start | bytes 524288 | tf_op jit(solution)/shard_map/all_to_all | solution.py:84

commit v10 on v5

--- a/solution.py
+++ b/solution.py
@@ -55,7 +55,9 @@
     partial = jnp.dot(
         spread_over(forward, virtual_sources), flat_traces, preferred_element_type=jnp.float32
     ).reshape(freq_total, 2, virtual_sources, source_count)
-    gathered = lax.all_to_all(partial, "freq", split_axis=0, concat_axis=0, tiled=True)
+    gathered = lax.all_to_all(
+        partial.reshape(freq_total, -1), "freq", split_axis=0, concat_axis=0, tiled=True
+    )
     summed = gathered.reshape(
         lax.axis_size("freq"), freq_local, 2, virtual_sources, source_count
     ).sum(axis=0)

time: 112 us -> 114 us (1.018)
  local copies, waits for them, and re-layouts: 3.94 us -> 7.52 us
  matrix products: 28.6 us -> 25.4 us
  other arithmetic: 1.14 us -> 2.95 us
    all_to_all x0 -> x1, local copies, waits for them, and re-layouts: none -> 3.47 us  [per_device(): lax.all_to_all(partial.reshape(freq_total, -1), 'freq', split_axis=0, con...]
    dot_general x1, matrix products: 11.6 us -> 8.84 us  [per_device(): jnp.dot(spread_over(forward, virtual_sources), flat_traces, preferred_ele...]
    reduce_sum x1, other arithmetic: 0.16 us -> 1.96 us  [per_device(): summed = gathered.reshape(lax.axis_size('freq'), freq_local, 2, virtual_s...]
where the time goes in v10:
time: 114 us
  waiting for transfers between devices  52.3 us (46%)
  matrix products  25.4 us (22%)
  blocking collectives  15.6 us (14%)
  starting transfers between devices  10 us (9%)
  local copies, waits for them, and re-layouts  7.52 us (7%)
  other arithmetic  2.95 us (3%)
    all_to_all x1, waiting for transfers between devices, per_device(): lax.all_to_all(partial.reshape(freq_total, -1), 'freq', split_axis=0, con...  47.9 us
    all_gather x1, blocking collectives, per_device(): piece = lax.all_gather(received, 'freq', axis=0, tiled=True)  15.6 us
    dot_general x1, matrix products, per_device(): jnp.dot(spread_over(forward, virtual_sources), flat_traces, preferred_ele...  8.84 us
    all_to_all x1, starting transfers between devices, per_device(): lax.all_to_all(partial.reshape(freq_total, -1), 'freq', split_axis=0, con...  6.45 us
    dot_general x1, matrix products, per_device(): jnp.dot(spread_over(backward, virtual_sources), piece.reshape(count * 2 *...  5.99 us
    dot_general x1, matrix products, per_device(): jnp.einsum('iajrs,oivjs->oajrv', emitter_factors, stacked_spectrum, prefe...  5.67 us
    all_to_all x1, waiting for transfers between devices, per_device(): lax.all_to_all(coefficients, 'tile', split_axis=1, concat_axis=2, tiled=T...  4.42 us
    all_to_all x1, starting transfers between devices, per_device(): lax.all_to_all(coefficients, 'tile', split_axis=1, concat_axis=2, tiled=T...  3.59 us
  transfers between devices with their start and end apart: 2, of which 2 were waited for; matrix products, arithmetic and copies ran while one was open for 2% of the time, Pallas kernels for 0%

profile of v10, /device:TPU:0, one launch (start us, length us, event | category | flops | bytes accessed | tf_op | source)
XLA Modules:
  0.0 114.0 jit_solution(2065033391644700895)
XLA Ops:
  0.0 0.1 fusion.50
  0.1 0.1 cosine_convert_fusion
  0.3 0.2 convolution_convert_fusion.1
  0.6 8.8 %fusion.10 = f32[128,4096]{1,0:T(8,128)S(1)} fusion(bf16[2560,4096]{1,0:T(8,128)(2,1)} %bitcast.68, bf16[128,160]{0,1:T(8,128)(2,1)S(1)} %convolution_convert_fusion.1, s32[2560]{0:T(1024)S(1)} %get-tuple-element.15, s32[2560]{0:T(1024)S(1)} %get-tuple-element.16, s32[128]{0:T(128)S(1)} %get-tuple-element.18), kind=kOutput, calls=%fused_computation.15 | convolution fusion | flops 2790604800 | bytes 23130624 | tf_op jit(solution)/shard_map/dot_general | solution.py:55
  9.4 3.5 %all_to_all.22 = f32[4,1,131072]{2,1,0:T(1,128)} reshape(f32[128,4096]{1,0:T(8,128)S(1)} %fusion.10) | data formatting | bytes 4194304 | tf_op jit(solution)/shard_map/all_to_all | solution.py:58
  12.9 0.0 copy-start
  12.9 6.5 %all-to-all-start = ((f32[4,1,131072]{2,1,0:T(1,128)}), f32[4,1,131072]{2,1,0:T(1,128)S(1)}, u32[]{:S(2)}, u32[]{:S(2)}) async-start(f32[4,1,131072]{2,1,0:T(1,128)} %all_to_all.22), calls=%async_computation | async-start | bytes 4194304 | tf_op jit(solution)/shard_map/all_to_all | solution.py:58
  19.4 0.1 fusion.49
  19.5 0.1 cosine_convert_fusion.1
  19.7 0.0 copy-done
  19.7 47.9 %all-to-all-done = f32[4,1,131072]{2,1,0:T(1,128)S(1)} async-done(((f32[4,1,131072]{2,1,0:T(1,128)}), f32[4,1,131072]{2,1,0:T(1,128)S(1)}, u32[]{:S(2)}, u32[]{:S(2)}) %all-to-all-start) | async-done | bytes 2097184 | tf_op jit(solution)/shard_map/all_to_all | solution.py:58
  67.6 2.0 %reduce_sum.9 = f32[131072]{0:T(1024)S(1)} reduce(f32[4,1,131072]{2,1,0:T(1,128)S(1)} %all-to-all-done, f32[]{:T(128)} %constant.116.clone.1), dimensions={0,1}, to_apply=%region_0.1 | reduce | flops 393216 | bytes 2621444 | tf_op jit(solution)/shard_map/reduce_sum | solution.py:63
  69.6 0.1 convert_element_type.133
  69.9 0.1 copy_negate_fusion
  70.0 5.7 %fusion.6 = bf16[2,32,16,8,16]{1,4,3,0,2:T(8,128)(2,1)S(1)} fusion(bf16[2,32,16,8,256,1]{4,3,2,1,0,5:T(8,128)(2,1)} %bitcast.77, pred[32,16,8]{0,2,1:T(8,128)(4,1)S(1)} %iota_compare_fusion.7, bf16[1,2,16,16,256]{4,2,1,0,3:T(8,128)(2,1)S(1)} %get-tuple-element.12, bf16[1,2,16,16,256]{4,2,1,0,3:T(8,128)(2,1)S(1)} %get-tuple-element.11), kind=kOutput, calls=%fused_computation.12 | convolution fusion | flops 135528448 | bytes 4984832 | tf_op jit(solution)/shard_map/iajrs,oivjs->oajrv/dot_general | solution.py:71
  75.6 1.2 %copy.65 = bf16[2,32,16,128]{3,2,0,1:T(8,128)(2,1)} copy(bf16[2,32,16,128]{1,3,0,2:T(8,128)(2,1)S(1)} %bitcast.70) | data formatting | bytes 524288 | tf_op jit(solution)/shard_map/reshape | solution.py:82
  76.9 3.6 %all-to-all-start.1 = ((bf16[2,32,16,128]{3,2,0,1:T(8,128)(2,1)}), bf16[2,32,16,128]{3,2,0,1:T(8,128)(2,1)S(1)}, u32[]{:S(2)}, u32[]{:S(2)}) async-start(bf16[2,32,16,128]{3,2,0,1:T(8,128)(2,1)} %copy.65), calls=%async_computation.1 | async-start | bytes 524288 | tf_op jit(solution)/shard_map/all_to_all | solution.py:83
  80.5 1.4 %convolution_convert_fusion = bf16[2560,8]{0,1:T(8,128)(2,1)S(1)} fusion(bf16[160,8]{0,1:T(8,128)(2,1)S(1)} %reshape.543, s32[2560]{0:T(1024)S(1)} %get-tuple-element.15), kind=kOutput, calls=%fused_computation.9 | convolution fusion | flops 6983680 | bytes 53760 | tf_op jit(solution)/shard_map/dot_general | solution.py:29
  81.9 4.4 %all-to-all-done.1 = bf16[2,32,16,128]{3,2,0,1:T(8,128)(2,1)S(1)} async-done(((bf16[2,32,16,128]{3,2,0,1:T(8,128)(2,1)}), bf16[2,32,16,128]{3,2,0,1:T(8,128)(2,1)S(1)}, u32[]{:S(2)}, u32[]{:S(2)}) %all-to-all-start.1) | async-done | bytes 262176 | tf_op jit(solution)/shard_map/all_to_all | solution.py:83
  86.4 0.7 copy.85
  87.0 0.5 reshape.555
  87.6 0.1 neg.43
  87.6 0.7 copy.84
  88.3 0.5 reshape.554
  88.8 0.2 maximum_bitcast_fusion.2
  89.0 3.2 %fusion.17 = bf16[2,16,8,256]{3,1,0,2:T(8,128)(2,1)S(1)} fusion(bf16[2,8,64,8,256,1]{4,3,2,1,0,5:T(8,128)(2,1)} %bitcast.78, bf16[1,2,8,64,8,16]{3,5,4,1,0,2:T(8,128)(2,1)S(1)} %get-tuple-element.6, bf16[1,2,8,64,8,16]{3,5,4,1,0,2:T(8,128)(2,1)S(1)} %get-tuple-element.5), kind=kOutput, calls=%fused_computation.18 | convolution fusion | flops 134545408 | bytes 4849664 | tf_op jit(solution)/shard_map/imdlh,oimdlu->oumh/dot_general | solution.py:94
  92.3 0.1 copy.74
  92.4 0.1 convert_element_type.137
  92.4 15.6 %all_gather.3 = bf16[4,2,16,2048]{3,2,1,0:T(8,128)(2,1)S(1)} all-gather(bf16[1,2,16,2048]{3,2,1,0:T(8,128)(2,1)S(1)} %convert_element_type.137), channel_id=1, replica_groups=mesh['groups'=2,'freq'=4,'tile'=4] {'freq'}, dimensions={0}, use_global_device_ids=true | all-gather | bytes 655360 | tf_op jit(solution)/shard_map/all_gather | solution.py:103
  108.0 6.0 %multiply_convert_fusion = bf16[2560,2048]{1,0:T(8,128)(2,1)} fusion(bf16[128,2048]{1,0:T(8,128)(2,1)S(1)} %bitcast.69, bf16[2560,8]{0,1:T(8,128)(2,1)S(1)} %convolution_convert_fusion, s32[128]{0:T(128)S(1)} %get-tuple-element.18, s32[2560]{0:T(1024)S(1)} %get-tuple-element.16, s32[128]{0:T(128)S(1)} %get-tuple-element.17), kind=kOutput, calls=%fused_computation | convolution fusion | flops 1358889984 | bytes 11062272 | tf_op jit(solution)/shard_map/dot_general | solution.py:107
  (19 shorter events, 0.3 us)
Async XLA Ops:
  12.9 6.8 %copy-start = (s32[1,32,16]{1,2,0:T(8,128)S(1)}, s32[1,32,16]{1,2,0:T(8,128)}, u32[]{:S(2)}) copy-start(s32[1,32,16]{1,2,0:T(8,128)} %param.7) | copy-start | bytes 6148
  12.9 54.7 %all-to-all-start = ((f32[4,1,131072]{2,1,0:T(1,128)}), f32[4,1,131072]{2,1,0:T(1,128)S(1)}, u32[]{:S(2)}, u32[]{:S(2)}) async-start(f32[4,1,131072]{2,1,0:T(1,128)} %all_to_all.22), calls=%async_computation | async-start | bytes 4194304 | tf_op jit(solution)/shard_map/all_to_all | solution.py:58
  76.9 9.4 %all-to-all-start.1 = ((bf16[2,32,16,128]{3,2,0,1:T(8,128)(2,1)}), bf16[2,32,16,128]{3,2,0,1:T(8,128)(2,1)S(1)}, u32[]{:S(2)}, u32[]{:S(2)}) async-start(bf16[2,32,16,128]{3,2,0,1:T(8,128)(2,1)} %copy.65), calls=%async_computation.1 | async-start | bytes 524288 | tf_op jit(solution)/shard_map/all_to_all | solution.py:83

commit v11 on v5

--- a/solution.py
+++ b/solution.py
@@ -54,7 +54,7 @@
     flat_traces = traces.reshape(time_count * virtual_sources, source_count)
     partial = jnp.dot(
         spread_over(forward, virtual_sources), flat_traces, preferred_element_type=jnp.float32
-    ).reshape(freq_total, 2, virtual_sources, source_count)
+    )
     gathered = lax.all_to_all(partial, "freq", split_axis=0, concat_axis=0, tiled=True)
     summed = gathered.reshape(
         lax.axis_size("freq"), freq_local, 2, virtual_sources, source_count

time: 112 us -> 112 us (level)
  no operation moved by 1% of the time
where the time goes in v11:
time: 112 us
  waiting for transfers between devices  52.5 us (47%)
  matrix products  28.6 us (26%)
  blocking collectives  15.6 us (14%)
  starting transfers between devices  9.86 us (9%)
  local copies, waits for them, and re-layouts  3.94 us (4%)
  other arithmetic  1.14 us (1%)
    all_to_all x1, waiting for transfers between devices, per_device(): lax.all_to_all(partial, 'freq', split_axis=0, concat_axis=0, tiled=True)  47.9 us
    all_gather x1, blocking collectives, per_device(): piece = lax.all_gather(received, 'freq', axis=0, tiled=True)  15.6 us
    dot_general x1, matrix products, per_device(): jnp.dot(spread_over(forward, virtual_sources), flat_traces, preferred_ele...  11.6 us
    all_to_all x1, starting transfers between devices, per_device(): lax.all_to_all(partial, 'freq', split_axis=0, concat_axis=0, tiled=True)  6.45 us
    dot_general x1, matrix products, per_device(): jnp.dot(spread_over(backward, virtual_sources), piece.reshape(count * 2 *...  5.99 us
    dot_general x1, matrix products, per_device(): jnp.einsum('iajrs,oivjs->oajrv', emitter_factors, stacked_spectrum, prefe...  5.68 us
    all_to_all x1, waiting for transfers between devices, per_device(): lax.all_to_all(coefficients, 'tile', split_axis=1, concat_axis=2, tiled=T...  4.6 us
    all_to_all x1, starting transfers between devices, per_device(): lax.all_to_all(coefficients, 'tile', split_axis=1, concat_axis=2, tiled=T...  3.41 us
  transfers between devices with their start and end apart: 2, of which 2 were waited for; matrix products, arithmetic and copies ran while one was open for 2% of the time, Pallas kernels for 0%

profile of v11, /device:TPU:0, one launch (start us, length us, event | category | flops | bytes accessed | tf_op | source)
XLA Modules:
  0.0 111.8 jit_solution(16876691791723271831)
XLA Ops:
  0.0 0.1 fusion.46
  0.1 0.1 cosine_convert_fusion
  0.3 0.7 fusion.5
  1.0 11.6 %fusion.54 = f32[4,32,4096]{2,1,0:T(8,128)} fusion(bf16[4,32,2560]{2,1,0:T(8,128)(2,1)S(1)} %bitcast.77, bf16[2560,4096,1]{1,0,2:T(8,128)(2,1)} %bitcast.72), kind=kOutput, calls=%fused_computation.84 | convolution fusion | flops 2684354560 | bytes 23724032 | tf_op jit(solution)/shard_map/dot_general | solution.py:55
  12.6 0.0 copy-start
  12.6 6.5 %all-to-all-start = ((f32[4,32,4096]{2,1,0:T(8,128)}), f32[4,32,4096]{2,1,0:T(8,128)S(1)}, u32[]{:S(2)}, u32[]{:S(2)}) async-start(f32[4,32,4096]{2,1,0:T(8,128)} %fusion.54), calls=%async_computation | async-start | bytes 4194304 | tf_op jit(solution)/shard_map/all_to_all | solution.py:58
  19.0 0.1 fusion.45
  19.2 0.1 cosine_convert_fusion.1
  19.4 0.0 copy-done
  19.4 47.9 %all-to-all-done = f32[4,32,4096]{2,1,0:T(8,128)S(1)} async-done(((f32[4,32,4096]{2,1,0:T(8,128)}), f32[4,32,4096]{2,1,0:T(8,128)S(1)}, u32[]{:S(2)}, u32[]{:S(2)}) %all-to-all-start) | async-done | bytes 2097184 | tf_op jit(solution)/shard_map/all_to_all | solution.py:58
  67.2 0.2 reduce_sum.9
  67.6 0.1 copy_negate_fusion
  67.7 5.7 %fusion.6 = bf16[2,32,16,8,16]{1,4,3,0,2:T(8,128)(2,1)S(1)} fusion(bf16[2,32,16,8,256,1]{4,3,2,1,0,5:T(8,128)(2,1)} %bitcast.83, pred[32,16,8]{0,2,1:T(8,128)(4,1)S(1)} %iota_compare_fusion.5, bf16[1,2,16,16,256]{4,2,1,0,3:T(8,128)(2,1)S(1)} %get-tuple-element.12, bf16[1,2,16,16,256]{4,2,1,0,3:T(8,128)(2,1)S(1)} %get-tuple-element.11), kind=kOutput, calls=%fused_computation.12 | convolution fusion | flops 135528448 | bytes 4984832 | tf_op jit(solution)/shard_map/iajrs,oivjs->oajrv/dot_general | solution.py:69
  73.4 1.2 %copy.62 = bf16[2,32,16,128]{3,2,0,1:T(8,128)(2,1)} copy(bf16[2,32,16,128]{1,3,0,2:T(8,128)(2,1)S(1)} %bitcast.74) | data formatting | bytes 524288 | tf_op jit(solution)/shard_map/reshape | solution.py:80
  74.6 3.4 %all-to-all-start.1 = ((bf16[2,32,16,128]{3,2,0,1:T(8,128)(2,1)}), bf16[2,32,16,128]{3,2,0,1:T(8,128)(2,1)S(1)}, u32[]{:S(2)}, u32[]{:S(2)}) async-start(bf16[2,32,16,128]{3,2,0,1:T(8,128)(2,1)} %copy.62), calls=%async_computation.1 | async-start | bytes 524288 | tf_op jit(solution)/shard_map/all_to_all | solution.py:81
  78.1 1.4 %convolution_convert_fusion = bf16[2560,8]{0,1:T(8,128)(2,1)S(1)} fusion(bf16[160,8]{0,1:T(8,128)(2,1)S(1)} %reshape.544, s32[2560]{0:T(1024)S(1)} %get-tuple-element.15), kind=kOutput, calls=%fused_computation.9 | convolution fusion | flops 6983680 | bytes 53760 | tf_op jit(solution)/shard_map/dot_general | solution.py:29
  79.5 4.6 %all-to-all-done.1 = bf16[2,32,16,128]{3,2,0,1:T(8,128)(2,1)S(1)} async-done(((bf16[2,32,16,128]{3,2,0,1:T(8,128)(2,1)}), bf16[2,32,16,128]{3,2,0,1:T(8,128)(2,1)S(1)}, u32[]{:S(2)}, u32[]{:S(2)}) %all-to-all-start.1) | async-done | bytes 262176 | tf_op jit(solution)/shard_map/all_to_all | solution.py:81
  84.1 0.7 copy.82
  84.8 0.5 reshape.557
  85.3 0.1 neg.43
  85.4 0.7 copy.81
  86.0 0.5 reshape.556
  86.6 0.2 maximum_bitcast_fusion.2
  86.8 3.2 %fusion.16 = bf16[2,16,8,256]{3,1,0,2:T(8,128)(2,1)S(1)} fusion(bf16[2,8,64,8,256,1]{4,3,2,1,0,5:T(8,128)(2,1)} %bitcast.84, bf16[1,2,8,64,8,16]{3,5,4,1,0,2:T(8,128)(2,1)S(1)} %get-tuple-element.6, bf16[1,2,8,64,8,16]{3,5,4,1,0,2:T(8,128)(2,1)S(1)} %get-tuple-element.5), kind=kOutput, calls=%fused_computation.17 | convolution fusion | flops 134545408 | bytes 4849664 | tf_op jit(solution)/shard_map/imdlh,oimdlu->oumh/dot_general | solution.py:92
  90.0 0.1 copy.71
  90.1 0.1 convert_element_type.137
  90.2 15.6 %all_gather.3 = bf16[4,2,16,2048]{3,2,1,0:T(8,128)(2,1)S(1)} all-gather(bf16[1,2,16,2048]{3,2,1,0:T(8,128)(2,1)S(1)} %convert_element_type.137), channel_id=1, replica_groups=mesh['groups'=2,'freq'=4,'tile'=4] {'freq'}, dimensions={0}, use_global_device_ids=true | all-gather | bytes 655360 | tf_op jit(solution)/shard_map/all_gather | solution.py:101
  105.8 6.0 %multiply_convert_fusion = bf16[2560,2048]{1,0:T(8,128)(2,1)} fusion(bf16[128,2048]{1,0:T(8,128)(2,1)S(1)} %bitcast.73, bf16[2560,8]{0,1:T(8,128)(2,1)S(1)} %convolution_convert_fusion, s32[128]{0:T(128)S(1)} %get-tuple-element.18, s32[2560]{0:T(1024)S(1)} %get-tuple-element.16, s32[128]{0:T(128)S(1)} %get-tuple-element.17), kind=kOutput, calls=%fused_computation | convolution fusion | flops 1358889984 | bytes 11062272 | tf_op jit(solution)/shard_map/dot_general | solution.py:105
  (19 shorter events, 0.3 us)
Async XLA Ops:
  12.6 6.8 %copy-start = (s32[1,32,16]{1,2,0:T(8,128)S(1)}, s32[1,32,16]{1,2,0:T(8,128)}, u32[]{:S(2)}) copy-start(s32[1,32,16]{1,2,0:T(8,128)} %param.7) | copy-start | bytes 6148
  12.6 54.7 %all-to-all-start = ((f32[4,32,4096]{2,1,0:T(8,128)}), f32[4,32,4096]{2,1,0:T(8,128)S(1)}, u32[]{:S(2)}, u32[]{:S(2)}) async-start(f32[4,32,4096]{2,1,0:T(8,128)} %fusion.54), calls=%async_computation | async-start | bytes 4194304 | tf_op jit(solution)/shard_map/all_to_all | solution.py:58
  74.6 9.4 %all-to-all-start.1 = ((bf16[2,32,16,128]{3,2,0,1:T(8,128)(2,1)}), bf16[2,32,16,128]{3,2,0,1:T(8,128)(2,1)S(1)}, u32[]{:S(2)}, u32[]{:S(2)}) async-start(bf16[2,32,16,128]{3,2,0,1:T(8,128)(2,1)} %copy.62), calls=%async_computation.1 | async-start | bytes 524288 | tf_op jit(solution)/shard_map/all_to_all | solution.py:81

commit v12 on v11

--- a/solution.py
+++ b/solution.py
@@ -52,8 +52,19 @@
 
     forward = jnp.stack([cosine, -sine], 1).reshape(freq_total * 2, time_count)
     flat_traces = traces.reshape(time_count * virtual_sources, source_count)
-    partial = jnp.dot(
-        spread_over(forward, virtual_sources), flat_traces, preferred_element_type=jnp.float32
+    weights = spread_over(forward, virtual_sources)
+    halves = 2 if source_count % 256 == 0 else 1
+    span = source_count // halves
+    partial = jnp.concatenate(
+        [
+            jnp.dot(
+                weights,
+                flat_traces[:, half * span:(half + 1) * span],
+                preferred_element_type=jnp.float32,
+            )
+            for half in range(halves)
+        ],
+        axis=1,
     )
     gathered = lax.all_to_all(partial, "freq", split_axis=0, concat_axis=0, tiled=True)
     summed = gathered.reshape(

time: 112 us -> 113 us (level)
  other arithmetic: 1.14 us -> 2.6 us
    concatenate x0 -> x1, other arithmetic: none -> 1.46 us  [per_device(): jnp.concatenate([jnp.dot(weights, flat_traces[:, half * span:(half + 1) *...]
    dot_general x1 -> x2, matrix products: 11.6 us -> 11.4 us  [per_device(): jnp.dot(weights, flat_traces[:, half * span:(half + 1) * span], preferred...]
where the time goes in v12:
time: 113 us
  waiting for transfers between devices  52.4 us (46%)
  matrix products  28.3 us (25%)
  blocking collectives  15.6 us (14%)
  starting transfers between devices  9.73 us (9%)
  local copies, waits for them, and re-layouts  3.93 us (3%)
  other arithmetic  2.6 us (2%)
    all_to_all x1, waiting for transfers between devices, per_device(): lax.all_to_all(partial, 'freq', split_axis=0, concat_axis=0, tiled=True)  47.8 us
    all_gather x1, blocking collectives, per_device(): piece = lax.all_gather(received, 'freq', axis=0, tiled=True)  15.6 us
    dot_general x2, matrix products, per_device(): jnp.dot(weights, flat_traces[:, half * span:(half + 1) * span], preferred...  11.4 us
    all_to_all x1, starting transfers between devices, per_device(): lax.all_to_all(partial, 'freq', split_axis=0, concat_axis=0, tiled=True)  6.32 us
    dot_general x1, matrix products, per_device(): jnp.dot(spread_over(backward, virtual_sources), piece.reshape(count * 2 *...  5.99 us
    dot_general x1, matrix products, per_device(): jnp.einsum('iajrs,oivjs->oajrv', emitter_factors, stacked_spectrum, prefe...  5.66 us
    all_to_all x1, waiting for transfers between devices, per_device(): lax.all_to_all(coefficients, 'tile', split_axis=1, concat_axis=2, tiled=T...  4.6 us
    all_to_all x1, starting transfers between devices, per_device(): lax.all_to_all(coefficients, 'tile', split_axis=1, concat_axis=2, tiled=T...  3.41 us
  transfers between devices with their start and end apart: 2, of which 2 were waited for; matrix products, arithmetic and copies ran while one was open for 2% of the time, Pallas kernels for 0%

profile of v12, /device:TPU:0, one launch (start us, length us, event | category | flops | bytes accessed | tf_op | source)
XLA Modules:
  0.0 112.9 jit_solution(14568832651376890657)
XLA Ops:
  0.0 0.1 fusion.50
  0.1 0.1 cosine_convert_fusion
  0.3 0.7 fusion.9
  1.0 5.7 %fusion = f32[128,2048]{1,0:T(8,128)S(1)} fusion(bf16[128,2560]{1,0:T(8,128)(2,1)S(1)} %fusion.9, bf16[2560,4096]{1,0:T(8,128)(2,1)} %bitcast.80), kind=kOutput, calls=%fused_computation.1 | convolution fusion | flops 1342177280 | bytes 12189696 | tf_op jit(solution)/shard_map/dot_general | solution.py:60
  6.7 5.7 %fusion.2 = f32[128,2048]{1,0:T(8,128)S(1)} fusion(bf16[128,2560]{1,0:T(8,128)(2,1)S(1)} %fusion.9, bf16[2560,4096]{1,0:T(8,128)(2,1)} %bitcast.81), kind=kOutput, calls=%fused_computation.3 | convolution fusion | flops 1342177280 | bytes 12189696 | tf_op jit(solution)/shard_map/dot_general | solution.py:60
  12.4 0.0 copy-start
  12.4 1.5 %pad_maximum_fusion = f32[128,4096]{1,0:T(8,128)} fusion(f32[128,2048]{1,0:T(8,128)S(1)} %fusion, f32[128,2048]{1,0:T(8,128)S(1)} %fusion.2), kind=kLoop, calls=%fused_computation.15 | loop fusion | flops 524288 | bytes 4194304 | tf_op jit(solution)/shard_map/concatenate | solution.py:58
  13.9 6.3 %all-to-all-start = ((f32[4,32,4096]{2,1,0:T(8,128)}), f32[4,32,4096]{2,1,0:T(8,128)S(1)}, u32[]{:S(2)}, u32[]{:S(2)}) async-start(f32[4,32,4096]{2,1,0:T(8,128)} %bitcast.70), calls=%async_computation | async-start | bytes 4194304 | tf_op jit(solution)/shard_map/all_to_all | solution.py:69
  20.2 0.1 fusion.49
  20.3 0.1 cosine_convert_fusion.1
  20.5 0.0 copy-done
  20.6 47.8 %all-to-all-done = f32[4,32,4096]{2,1,0:T(8,128)S(1)} async-done(((f32[4,32,4096]{2,1,0:T(8,128)}), f32[4,32,4096]{2,1,0:T(8,128)S(1)}, u32[]{:S(2)}, u32[]{:S(2)}) %all-to-all-start) | async-done | bytes 2097184 | tf_op jit(solution)/shard_map/all_to_all | solution.py:69
  68.4 0.2 reduce_sum.9
  68.8 0.1 copy_negate_fusion
  68.9 5.7 %fusion.10 = bf16[2,32,16,8,16]{1,4,3,0,2:T(8,128)(2,1)S(1)} fusion(bf16[2,32,16,8,256,1]{4,3,2,1,0,5:T(8,128)(2,1)} %bitcast.82, pred[32,16,8]{0,2,1:T(8,128)(4,1)S(1)} %iota_compare_fusion.5, bf16[1,2,16,16,256]{4,2,1,0,3:T(8,128)(2,1)S(1)} %get-tuple-element.12, bf16[1,2,16,16,256]{4,2,1,0,3:T(8,128)(2,1)S(1)} %get-tuple-element.11), kind=kOutput, calls=%fused_computation.17 | convolution fusion | flops 135528448 | bytes 4984832 | tf_op jit(solution)/shard_map/iajrs,oivjs->oajrv/dot_general | solution.py:80
  74.5 1.2 %copy.62 = bf16[2,32,16,128]{3,2,0,1:T(8,128)(2,1)} copy(bf16[2,32,16,128]{1,3,0,2:T(8,128)(2,1)S(1)} %bitcast.72) | data formatting | bytes 524288 | tf_op jit(solution)/shard_map/reshape | solution.py:91
  75.8 3.4 %all-to-all-start.1 = ((bf16[2,32,16,128]{3,2,0,1:T(8,128)(2,1)}), bf16[2,32,16,128]{3,2,0,1:T(8,128)(2,1)S(1)}, u32[]{:S(2)}, u32[]{:S(2)}) async-start(bf16[2,32,16,128]{3,2,0,1:T(8,128)(2,1)} %copy.62), calls=%async_computation.1 | async-start | bytes 524288 | tf_op jit(solution)/shard_map/all_to_all | solution.py:92
  79.2 1.4 %convolution_convert_fusion = bf16[2560,8]{0,1:T(8,128)(2,1)S(1)} fusion(bf16[160,8]{0,1:T(8,128)(2,1)S(1)} %reshape.543, s32[2560]{0:T(1024)S(1)} %get-tuple-element.15), kind=kOutput, calls=%fused_computation.13 | convolution fusion | flops 6983680 | bytes 53760 | tf_op jit(solution)/shard_map/dot_general | solution.py:29
  80.6 4.6 %all-to-all-done.1 = bf16[2,32,16,128]{3,2,0,1:T(8,128)(2,1)S(1)} async-done(((bf16[2,32,16,128]{3,2,0,1:T(8,128)(2,1)}), bf16[2,32,16,128]{3,2,0,1:T(8,128)(2,1)S(1)}, u32[]{:S(2)}, u32[]{:S(2)}) %all-to-all-start.1) | async-done | bytes 262176 | tf_op jit(solution)/shard_map/all_to_all | solution.py:92
  85.2 0.6 copy.82
  85.9 0.5 reshape.555
  86.4 0.1 neg.43
  86.5 0.6 copy.81
  87.1 0.5 reshape.554
  87.7 0.2 maximum_bitcast_fusion.2
  87.9 3.2 %fusion.20 = bf16[2,16,8,256]{3,1,0,2:T(8,128)(2,1)S(1)} fusion(bf16[2,8,64,8,256,1]{4,3,2,1,0,5:T(8,128)(2,1)} %bitcast.83, bf16[1,2,8,64,8,16]{3,5,4,1,0,2:T(8,128)(2,1)S(1)} %get-tuple-element.6, bf16[1,2,8,64,8,16]{3,5,4,1,0,2:T(8,128)(2,1)S(1)} %get-tuple-element.5), kind=kOutput, calls=%fused_computation.22 | convolution fusion | flops 134545408 | bytes 4849664 | tf_op jit(solution)/shard_map/imdlh,oimdlu->oumh/dot_general | solution.py:103
  91.1 0.1 copy.71
  91.2 0.1 convert_element_type.137
  91.3 15.6 %all_gather.3 = bf16[4,2,16,2048]{3,2,1,0:T(8,128)(2,1)S(1)} all-gather(bf16[1,2,16,2048]{3,2,1,0:T(8,128)(2,1)S(1)} %convert_element_type.137), channel_id=1, replica_groups=mesh['groups'=2,'freq'=4,'tile'=4] {'freq'}, dimensions={0}, use_global_device_ids=true | all-gather | bytes 655360 | tf_op jit(solution)/shard_map/all_gather | solution.py:112
  106.9 6.0 %multiply_convert_fusion = bf16[2560,2048]{1,0:T(8,128)(2,1)} fusion(bf16[128,2048]{1,0:T(8,128)(2,1)S(1)} %bitcast.71, bf16[2560,8]{0,1:T(8,128)(2,1)S(1)} %convolution_convert_fusion, s32[128]{0:T(128)S(1)} %get-tuple-element.18, s32[2560]{0:T(1024)S(1)} %get-tuple-element.16, s32[128]{0:T(128)S(1)} %get-tuple-element.17), kind=kOutput, calls=%fused_computation | convolution fusion | flops 1358889984 | bytes 11062272 | tf_op jit(solution)/shard_map/dot_general | solution.py:116
  (19 shorter events, 0.3 us)
Async XLA Ops:
  12.4 8.1 %copy-start = (s32[1,32,16]{1,2,0:T(8,128)S(1)}, s32[1,32,16]{1,2,0:T(8,128)}, u32[]{:S(2)}) copy-start(s32[1,32,16]{1,2,0:T(8,128)} %param.7) | copy-start | bytes 6148
  13.9 54.5 %all-to-all-start = ((f32[4,32,4096]{2,1,0:T(8,128)}), f32[4,32,4096]{2,1,0:T(8,128)S(1)}, u32[]{:S(2)}, u32[]{:S(2)}) async-start(f32[4,32,4096]{2,1,0:T(8,128)} %bitcast.70), calls=%async_computation | async-start | bytes 4194304 | tf_op jit(solution)/shard_map/all_to_all | solution.py:69
  75.8 9.4 %all-to-all-start.1 = ((bf16[2,32,16,128]{3,2,0,1:T(8,128)(2,1)}), bf16[2,32,16,128]{3,2,0,1:T(8,128)(2,1)S(1)}, u32[]{:S(2)}, u32[]{:S(2)}) async-start(bf16[2,32,16,128]{3,2,0,1:T(8,128)(2,1)} %copy.62), calls=%async_computation.1 | async-start | bytes 524288 | tf_op jit(solution)/shard_map/all_to_all | solution.py:92

commit v13 on v4

--- a/solution.py
+++ b/solution.py
@@ -35,6 +35,23 @@
     return jnp.where(same, wide, jnp.float32(0.0)).astype(kind)
 
 
+def line_reduce_scatter(partial, axis):
+    count = partial.shape[0]
+    own = lax.axis_index(axis)
+
+    def block(index):
+        return lax.dynamic_index_in_dim(partial, jnp.clip(index, 0, count - 1), 0, keepdims=False)
+
+    right = jnp.zeros_like(partial[0])
+    left = jnp.zeros_like(partial[0])
+    for step in range(1, count):
+        send_right = block(count - step + own) + right
+        send_left = block(own + step - count) + left
+        right = lax.ppermute(send_right, axis, [(p, p + 1) for p in range(step)])
+        left = lax.ppermute(send_left, axis, [(count - 1 - p, count - 2 - p) for p in range(step)])
+    return block(own) + right + left
+
+
 def per_device(traces, v_factors, u_factors, ranks):
     time_count = traces.shape[0]
     virtual_sources = traces.shape[1]
@@ -55,7 +72,12 @@
     partial = jnp.dot(
         spread_over(forward, virtual_sources), flat_traces, preferred_element_type=jnp.float32
     ).reshape(freq_total, 2, virtual_sources, source_count)
-    summed = lax.psum_scatter(partial, "freq", scatter_dimension=0, tiled=True)
+    gathered = lax.all_to_all(partial[:, 0], "freq", split_axis=0, concat_axis=0, tiled=True)
+    real_sum = gathered.reshape(
+        lax.axis_size("freq"), freq_local, virtual_sources, source_count
+    ).sum(axis=0)
+    imag_sum = line_reduce_scatter(partial[:, 1], "freq")[None]
+    summed = jnp.stack([real_sum, imag_sum], axis=1)
     spectrum = (summed * scale_time).astype(jnp.bfloat16)[0]
     spectral_tiles = spectrum.reshape(2, virtual_sources, columns, tile_width)
     emitter_factors = v_factors[0]

time: 119 us -> 113 us (0.950)
  starting transfers between devices: 3.41 us -> 23.9 us
  between operations: 13.6 us -> 0.35 us
  waiting for transfers between devices: 51 us -> 40.4 us
  matrix products: 28.5 us -> 25.7 us
    reduce_scatter x1 -> x0, waiting for transfers between devices: 46.4 us -> none  [per_device(): summed = lax.psum_scatter(partial, 'freq', scatter_dimension=0, tiled=True)]
    ppermute x0 -> x6, waiting for transfers between devices: none -> 35.8 us  [the longest x3 21 us: line_reduce_scatter(): right = lax.ppermute(send_right, axis, [(p, p + 1) for p in range(step)])]
    ppermute x0 -> x6, starting transfers between devices: none -> 17 us  [the longest x3 14.4 us: line_reduce_scatter(): right = lax.ppermute(send_right, axis, [(p, p + 1) for p in range(step)])]
    all_to_all x0 -> x1, starting transfers between devices: none -> 3.53 us  [per_device(): lax.all_to_all(partial[:, 0], 'freq', split_axis=0, concat_axis=0, tiled=...]
    dot_general x1, matrix products: 11.6 us -> 8.71 us  [per_device(): jnp.dot(spread_over(forward, virtual_sources), flat_traces, preferred_ele...]
  transfers between devices with their start and end apart: 2 -> 8, of which waited for: 2 -> 5; matrix products, arithmetic and copies ran while one was open for 1% -> 2% of each run, Pallas kernels for 0% -> 0%
where the time goes in v13:
time: 113 us; the launch traced here: 112 us
  waiting for transfers between devices  40.4 us (36%)
  matrix products  25.7 us (23%)
  starting transfers between devices  23.9 us (21%)
  blocking collectives  15.6 us (14%)
  local copies, waits for them, and re-layouts  5.07 us (4%)
  other arithmetic  1.25 us (1%)
    ppermute x3, waiting for transfers between devices, line_reduce_scatter(): right = lax.ppermute(send_right, axis, [(p, p + 1) for p in range(step)])  21 us
    all_gather x1, blocking collectives, per_device(): piece = lax.all_gather(received, 'freq', axis=0, tiled=True)  15.6 us
    ppermute x3, waiting for transfers between devices, line_reduce_scatter(): lax.ppermute(send_left, axis, [(count - 1 - p, count - 2 - p) for p in ra...  14.8 us
    ppermute x3, starting transfers between devices, line_reduce_scatter(): right = lax.ppermute(send_right, axis, [(p, p + 1) for p in range(step)])  14.4 us
    dot_general x1, matrix products, per_device(): jnp.dot(spread_over(forward, virtual_sources), flat_traces, preferred_ele...  8.71 us
    dot_general x1, matrix products, per_device(): jnp.dot(spread_over(backward, virtual_sources), piece.reshape(count * 2 *...  5.99 us
    dot_general x1, matrix products, per_device(): jnp.einsum('iajrs,oivjs->oajrv', emitter_factors, stacked_spectrum, prefe...  5.66 us
    all_to_all x1, waiting for transfers between devices, per_device(): lax.all_to_all(coefficients, 'tile', split_axis=1, concat_axis=2, tiled=T...  4.6 us
  transfers between devices with their start and end apart: 8, of which 5 were waited for; matrix products, arithmetic and copies ran while one was open for 2% of the time, Pallas kernels for 0%

profile of v13, /device:TPU:0, one launch (start us, length us, event | category | flops | bytes accessed | tf_op | source)
XLA Modules:
  0.0 112.2 jit_solution(13356745956112649959)
XLA Ops:
  0.0 0.1 fusion.49
  0.1 0.1 cosine_convert_fusion
  0.4 0.7 fusion.5
  1.0 8.7 %fusion.57 = f32[4,2,16,4096]{3,2,1,0:T(8,128)S(1)} fusion(bf16[4,2,16,2560]{3,2,1,0:T(8,128)(2,1)S(1)} %bitcast.101, bf16[2560,4096,1,1]{1,0,3,2:T(8,128)(2,1)} %bitcast.96), kind=kOutput, calls=%fused_computation.95 | convolution fusion | flops 2684354560 | bytes 23724032 | tf_op jit(solution)/shard_map/dot_general | solution.py:72
  9.7 1.1 slice_bitcast_fusion
  10.9 4.9 %collective-permute-start = (f32[16,4096]{1,0:T(8,128)S(1)}, f32[16,4096]{1,0:T(8,128)S(1)}, u32[]{:S(2)}, u32[]{:S(2)}) collective-permute-start(f32[16,4096]{1,0:T(8,128)S(1)} %get-tuple-element.9), channel_id=1, source_target_pairs={{0,4},{1,5},{2,6},{3,7},{16,20},{17,21},{18,22},{19,23}} | collective-permute-start | bytes 786440 | tf_op jit(solution)/shard_map/ppermute | solution.py:50
  15.8 0.7 collective-permute-start.3
  16.5 4.8 %collective-permute-done = f32[16,4096]{1,0:T(8,128)S(1)} collective-permute-done((f32[16,4096]{1,0:T(8,128)S(1)}, f32[16,4096]{1,0:T(8,128)S(1)}, u32[]{:S(2)}, u32[]{:S(2)}) %collective-permute-start) | collective-permute-done | bytes 262176 | tf_op jit(solution)/shard_map/ppermute | solution.py:50
  21.4 4.4 %collective-permute-start.1 = (f32[16,4096]{1,0:T(8,128)S(1)}, f32[16,4096]{1,0:T(8,128)S(1)}, u32[]{:S(2)}, u32[]{:S(2)}) collective-permute-start(f32[16,4096]{1,0:T(8,128)S(1)} %bitcast_add_fusion.2), channel_id=1, source_target_pairs={{0,4},{4,8},{1,5},{5,9},{2,6},{6,10},{3,7},{7,11},{16,20},{20,24},... | collective-permute-start | bytes 786440 | tf_op jit(solution)/shard_map/ppermute | solution.py:50
  25.8 3.5 %all-to-all-start = ((f32[4,16,4096]{2,1,0:T(8,128)}), f32[4,16,4096]{2,1,0:T(8,128)S(1)}, u32[]{:S(2)}, u32[]{:S(2)}) async-start(f32[4,16,4096]{2,1,0:T(8,128)} %get-tuple-element.5), calls=%async_computation | async-start | bytes 2097152 | tf_op jit(solution)/shard_map/all_to_all | solution.py:75
  29.4 2.9 %collective-permute-done.1 = f32[16,4096]{1,0:T(8,128)S(1)} collective-permute-done((f32[16,4096]{1,0:T(8,128)S(1)}, f32[16,4096]{1,0:T(8,128)S(1)}, u32[]{:S(2)}, u32[]{:S(2)}) %collective-permute-start.1) | collective-permute-done | bytes 262176 | tf_op jit(solution)/shard_map/ppermute | solution.py:50
  32.3 0.7 collective-permute-start.4
  33.0 0.1 fusion.48
  33.2 0.1 cosine_convert_fusion.1
  33.3 5.0 %collective-permute-start.2 = (f32[16,4096]{1,0:T(8,128)S(1)}, f32[16,4096]{1,0:T(8,128)S(1)}, u32[]{:S(2)}, u32[]{:S(2)}) collective-permute-start(f32[16,4096]{1,0:T(8,128)S(1)} %get-tuple-element.7), channel_id=1, source_target_pairs={{0,4},{4,8},{8,12},{1,5},{5,9},{9,13},{2,6},{6,10},{10,14},{3,7},{... | collective-permute-start | bytes 786440 | tf_op jit(solution)/shard_map/ppermute | solution.py:50
  38.4 1.3 %collective-permute-start.5 = (f32[16,4096]{1,0:T(8,128)S(1)}, f32[16,4096]{1,0:T(8,128)S(1)}, u32[]{:S(2)}, u32[]{:S(2)}) collective-permute-start(f32[16,4096]{1,0:T(8,128)S(1)} %bitcast_add_fusion.1), channel_id=1, source_target_pairs={{12,8},{8,4},{4,0},{13,9},{9,5},{5,1},{14,10},{10,6},{6,2},{15,11}... | collective-permute-start | bytes 786440 | tf_op jit(solution)/shard_map/ppermute | solution.py:51
  39.8 13.2 %collective-permute-done.2 = f32[16,4096]{1,0:T(8,128)S(1)} collective-permute-done((f32[16,4096]{1,0:T(8,128)S(1)}, f32[16,4096]{1,0:T(8,128)S(1)}, u32[]{:S(2)}, u32[]{:S(2)}) %collective-permute-start.2) | collective-permute-done | bytes 262176 | tf_op jit(solution)/shard_map/ppermute | solution.py:50
  53.0 14.8 %collective-permute-done.5 = f32[16,4096]{1,0:T(8,128)S(1)} collective-permute-done((f32[16,4096]{1,0:T(8,128)S(1)}, f32[16,4096]{1,0:T(8,128)S(1)}, u32[]{:S(2)}, u32[]{:S(2)}) %collective-permute-start.5) | collective-permute-done | bytes 262176 | tf_op jit(solution)/shard_map/ppermute | solution.py:51
  68.3 5.7 %fusion.6 = bf16[2,32,16,8,16]{1,4,3,0,2:T(8,128)(2,1)S(1)} fusion(bf16[2,32,16,8,256,1]{4,3,2,1,0,5:T(8,128)(2,1)} %bitcast.107, pred[32,16,8]{0,2,1:T(8,128)(4,1)S(1)} %iota_compare_fusion.5, bf16[1,2,16,16,256]{4,2,1,0,3:T(8,128)(2,1)S(1)} %get-tuple-element.18, bf16[1,2,16,16,256]{4,2,1,0,3:T(8,128)(2,1)S(1)} %get-tuple-element.17), kind=kOutput, calls=%fused_computation.12 | convolution fusion | flops 135528448 | bytes 4984832 | tf_op jit(solution)/shard_map/iajrs,oivjs->oajrv/dot_general | solution.py:88
  73.9 1.2 %copy.62 = bf16[2,32,16,128]{3,2,0,1:T(8,128)(2,1)} copy(bf16[2,32,16,128]{1,3,0,2:T(8,128)(2,1)S(1)} %bitcast.99) | data formatting | bytes 524288 | tf_op jit(solution)/shard_map/reshape | solution.py:99
  75.2 3.4 %all-to-all-start.1 = ((bf16[2,32,16,128]{3,2,0,1:T(8,128)(2,1)}), bf16[2,32,16,128]{3,2,0,1:T(8,128)(2,1)S(1)}, u32[]{:S(2)}, u32[]{:S(2)}) async-start(bf16[2,32,16,128]{3,2,0,1:T(8,128)(2,1)} %copy.62), calls=%async_computation.1 | async-start | bytes 524288 | tf_op jit(solution)/shard_map/all_to_all | solution.py:100
  78.6 1.4 %convolution_convert_fusion = bf16[2560,8]{0,1:T(8,128)(2,1)S(1)} fusion(bf16[160,8]{0,1:T(8,128)(2,1)S(1)} %reshape.577, s32[2560]{0:T(1024)S(1)} %get-tuple-element.23), kind=kOutput, calls=%fused_computation.9 | convolution fusion | flops 6983680 | bytes 53760 | tf_op jit(solution)/shard_map/dot_general | solution.py:29
  80.0 4.6 %all-to-all-done.1 = bf16[2,32,16,128]{3,2,0,1:T(8,128)(2,1)S(1)} async-done(((bf16[2,32,16,128]{3,2,0,1:T(8,128)(2,1)}), bf16[2,32,16,128]{3,2,0,1:T(8,128)(2,1)S(1)}, u32[]{:S(2)}, u32[]{:S(2)}) %all-to-all-start.1) | async-done | bytes 262176 | tf_op jit(solution)/shard_map/all_to_all | solution.py:100
  84.6 0.6 copy.83
  85.3 0.5 reshape.590
  85.9 0.6 copy.82
  86.5 0.5 reshape.589
  87.1 0.2 maximum_bitcast_fusion.2
  87.3 3.2 %fusion.16 = bf16[2,16,8,256]{3,1,0,2:T(8,128)(2,1)S(1)} fusion(bf16[2,8,64,8,256,1]{4,3,2,1,0,5:T(8,128)(2,1)} %bitcast.108, bf16[1,2,8,64,8,16]{3,5,4,1,0,2:T(8,128)(2,1)S(1)} %get-tuple-element.12, bf16[1,2,8,64,8,16]{3,5,4,1,0,2:T(8,128)(2,1)S(1)} %get-tuple-element.11), kind=kOutput, calls=%fused_computation.17 | convolution fusion | flops 134545408 | bytes 4849664 | tf_op jit(solution)/shard_map/imdlh,oimdlu->oumh/dot_general | solution.py:111
  90.5 0.1 copy.71
  90.7 15.6 %all_gather.3 = bf16[4,2,16,2048]{3,2,1,0:T(8,128)(2,1)S(1)} all-gather(bf16[1,2,16,2048]{3,2,1,0:T(8,128)(2,1)S(1)} %convert_element_type.133), channel_id=1, replica_groups=mesh['groups'=2,'freq'=4,'tile'=4] {'freq'}, dimensions={0}, use_global_device_ids=true | all-gather | bytes 655360 | tf_op jit(solution)/shard_map/all_gather | solution.py:120
  106.3 6.0 %multiply_convert_fusion = bf16[2560,2048]{1,0:T(8,128)(2,1)} fusion(bf16[128,2048]{1,0:T(8,128)(2,1)S(1)} %bitcast.97, bf16[2560,8]{0,1:T(8,128)(2,1)S(1)} %convolution_convert_fusion, s32[128]{0:T(128)S(1)} %get-tuple-element.22, s32[2560]{0:T(1024)S(1)} %get-tuple-element.24, s32[128]{0:T(128)S(1)} %get-tuple-element.21), kind=kOutput, calls=%fused_computation | convolution fusion | flops 1358889984 | bytes 11062272 | tf_op jit(solution)/shard_map/dot_general | solution.py:124
  (33 shorter events, 0.8 us)
Async XLA Ops:
  10.9 10.5 %collective-permute-start = (f32[16,4096]{1,0:T(8,128)S(1)}, f32[16,4096]{1,0:T(8,128)S(1)}, u32[]{:S(2)}, u32[]{:S(2)}) collective-permute-start(f32[16,4096]{1,0:T(8,128)S(1)} %get-tuple-element.9), channel_id=1, source_target_pairs={{0,4},{1,5},{2,6},{3,7},{16,20},{17,21},{18,22},{19,23}} | collective-permute-start | bytes 786440 | tf_op jit(solution)/shard_map/ppermute | solution.py:50
  15.8 13.5 %collective-permute-start.3 = (f32[16,4096]{1,0:T(8,128)S(1)}, f32[16,4096]{1,0:T(8,128)S(1)}, u32[]{:S(2)}, u32[]{:S(2)}) collective-permute-start(f32[16,4096]{1,0:T(8,128)S(1)} %get-tuple-element.10), channel_id=1, source_target_pairs={{12,8},{13,9},{14,10},{15,11},{28,24},{29,25},{30,26},{31,27}} | collective-permute-start | bytes 786440 | tf_op jit(solution)/shard_map/ppermute | solution.py:51
  16.5 23.2 %copy-start = (s32[1,32,16]{1,2,0:T(8,128)S(1)}, s32[1,32,16]{1,2,0:T(8,128)}, u32[]{:S(2)}) copy-start(s32[1,32,16]{1,2,0:T(8,128)} %param.7) | copy-start | bytes 6148
  21.4 10.9 %collective-permute-start.1 = (f32[16,4096]{1,0:T(8,128)S(1)}, f32[16,4096]{1,0:T(8,128)S(1)}, u32[]{:S(2)}, u32[]{:S(2)}) collective-permute-start(f32[16,4096]{1,0:T(8,128)S(1)} %bitcast_add_fusion.2), channel_id=1, source_target_pairs={{0,4},{4,8},{1,5},{5,9},{2,6},{6,10},{3,7},{7,11},{16,20},{20,24},... | collective-permute-start | bytes 786440 | tf_op jit(solution)/shard_map/ppermute | solution.py:50
  25.8 42.0 %all-to-all-start = ((f32[4,16,4096]{2,1,0:T(8,128)}), f32[4,16,4096]{2,1,0:T(8,128)S(1)}, u32[]{:S(2)}, u32[]{:S(2)}) async-start(f32[4,16,4096]{2,1,0:T(8,128)} %get-tuple-element.5), calls=%async_computation | async-start | bytes 2097152 | tf_op jit(solution)/shard_map/all_to_all | solution.py:75
  32.3 6.0 %collective-permute-start.4 = (f32[16,4096]{1,0:T(8,128)S(1)}, f32[16,4096]{1,0:T(8,128)S(1)}, u32[]{:S(2)}, u32[]{:S(2)}) collective-permute-start(f32[16,4096]{1,0:T(8,128)S(1)} %get-tuple-element.8), channel_id=1, source_target_pairs={{12,8},{8,4},{13,9},{9,5},{14,10},{10,6},{15,11},{11,7},{28,24},{2... | collective-permute-start | bytes 786440 | tf_op jit(solution)/shard_map/ppermute | solution.py:51
  33.3 19.7 %collective-permute-start.2 = (f32[16,4096]{1,0:T(8,128)S(1)}, f32[16,4096]{1,0:T(8,128)S(1)}, u32[]{:S(2)}, u32[]{:S(2)}) collective-permute-start(f32[16,4096]{1,0:T(8,128)S(1)} %get-tuple-element.7), channel_id=1, source_target_pairs={{0,4},{4,8},{8,12},{1,5},{5,9},{9,13},{2,6},{6,10},{10,14},{3,7},{... | collective-permute-start | bytes 786440 | tf_op jit(solution)/shard_map/ppermute | solution.py:50
  38.4 29.4 %collective-permute-start.5 = (f32[16,4096]{1,0:T(8,128)S(1)}, f32[16,4096]{1,0:T(8,128)S(1)}, u32[]{:S(2)}, u32[]{:S(2)}) collective-permute-start(f32[16,4096]{1,0:T(8,128)S(1)} %bitcast_add_fusion.1), channel_id=1, source_target_pairs={{12,8},{8,4},{4,0},{13,9},{9,5},{5,1},{14,10},{10,6},{6,2},{15,11}... | collective-permute-start | bytes 786440 | tf_op jit(solution)/shard_map/ppermute | solution.py:51
  75.2 9.4 %all-to-all-start.1 = ((bf16[2,32,16,128]{3,2,0,1:T(8,128)(2,1)}), bf16[2,32,16,128]{3,2,0,1:T(8,128)(2,1)S(1)}, u32[]{:S(2)}, u32[]{:S(2)}) async-start(bf16[2,32,16,128]{3,2,0,1:T(8,128)(2,1)} %copy.62), calls=%async_computation.1 | async-start | bytes 524288 | tf_op jit(solution)/shard_map/all_to_all | solution.py:100

commit v14 on v5

--- a/solution.py
+++ b/solution.py
@@ -55,10 +55,10 @@
     partial = jnp.dot(
         spread_over(forward, virtual_sources), flat_traces, preferred_element_type=jnp.float32
     ).reshape(freq_total, 2, virtual_sources, source_count)
-    gathered = lax.all_to_all(partial, "freq", split_axis=0, concat_axis=0, tiled=True)
+    gathered = lax.all_to_all(partial[:, ::-1], "freq", split_axis=0, concat_axis=0, tiled=True)
     summed = gathered.reshape(
         lax.axis_size("freq"), freq_local, 2, virtual_sources, source_count
-    ).sum(axis=0)
+    ).sum(axis=0)[:, ::-1]
     spectrum = (summed * scale_time).astype(jnp.bfloat16)[0]
     spectral_tiles = spectrum.reshape(2, virtual_sources, columns, tile_width)
     emitter_factors = v_factors[0]

time: 112 us -> 111 us (level)
  matrix products: 28.6 us -> 25.7 us
  local copies, waits for them, and re-layouts: 3.94 us -> 5.4 us
    dot_general x1, matrix products: 11.6 us -> 8.71 us  [per_device(): jnp.dot(spread_over(forward, virtual_sources), flat_traces, preferred_ele...]
    rev x0 -> x1, local copies, waits for them, and re-layouts: none -> 1.46 us  [per_device(): partial[:, ::-1]]
where the time goes in v14:
time: 111 us; the launch traced here: 110 us
  waiting for transfers between devices  52.4 us (47%)
  matrix products  25.7 us (23%)
  blocking collectives  15.6 us (14%)
  starting transfers between devices  9.86 us (9%)
  local copies, waits for them, and re-layouts  5.4 us (5%)
  other arithmetic  1.14 us (1%)
    all_to_all x1, waiting for transfers between devices, per_device(): lax.all_to_all(partial[:, ::-1], 'freq', split_axis=0, concat_axis=0, til...  47.8 us
    all_gather x1, blocking collectives, per_device(): piece = lax.all_gather(received, 'freq', axis=0, tiled=True)  15.6 us
    dot_general x1, matrix products, per_device(): jnp.dot(spread_over(forward, virtual_sources), flat_traces, preferred_ele...  8.71 us
    all_to_all x1, starting transfers between devices, per_device(): lax.all_to_all(partial[:, ::-1], 'freq', split_axis=0, concat_axis=0, til...  6.46 us
    dot_general x1, matrix products, per_device(): jnp.dot(spread_over(backward, virtual_sources), piece.reshape(count * 2 *...  5.99 us
    dot_general x1, matrix products, per_device(): jnp.einsum('iajrs,oivjs->oajrv', emitter_factors, stacked_spectrum, prefe...  5.67 us
    all_to_all x1, waiting for transfers between devices, per_device(): lax.all_to_all(coefficients, 'tile', split_axis=1, concat_axis=2, tiled=T...  4.6 us
    all_to_all x1, starting transfers between devices, per_device(): lax.all_to_all(coefficients, 'tile', split_axis=1, concat_axis=2, tiled=T...  3.41 us
  transfers between devices with their start and end apart: 2, of which 2 were waited for; matrix products, arithmetic and copies ran while one was open for 2% of the time, Pallas kernels for 0%

profile of v14, /device:TPU:0, one launch (start us, length us, event | category | flops | bytes accessed | tf_op | source)
XLA Modules:
  0.0 110.4 jit_solution(7334195748054421044)
XLA Ops:
  0.0 0.1 fusion.47
  0.1 0.1 cosine_convert_fusion
  0.3 0.7 fusion.5
  1.0 8.7 %fusion.55 = f32[4,2,16,4096]{3,2,1,0:T(8,128)S(1)} fusion(bf16[4,2,16,2560]{3,2,1,0:T(8,128)(2,1)S(1)} %bitcast.79, bf16[2560,4096,1,1]{1,0,3,2:T(8,128)(2,1)} %bitcast.75), kind=kOutput, calls=%fused_computation.85 | convolution fusion | flops 2684354560 | bytes 23724032 | tf_op jit(solution)/shard_map/dot_general | solution.py:55
  9.7 1.5 %rev.4 = f32[4,2,16,4096]{3,2,1,0:T(8,128)} reverse(f32[4,2,16,4096]{3,2,1,0:T(8,128)S(1)} %fusion.55), dimensions={1} | reverse | bytes 4194304 | tf_op jit(solution)/shard_map/rev | solution.py:58
  11.2 0.0 copy-start
  11.2 6.5 %all-to-all-start = ((f32[4,2,16,4096]{3,2,1,0:T(8,128)}), f32[4,2,16,4096]{3,2,1,0:T(8,128)S(1)}, u32[]{:S(2)}, u32[]{:S(2)}) async-start(f32[4,2,16,4096]{3,2,1,0:T(8,128)} %rev.4), calls=%async_computation | async-start | bytes 4194304 | tf_op jit(solution)/shard_map/all_to_all | solution.py:58
  17.7 0.1 fusion.46
  17.8 0.1 cosine_convert_fusion.1
  18.0 0.0 copy-done
  18.0 47.8 %all-to-all-done = f32[4,2,16,4096]{3,2,1,0:T(8,128)S(1)} async-done(((f32[4,2,16,4096]{3,2,1,0:T(8,128)}), f32[4,2,16,4096]{3,2,1,0:T(8,128)S(1)}, u32[]{:S(2)}, u32[]{:S(2)}) %all-to-all-start) | async-done | bytes 2097184 | tf_op jit(solution)/shard_map/all_to_all | solution.py:58
  65.9 0.2 reduce_sum.9
  66.2 0.1 copy_negate_fusion
  66.3 5.7 %fusion.6 = bf16[2,32,16,8,16]{1,4,3,0,2:T(8,128)(2,1)S(1)} fusion(bf16[2,32,16,8,256,1]{4,3,2,1,0,5:T(8,128)(2,1)} %bitcast.85, pred[32,16,8]{0,2,1:T(8,128)(4,1)S(1)} %iota_compare_fusion.5, bf16[1,2,16,16,256]{4,2,1,0,3:T(8,128)(2,1)S(1)} %get-tuple-element.12, bf16[1,2,16,16,256]{4,2,1,0,3:T(8,128)(2,1)S(1)} %get-tuple-element.11), kind=kOutput, calls=%fused_computation.12 | convolution fusion | flops 135528448 | bytes 4984832 | tf_op jit(solution)/shard_map/iajrs,oivjs->oajrv/dot_general | solution.py:69
  72.0 1.2 %copy.62 = bf16[2,32,16,128]{3,2,0,1:T(8,128)(2,1)} copy(bf16[2,32,16,128]{1,3,0,2:T(8,128)(2,1)S(1)} %bitcast.77) | data formatting | bytes 524288 | tf_op jit(solution)/shard_map/reshape | solution.py:80
  73.2 3.4 %all-to-all-start.1 = ((bf16[2,32,16,128]{3,2,0,1:T(8,128)(2,1)}), bf16[2,32,16,128]{3,2,0,1:T(8,128)(2,1)S(1)}, u32[]{:S(2)}, u32[]{:S(2)}) async-start(bf16[2,32,16,128]{3,2,0,1:T(8,128)(2,1)} %copy.62), calls=%async_computation.1 | async-start | bytes 524288 | tf_op jit(solution)/shard_map/all_to_all | solution.py:81
  76.7 1.4 %convolution_convert_fusion = bf16[2560,8]{0,1:T(8,128)(2,1)S(1)} fusion(bf16[160,8]{0,1:T(8,128)(2,1)S(1)} %reshape.525, s32[2560]{0:T(1024)S(1)} %get-tuple-element.15), kind=kOutput, calls=%fused_computation.9 | convolution fusion | flops 6983680 | bytes 53760 | tf_op jit(solution)/shard_map/dot_general | solution.py:29
  78.1 4.6 %all-to-all-done.1 = bf16[2,32,16,128]{3,2,0,1:T(8,128)(2,1)S(1)} async-done(((bf16[2,32,16,128]{3,2,0,1:T(8,128)(2,1)}), bf16[2,32,16,128]{3,2,0,1:T(8,128)(2,1)S(1)}, u32[]{:S(2)}, u32[]{:S(2)}) %all-to-all-start.1) | async-done | bytes 262176 | tf_op jit(solution)/shard_map/all_to_all | solution.py:81
  82.7 0.7 copy.83
  83.4 0.5 reshape.538
  83.9 0.1 neg.43
  84.0 0.7 copy.82
  84.6 0.5 reshape.537
  85.2 0.2 maximum_bitcast_fusion.2
  85.4 3.2 %fusion.16 = bf16[2,16,8,256]{3,1,0,2:T(8,128)(2,1)S(1)} fusion(bf16[2,8,64,8,256,1]{4,3,2,1,0,5:T(8,128)(2,1)} %bitcast.86, bf16[1,2,8,64,8,16]{3,5,4,1,0,2:T(8,128)(2,1)S(1)} %get-tuple-element.6, bf16[1,2,8,64,8,16]{3,5,4,1,0,2:T(8,128)(2,1)S(1)} %get-tuple-element.5), kind=kOutput, calls=%fused_computation.17 | convolution fusion | flops 134545408 | bytes 4849664 | tf_op jit(solution)/shard_map/imdlh,oimdlu->oumh/dot_general | solution.py:92
  88.6 0.1 copy.71
  88.7 0.1 convert_element_type.129
  88.8 15.6 %all_gather.3 = bf16[4,2,16,2048]{3,2,1,0:T(8,128)(2,1)S(1)} all-gather(bf16[1,2,16,2048]{3,2,1,0:T(8,128)(2,1)S(1)} %convert_element_type.129), channel_id=1, replica_groups=mesh['groups'=2,'freq'=4,'tile'=4] {'freq'}, dimensions={0}, use_global_device_ids=true | all-gather | bytes 655360 | tf_op jit(solution)/shard_map/all_gather | solution.py:101
  104.4 6.0 %multiply_convert_fusion = bf16[2560,2048]{1,0:T(8,128)(2,1)} fusion(bf16[128,2048]{1,0:T(8,128)(2,1)S(1)} %bitcast.76, bf16[2560,8]{0,1:T(8,128)(2,1)S(1)} %convolution_convert_fusion, s32[128]{0:T(128)S(1)} %get-tuple-element.18, s32[2560]{0:T(1024)S(1)} %get-tuple-element.16, s32[128]{0:T(128)S(1)} %get-tuple-element.17), kind=kOutput, calls=%fused_computation | convolution fusion | flops 1358889984 | bytes 11062272 | tf_op jit(solution)/shard_map/dot_general | solution.py:105
  (19 shorter events, 0.3 us)
Async XLA Ops:
  11.2 6.8 %copy-start = (s32[1,32,16]{1,2,0:T(8,128)S(1)}, s32[1,32,16]{1,2,0:T(8,128)}, u32[]{:S(2)}) copy-start(s32[1,32,16]{1,2,0:T(8,128)} %param.7) | copy-start | bytes 6148
  11.2 54.6 %all-to-all-start = ((f32[4,2,16,4096]{3,2,1,0:T(8,128)}), f32[4,2,16,4096]{3,2,1,0:T(8,128)S(1)}, u32[]{:S(2)}, u32[]{:S(2)}) async-start(f32[4,2,16,4096]{3,2,1,0:T(8,128)} %rev.4), calls=%async_computation | async-start | bytes 4194304 | tf_op jit(solution)/shard_map/all_to_all | solution.py:58
  73.2 9.4 %all-to-all-start.1 = ((bf16[2,32,16,128]{3,2,0,1:T(8,128)(2,1)}), bf16[2,32,16,128]{3,2,0,1:T(8,128)(2,1)S(1)}, u32[]{:S(2)}, u32[]{:S(2)}) async-start(bf16[2,32,16,128]{3,2,0,1:T(8,128)(2,1)} %copy.62), calls=%async_computation.1 | async-start | bytes 524288 | tf_op jit(solution)/shard_map/all_to_all | solution.py:81

commit v15 on v9

--- a/solution.py
+++ b/solution.py
@@ -55,13 +55,13 @@
     partial = jnp.dot(
         spread_over(forward, virtual_sources), flat_traces, preferred_element_type=jnp.float32
     ).reshape(freq_total, 2, virtual_sources, source_count)
-    gathered = lax.all_to_all(partial, "freq", split_axis=0, concat_axis=0, tiled=True)
+    gathered = lax.all_to_all(partial[:, ::-1], "freq", split_axis=0, concat_axis=0, tiled=True)
     real_u, imag_u = u_factors[0, 0], u_factors[0, 1]
     receiver_factors = jnp.stack([jnp.stack([real_u, -imag_u]), jnp.stack([imag_u, real_u])])
     gathered, receiver_factors = lax.optimization_barrier((gathered, receiver_factors))
     summed = gathered.reshape(
         lax.axis_size("freq"), freq_local, 2, virtual_sources, source_count
-    ).sum(axis=0)
+    ).sum(axis=0)[:, ::-1]
     spectrum = (summed * scale_time).astype(jnp.bfloat16)[0]
     spectral_tiles = spectrum.reshape(2, virtual_sources, columns, tile_width)
     emitter_factors = v_factors[0]

time: 112 us -> 111 us (level)
  matrix products: 29.5 us -> 26.8 us
  local copies, waits for them, and re-layouts: 4.42 us -> 5.89 us
    dot_general x1, matrix products: 11.2 us -> 8.52 us  [per_device(): jnp.dot(spread_over(forward, virtual_sources), flat_traces, preferred_ele...]
    rev x0 -> x1, local copies, waits for them, and re-layouts: none -> 1.47 us  [per_device(): partial[:, ::-1]]
where the time goes in v15:
time: 111 us; the launch traced here: 110 us
  waiting for transfers between devices  40.6 us (37%)
  matrix products  26.8 us (24%)
  blocking collectives  15.6 us (14%)
  other arithmetic  11.4 us (10%)
  starting transfers between devices  9.72 us (9%)
  local copies, waits for them, and re-layouts  5.89 us (5%)
    all_to_all x1, waiting for transfers between devices, per_device(): lax.all_to_all(partial[:, ::-1], 'freq', split_axis=0, concat_axis=0, til...  36 us
    all_gather x1, blocking collectives, per_device(): piece = lax.all_gather(received, 'freq', axis=0, tiled=True)  15.6 us
    another operation x2, other arithmetic, per_device(): jnp.stack([jnp.stack([real_u, -imag_u]), jnp.stack([imag_u, real_u])])  8.67 us
    dot_general x1, matrix products, per_device(): jnp.dot(spread_over(forward, virtual_sources), flat_traces, preferred_ele...  8.52 us
    all_to_all x1, starting transfers between devices, per_device(): lax.all_to_all(partial[:, ::-1], 'freq', split_axis=0, concat_axis=0, til...  6.32 us
    dot_general x1, matrix products, per_device(): jnp.dot(spread_over(backward, virtual_sources), piece.reshape(count * 2 *...  5.99 us
    dot_general x1, matrix products, per_device(): jnp.einsum('iajrs,oivjs->oajrv', emitter_factors, stacked_spectrum, prefe...  5.65 us
    dot_general x1, matrix products, per_device(): jnp.einsum('oimdlh,imdlu->oumh', receiver_factors, arrived, preferred_ele...  4.61 us
  transfers between devices with their start and end apart: 2, of which 2 were waited for; matrix products, arithmetic and copies ran while one was open for 11% of the time, Pallas kernels for 0%

profile of v15, /device:TPU:0, one launch (start us, length us, event | category | flops | bytes accessed | tf_op | source)
XLA Modules:
  0.0 110.3 jit_solution(2165017994113186760)
XLA Ops:
  0.0 0.1 cosine_convert_fusion
  0.1 0.1 fusion.51
  0.4 0.7 fusion.5
  1.0 8.5 %fusion.58 = f32[4,2,16,4096]{3,2,1,0:T(8,128)S(1)} fusion(bf16[4,2,16,2560]{3,2,1,0:T(8,128)(2,1)S(1)} %bitcast.89, bf16[2560,4096,1,1]{1,0,3,2:T(8,128)(2,1)} %bitcast.85), kind=kOutput, calls=%fused_computation.85 | convolution fusion | flops 2684354560 | bytes 23724032 | tf_op jit(solution)/shard_map/dot_general | solution.py:55
  9.6 0.0 copy-start.1
  9.6 1.5 %rev.4 = f32[4,2,16,4096]{3,2,1,0:T(8,128)} reverse(f32[4,2,16,4096]{3,2,1,0:T(8,128)S(1)} %fusion.58), dimensions={1} | reverse | bytes 4194304 | tf_op jit(solution)/shard_map/rev | solution.py:58
  11.0 6.3 %all-to-all-start = ((f32[4,2,16,4096]{3,2,1,0:T(8,128)}), f32[4,2,16,4096]{3,2,1,0:T(8,128)S(1)}, u32[]{:S(2)}, u32[]{:S(2)}) async-start(f32[4,2,16,4096]{3,2,1,0:T(8,128)} %rev.4), calls=%async_computation | async-start | bytes 4194304 | tf_op jit(solution)/shard_map/all_to_all | solution.py:58
  17.4 0.1 cosine_convert_fusion.1
  17.5 0.1 fusion.50
  17.7 0.0 copy-start
  17.7 0.0 copy-done.1
  17.7 1.9 %fusion.56 = bf16[1,8,64,8,256]{4,3,2,1,0:T(8,128)(2,1)S(1)} fusion(bf16[1,2,8,64,8,256]{5,4,3,2,1,0:T(8,128)(2,1)} %param.6), kind=kLoop, calls=%fused_computation.83 | loop fusion | flops 1048576 | bytes 4194304 | tf_op jit(solution)/shard_map/neg | solution.py:60
  19.6 0.9 copy-done
  20.5 0.4 slice_bitcast_fusion
  20.9 2.3 %maximum_bitcast_fusion = (bf16[1,2,8,64,8,256]{5,4,3,2,1,0:T(8,128)(2,1)S(1)}, bf16[1,2,8,64,8,256]{5,4,3,2,1,0:T(8,128)(2,1)}) fusion(bf16[1,8,64,8,256]{4,3,2,1,0:T(8,128)(2,1)S(1)} %fusion.56, bf16[1,8,64,8,256]{4,3,2,1,0:T(8,128)(2,1)S(1)} %get-tuple-element.10, bf16[1,8,64,8,256]{4,3,2,1,0:T(8,128)(2,1)S(1)} %get-tuple-element.9), kind=kLoop, calls=%fused_computation.4 | loop fusion | flops 4194304 | bytes 14680064 | tf_op jit(solution)/shard_map/stack | solution.py:60
  23.2 6.3 %pad_maximum_fusion = bf16[2,2,8,64,8,256]{5,4,3,2,1,0:T(8,128)(2,1)} fusion(bf16[1,2,8,64,8,256]{5,4,3,2,1,0:T(8,128)(2,1)} %get-tuple-element.12, bf16[1,2,8,64,8,256]{5,4,3,2,1,0:T(8,128)(2,1)S(1)} %get-tuple-element.11), kind=kLoop, calls=%fused_computation.1 | loop fusion | flops 4194304 | bytes 16777216 | tf_op jit(solution)/shard_map/stack | solution.py:60
  29.6 36.0 %all-to-all-done = f32[4,2,16,4096]{3,2,1,0:T(8,128)S(1)} async-done(((f32[4,2,16,4096]{3,2,1,0:T(8,128)}), f32[4,2,16,4096]{3,2,1,0:T(8,128)S(1)}, u32[]{:S(2)}, u32[]{:S(2)}) %all-to-all-start) | async-done | bytes 2097184 | tf_op jit(solution)/shard_map/all_to_all | solution.py:58
  65.6 0.2 reduce_sum.9
  65.8 0.1 copy_negate_fusion
  66.0 5.7 %fusion.6 = bf16[2,32,16,8,16]{1,4,3,0,2:T(8,128)(2,1)S(1)} fusion(bf16[2,32,16,8,256,1]{4,3,2,1,0,5:T(8,128)(2,1)} %bitcast.95, pred[32,16,8]{0,2,1:T(8,128)(4,1)S(1)} %iota_compare_fusion.5, bf16[1,2,16,16,256]{4,2,1,0,3:T(8,128)(2,1)S(1)} %get-tuple-element.16, bf16[1,2,16,16,256]{4,2,1,0,3:T(8,128)(2,1)S(1)} %get-tuple-element.15), kind=kOutput, calls=%fused_computation.15 | convolution fusion | flops 135528448 | bytes 4984832 | tf_op jit(solution)/shard_map/iajrs,oivjs->oajrv/dot_general | solution.py:72
  71.7 1.2 %copy.49 = bf16[2,32,16,128]{3,2,0,1:T(8,128)(2,1)} copy(bf16[2,32,16,128]{1,3,0,2:T(8,128)(2,1)S(1)} %bitcast.87) | data formatting | bytes 524288 | tf_op jit(solution)/shard_map/reshape | solution.py:83
  72.9 3.4 %all-to-all-start.1 = ((bf16[2,32,16,128]{3,2,0,1:T(8,128)(2,1)}), bf16[2,32,16,128]{3,2,0,1:T(8,128)(2,1)S(1)}, u32[]{:S(2)}, u32[]{:S(2)}) async-start(bf16[2,32,16,128]{3,2,0,1:T(8,128)(2,1)} %copy.49), calls=%async_computation.1 | async-start | bytes 524288 | tf_op jit(solution)/shard_map/all_to_all | solution.py:84
  76.3 1.4 %convolution_convert_fusion = bf16[2560,8]{0,1:T(8,128)(2,1)S(1)} fusion(bf16[160,8]{0,1:T(8,128)(2,1)S(1)} %reshape.524, s32[2560]{0:T(1024)S(1)} %get-tuple-element.19), kind=kOutput, calls=%fused_computation.12 | convolution fusion | flops 6983680 | bytes 53760 | tf_op jit(solution)/shard_map/dot_general | solution.py:29
  77.7 4.6 %all-to-all-done.1 = bf16[2,32,16,128]{3,2,0,1:T(8,128)(2,1)S(1)} async-done(((bf16[2,32,16,128]{3,2,0,1:T(8,128)(2,1)}), bf16[2,32,16,128]{3,2,0,1:T(8,128)(2,1)S(1)}, u32[]{:S(2)}, u32[]{:S(2)}) %all-to-all-start.1) | async-done | bytes 262176 | tf_op jit(solution)/shard_map/all_to_all | solution.py:84
  82.3 0.2 copy.64
  82.6 1.4 %reshape.535 = bf16[2,8,64,8,16,1]{4,3,0,2,1,5:T(8,128)(2,1)S(1)} reshape(bf16[2,8,4,16,128]{4,0,3,2,1:T(2,128)(2,1)S(1)} %copy.64) | data formatting | bytes 524288 | tf_op jit(solution)/shard_map/reshape | solution.py:87
  83.9 4.6 %fusion.21 = bf16[2,16,8,256]{3,1,0,2:T(8,128)(2,1)S(1)} fusion(bf16[2,2,8,64,8,256]{5,4,3,2,1,0:T(8,128)(2,1)} %pad_maximum_fusion, bf16[2,8,64,8,16,1]{4,3,0,2,1,5:T(8,128)(2,1)S(1)} %reshape.535), kind=kOutput, calls=%fused_computation.23 | convolution fusion | flops 134283264 | bytes 8781824 | tf_op jit(solution)/shard_map/oimdlh,imdlu->oumh/dot_general | solution.py:90
  88.5 0.1 copy.54
  88.6 0.1 convert_element_type.129
  88.7 15.6 %all_gather.3 = bf16[4,2,16,2048]{3,2,1,0:T(8,128)(2,1)S(1)} all-gather(bf16[1,2,16,2048]{3,2,1,0:T(8,128)(2,1)S(1)} %convert_element_type.129), channel_id=1, replica_groups=mesh['groups'=2,'freq'=4,'tile'=4] {'freq'}, dimensions={0}, use_global_device_ids=true | all-gather | bytes 655360 | tf_op jit(solution)/shard_map/all_gather | solution.py:99
  104.3 6.0 %multiply_convert_fusion = bf16[2560,2048]{1,0:T(8,128)(2,1)} fusion(bf16[128,2048]{1,0:T(8,128)(2,1)S(1)} %bitcast.86, bf16[2560,8]{0,1:T(8,128)(2,1)S(1)} %convolution_convert_fusion, s32[128]{0:T(128)S(1)} %get-tuple-element.22, s32[2560]{0:T(1024)S(1)} %get-tuple-element.20, s32[128]{0:T(128)S(1)} %get-tuple-element.21), kind=kOutput, calls=%fused_computation | convolution fusion | flops 1358889984 | bytes 11062272 | tf_op jit(solution)/shard_map/dot_general | solution.py:103
  (17 shorter events, 0.3 us)
Async XLA Ops:
  9.6 8.1 %copy-start.1 = (s32[1,32,16]{1,2,0:T(8,128)S(1)}, s32[1,32,16]{1,2,0:T(8,128)}, u32[]{:S(2)}) copy-start(s32[1,32,16]{1,2,0:T(8,128)} %param.7) | copy-start | bytes 6148
  11.0 54.5 %all-to-all-start = ((f32[4,2,16,4096]{3,2,1,0:T(8,128)}), f32[4,2,16,4096]{3,2,1,0:T(8,128)S(1)}, u32[]{:S(2)}, u32[]{:S(2)}) async-start(f32[4,2,16,4096]{3,2,1,0:T(8,128)} %rev.4), calls=%async_computation | async-start | bytes 4194304 | tf_op jit(solution)/shard_map/all_to_all | solution.py:58
  17.7 2.8 %copy-start = (bf16[1,2,8,64,8,256]{5,4,3,2,1,0:T(8,128)(2,1)S(1)}, bf16[1,2,8,64,8,256]{5,4,3,2,1,0:T(8,128)(2,1)}, u32[]{:S(2)}) copy-start(bf16[1,2,8,64,8,256]{5,4,3,2,1,0:T(8,128)(2,1)} %param.6) | copy-start | bytes 12582916
  72.9 9.4 %all-to-all-start.1 = ((bf16[2,32,16,128]{3,2,0,1:T(8,128)(2,1)}), bf16[2,32,16,128]{3,2,0,1:T(8,128)(2,1)S(1)}, u32[]{:S(2)}, u32[]{:S(2)}) async-start(bf16[2,32,16,128]{3,2,0,1:T(8,128)(2,1)} %copy.49), calls=%async_computation.1 | async-start | bytes 524288 | tf_op jit(solution)/shard_map/all_to_all | solution.py:84

commit v16 on v14

--- a/solution.py
+++ b/solution.py
@@ -102,13 +102,18 @@
     count = piece.shape[0]
 
     backward = jnp.stack([cosine.T, -sine.T], 2).reshape(time_count, count * 2)
+    scale_freq = 1.0 / math.sqrt(freq_total)
+    exact_scale = math.log2(scale_freq).is_integer()
+    if exact_scale:
+        backward = backward * jnp.bfloat16(scale_freq)
     added = jnp.dot(
         spread_over(backward, virtual_sources),
         piece.reshape(count * 2 * virtual_sources, receivers),
         preferred_element_type=jnp.float32,
     )
-    scale_freq = 1.0 / math.sqrt(freq_total)
-    return (added * scale_freq).astype(jnp.bfloat16).reshape(time_count, virtual_sources, receivers)
+    if not exact_scale:
+        added = added * scale_freq
+    return added.astype(jnp.bfloat16).reshape(time_count, virtual_sources, receivers)
 
 
 def solution(mesh):

time: 111 us -> 111 us (level)
  no operation moved by 1% of the time
where the time goes in v16:
time: 111 us; the launch traced here: 110 us
  waiting for transfers between devices  52.4 us (47%)
  matrix products  25.7 us (23%)
  blocking collectives  15.6 us (14%)
  starting transfers between devices  9.86 us (9%)
  local copies, waits for them, and re-layouts  5.4 us (5%)
  other arithmetic  1.14 us (1%)
    all_to_all x1, waiting for transfers between devices, per_device(): lax.all_to_all(partial[:, ::-1], 'freq', split_axis=0, concat_axis=0, til...  47.8 us
    all_gather x1, blocking collectives, per_device(): piece = lax.all_gather(received, 'freq', axis=0, tiled=True)  15.6 us
    dot_general x1, matrix products, per_device(): jnp.dot(spread_over(forward, virtual_sources), flat_traces, preferred_ele...  8.71 us
    all_to_all x1, starting transfers between devices, per_device(): lax.all_to_all(partial[:, ::-1], 'freq', split_axis=0, concat_axis=0, til...  6.46 us
    dot_general x1, matrix products, per_device(): jnp.dot(spread_over(backward, virtual_sources), piece.reshape(count * 2 *...  5.99 us
    dot_general x1, matrix products, per_device(): jnp.einsum('iajrs,oivjs->oajrv', emitter_factors, stacked_spectrum, prefe...  5.67 us
    all_to_all x1, waiting for transfers between devices, per_device(): lax.all_to_all(coefficients, 'tile', split_axis=1, concat_axis=2, tiled=T...  4.6 us
    all_to_all x1, starting transfers between devices, per_device(): lax.all_to_all(coefficients, 'tile', split_axis=1, concat_axis=2, tiled=T...  3.41 us
  transfers between devices with their start and end apart: 2, of which 2 were waited for; matrix products, arithmetic and copies ran while one was open for 2% of the time, Pallas kernels for 0%

profile of v16, /device:TPU:0, one launch (start us, length us, event | category | flops | bytes accessed | tf_op | source)
XLA Modules:
  0.0 110.4 jit_solution(14232672328520298374)
XLA Ops:
  0.0 0.1 fusion.47
  0.1 0.1 cosine_convert_fusion
  0.3 0.7 fusion.5
  1.0 8.7 %fusion.55 = f32[4,2,16,4096]{3,2,1,0:T(8,128)S(1)} fusion(bf16[4,2,16,2560]{3,2,1,0:T(8,128)(2,1)S(1)} %bitcast.79, bf16[2560,4096,1,1]{1,0,3,2:T(8,128)(2,1)} %bitcast.75), kind=kOutput, calls=%fused_computation.85 | convolution fusion | flops 2684354560 | bytes 23724032 | tf_op jit(solution)/shard_map/dot_general | solution.py:55
  9.7 1.5 %rev.4 = f32[4,2,16,4096]{3,2,1,0:T(8,128)} reverse(f32[4,2,16,4096]{3,2,1,0:T(8,128)S(1)} %fusion.55), dimensions={1} | reverse | bytes 4194304 | tf_op jit(solution)/shard_map/rev | solution.py:58
  11.2 0.0 copy-start
  11.2 6.5 %all-to-all-start = ((f32[4,2,16,4096]{3,2,1,0:T(8,128)}), f32[4,2,16,4096]{3,2,1,0:T(8,128)S(1)}, u32[]{:S(2)}, u32[]{:S(2)}) async-start(f32[4,2,16,4096]{3,2,1,0:T(8,128)} %rev.4), calls=%async_computation | async-start | bytes 4194304 | tf_op jit(solution)/shard_map/all_to_all | solution.py:58
  17.7 0.1 fusion.46
  17.8 0.1 cosine_convert_fusion.1
  18.0 0.0 copy-done
  18.0 47.8 %all-to-all-done = f32[4,2,16,4096]{3,2,1,0:T(8,128)S(1)} async-done(((f32[4,2,16,4096]{3,2,1,0:T(8,128)}), f32[4,2,16,4096]{3,2,1,0:T(8,128)S(1)}, u32[]{:S(2)}, u32[]{:S(2)}) %all-to-all-start) | async-done | bytes 2097184 | tf_op jit(solution)/shard_map/all_to_all | solution.py:58
  65.9 0.2 reduce_sum.9
  66.2 0.1 copy_negate_fusion
  66.3 5.7 %fusion.6 = bf16[2,32,16,8,16]{1,4,3,0,2:T(8,128)(2,1)S(1)} fusion(bf16[2,32,16,8,256,1]{4,3,2,1,0,5:T(8,128)(2,1)} %bitcast.85, pred[32,16,8]{0,2,1:T(8,128)(4,1)S(1)} %iota_compare_fusion.5, bf16[1,2,16,16,256]{4,2,1,0,3:T(8,128)(2,1)S(1)} %get-tuple-element.12, bf16[1,2,16,16,256]{4,2,1,0,3:T(8,128)(2,1)S(1)} %get-tuple-element.11), kind=kOutput, calls=%fused_computation.12 | convolution fusion | flops 135528448 | bytes 4984832 | tf_op jit(solution)/shard_map/iajrs,oivjs->oajrv/dot_general | solution.py:69
  72.0 1.2 %copy.62 = bf16[2,32,16,128]{3,2,0,1:T(8,128)(2,1)} copy(bf16[2,32,16,128]{1,3,0,2:T(8,128)(2,1)S(1)} %bitcast.77) | data formatting | bytes 524288 | tf_op jit(solution)/shard_map/reshape | solution.py:80
  73.2 3.4 %all-to-all-start.1 = ((bf16[2,32,16,128]{3,2,0,1:T(8,128)(2,1)}), bf16[2,32,16,128]{3,2,0,1:T(8,128)(2,1)S(1)}, u32[]{:S(2)}, u32[]{:S(2)}) async-start(bf16[2,32,16,128]{3,2,0,1:T(8,128)(2,1)} %copy.62), calls=%async_computation.1 | async-start | bytes 524288 | tf_op jit(solution)/shard_map/all_to_all | solution.py:81
  76.7 1.4 %convolution_convert_fusion.1 = bf16[2560,8]{0,1:T(8,128)(2,1)S(1)} fusion(bf16[160,8]{0,1:T(8,128)(2,1)S(1)} %mul.104, s32[2560]{0:T(1024)S(1)} %get-tuple-element.15), kind=kOutput, calls=%fused_computation.9 | convolution fusion | flops 6983680 | bytes 53760 | tf_op jit(solution)/shard_map/dot_general | solution.py:29
  78.1 4.6 %all-to-all-done.1 = bf16[2,32,16,128]{3,2,0,1:T(8,128)(2,1)S(1)} async-done(((bf16[2,32,16,128]{3,2,0,1:T(8,128)(2,1)}), bf16[2,32,16,128]{3,2,0,1:T(8,128)(2,1)S(1)}, u32[]{:S(2)}, u32[]{:S(2)}) %all-to-all-start.1) | async-done | bytes 262176 | tf_op jit(solution)/shard_map/all_to_all | solution.py:81
  82.7 0.7 copy.83
  83.4 0.5 reshape.537
  83.9 0.1 neg.43
  84.0 0.7 copy.82
  84.6 0.5 reshape.536
  85.2 0.2 maximum_bitcast_fusion.2
  85.4 3.2 %fusion.16 = bf16[2,16,8,256]{3,1,0,2:T(8,128)(2,1)S(1)} fusion(bf16[2,8,64,8,256,1]{4,3,2,1,0,5:T(8,128)(2,1)} %bitcast.86, bf16[1,2,8,64,8,16]{3,5,4,1,0,2:T(8,128)(2,1)S(1)} %get-tuple-element.6, bf16[1,2,8,64,8,16]{3,5,4,1,0,2:T(8,128)(2,1)S(1)} %get-tuple-element.5), kind=kOutput, calls=%fused_computation.17 | convolution fusion | flops 134545408 | bytes 4849664 | tf_op jit(solution)/shard_map/imdlh,oimdlu->oumh/dot_general | solution.py:92
  88.6 0.1 copy.71
  88.7 0.1 convert_element_type.129
  88.8 15.6 %all_gather.3 = bf16[4,2,16,2048]{3,2,1,0:T(8,128)(2,1)S(1)} all-gather(bf16[1,2,16,2048]{3,2,1,0:T(8,128)(2,1)S(1)} %convert_element_type.129), channel_id=1, replica_groups=mesh['groups'=2,'freq'=4,'tile'=4] {'freq'}, dimensions={0}, use_global_device_ids=true | all-gather | bytes 655360 | tf_op jit(solution)/shard_map/all_gather | solution.py:101
  104.4 6.0 %convolution_convert_fusion = bf16[2560,2048]{1,0:T(8,128)(2,1)} fusion(bf16[128,2048]{1,0:T(8,128)(2,1)S(1)} %bitcast.76, bf16[2560,8]{0,1:T(8,128)(2,1)S(1)} %convolution_convert_fusion.1, s32[128]{0:T(128)S(1)} %get-tuple-element.18, s32[2560]{0:T(1024)S(1)} %get-tuple-element.16, s32[128]{0:T(128)S(1)} %get-tuple-element.17), kind=kOutput, calls=%fused_computation | convolution fusion | flops 1353647104 | bytes 11062272 | tf_op jit(solution)/shard_map/dot_general | solution.py:109
  (19 shorter events, 0.3 us)
Async XLA Ops:
  11.2 6.8 %copy-start = (s32[1,32,16]{1,2,0:T(8,128)S(1)}, s32[1,32,16]{1,2,0:T(8,128)}, u32[]{:S(2)}) copy-start(s32[1,32,16]{1,2,0:T(8,128)} %param.7) | copy-start | bytes 6148
  11.2 54.6 %all-to-all-start = ((f32[4,2,16,4096]{3,2,1,0:T(8,128)}), f32[4,2,16,4096]{3,2,1,0:T(8,128)S(1)}, u32[]{:S(2)}, u32[]{:S(2)}) async-start(f32[4,2,16,4096]{3,2,1,0:T(8,128)} %rev.4), calls=%async_computation | async-start | bytes 4194304 | tf_op jit(solution)/shard_map/all_to_all | solution.py:58
  73.2 9.4 %all-to-all-start.1 = ((bf16[2,32,16,128]{3,2,0,1:T(8,128)(2,1)}), bf16[2,32,16,128]{3,2,0,1:T(8,128)(2,1)S(1)}, u32[]{:S(2)}, u32[]{:S(2)}) async-start(bf16[2,32,16,128]{3,2,0,1:T(8,128)(2,1)} %copy.62), calls=%async_computation.1 | async-start | bytes 524288 | tf_op jit(solution)/shard_map/all_to_all | solution.py:81

commit v17 on v14

--- a/solution.py
+++ b/solution.py
@@ -77,11 +77,16 @@
         < ranks[0][:, :, None, None]
     )
     coefficients = jnp.where(rank_mask[None], stacked, jnp.float32(0.0)).astype(jnp.bfloat16)
-    coefficients = coefficients.reshape(2, rows_all, columns, rank_positions * virtual_sources)
-    arrived = lax.all_to_all(coefficients, "tile", split_axis=1, concat_axis=2, tiled=True)
-    rows_local = arrived.shape[1]
-    columns_all = arrived.shape[2]
-    arrived = arrived.reshape(2, rows_local, columns_all, rank_positions, virtual_sources)
+    tile_count = lax.axis_size("tile")
+    rows_local = rows_all // tile_count
+    columns_all = tile_count * columns
+    coefficients = coefficients.reshape(
+        2, tile_count, rows_local, columns, rank_positions * virtual_sources
+    ).transpose(1, 0, 2, 3, 4)
+    arrived = lax.all_to_all(coefficients, "tile", split_axis=0, concat_axis=0, tiled=True)
+    arrived = arrived.transpose(1, 2, 0, 3, 4).reshape(
+        2, rows_local, columns_all, rank_positions, virtual_sources
+    )
     receiver_factors = u_factors[0]
     real_arrived, imag_arrived = arrived[0], arrived[1]
     stacked_arrived = jnp.stack(

time: 111 us -> 115 us (1.036)
  local copies, waits for them, and re-layouts: 5.4 us -> 9.76 us
    convert_element_type x0 -> x1, local copies, waits for them, and re-layouts: none -> 3.52 us  [per_device(): jnp.where(rank_mask[None], stacked, jnp.float32(0.0)).astype(jnp.bfloat16)]
  transfers between devices with their start and end apart: 2 -> 2, of which waited for: 2 -> 2; matrix products, arithmetic and copies ran while one was open for 2% -> 1% of each run, Pallas kernels for 0% -> 0%
where the time goes in v17:
time: 115 us
  waiting for transfers between devices  52.4 us (46%)
  matrix products  25.7 us (22%)
  blocking collectives  15.6 us (14%)
  starting transfers between devices  9.86 us (9%)
  local copies, waits for them, and re-layouts  9.76 us (8%)
    all_to_all x1, waiting for transfers between devices, per_device(): lax.all_to_all(partial[:, ::-1], 'freq', split_axis=0, concat_axis=0, til...  47.8 us
    all_gather x1, blocking collectives, per_device(): piece = lax.all_gather(received, 'freq', axis=0, tiled=True)  15.6 us
    dot_general x1, matrix products, per_device(): jnp.dot(spread_over(forward, virtual_sources), flat_traces, preferred_ele...  8.71 us
    all_to_all x1, starting transfers between devices, per_device(): lax.all_to_all(partial[:, ::-1], 'freq', split_axis=0, concat_axis=0, til...  6.46 us
    dot_general x1, matrix products, per_device(): jnp.dot(spread_over(backward, virtual_sources), piece.reshape(count * 2 *...  5.99 us
    dot_general x1, matrix products, per_device(): jnp.einsum('iajrs,oivjs->oajrv', emitter_factors, stacked_spectrum, prefe...  5.71 us
    all_to_all x1, waiting for transfers between devices, per_device(): lax.all_to_all(coefficients, 'tile', split_axis=0, concat_axis=0, tiled=T...  4.6 us
    convert_element_type x1, local copies, waits for them, and re-layouts, per_device(): jnp.where(rank_mask[None], stacked, jnp.float32(0.0)).astype(jnp.bfloat16)  3.52 us
  transfers between devices with their start and end apart: 2, of which 2 were waited for; matrix products, arithmetic and copies ran while one was open for 1% of the time, Pallas kernels for 0%

profile of v17, /device:TPU:0, one launch (start us, length us, event | category | flops | bytes accessed | tf_op | source)
XLA Modules:
  0.0 114.8 jit_solution(9500581544767455237)
XLA Ops:
  0.0 0.1 fusion.47
  0.1 0.1 cosine_convert_fusion
  0.3 0.7 fusion.5
  1.0 8.7 %fusion.55 = f32[4,2,16,4096]{3,2,1,0:T(8,128)S(1)} fusion(bf16[4,2,16,2560]{3,2,1,0:T(8,128)(2,1)S(1)} %bitcast.79, bf16[2560,4096,1,1]{1,0,3,2:T(8,128)(2,1)} %bitcast.75), kind=kOutput, calls=%fused_computation.85 | convolution fusion | flops 2684354560 | bytes 23724032 | tf_op jit(solution)/shard_map/dot_general | solution.py:55
  9.7 1.5 %rev.4 = f32[4,2,16,4096]{3,2,1,0:T(8,128)} reverse(f32[4,2,16,4096]{3,2,1,0:T(8,128)S(1)} %fusion.55), dimensions={1} | reverse | bytes 4194304 | tf_op jit(solution)/shard_map/rev | solution.py:58
  11.2 0.0 copy-start
  11.2 6.5 %all-to-all-start = ((f32[4,2,16,4096]{3,2,1,0:T(8,128)}), f32[4,2,16,4096]{3,2,1,0:T(8,128)S(1)}, u32[]{:S(2)}, u32[]{:S(2)}) async-start(f32[4,2,16,4096]{3,2,1,0:T(8,128)} %rev.4), calls=%async_computation | async-start | bytes 4194304 | tf_op jit(solution)/shard_map/all_to_all | solution.py:58
  17.7 0.1 fusion.46
  17.8 0.1 cosine_convert_fusion.1
  18.0 0.0 copy-done
  18.0 47.8 %all-to-all-done = f32[4,2,16,4096]{3,2,1,0:T(8,128)S(1)} async-done(((f32[4,2,16,4096]{3,2,1,0:T(8,128)}), f32[4,2,16,4096]{3,2,1,0:T(8,128)S(1)}, u32[]{:S(2)}, u32[]{:S(2)}) %all-to-all-start) | async-done | bytes 2097184 | tf_op jit(solution)/shard_map/all_to_all | solution.py:58
  65.9 0.2 reduce_sum.9
  66.2 0.1 copy_negate_fusion
  66.3 5.7 %fusion.6 = bf16[2,32,16,8,16]{1,4,3,0,2:T(8,128)(2,1)S(1)} fusion(bf16[2,32,16,8,256,1]{4,3,2,1,0,5:T(8,128)(2,1)} %bitcast.85, pred[32,16,8]{0,2,1:T(8,128)(4,1)S(1)} %iota_compare_fusion.5, bf16[1,2,16,16,256]{4,2,1,0,3:T(8,128)(2,1)S(1)} %get-tuple-element.12, bf16[1,2,16,16,256]{4,2,1,0,3:T(8,128)(2,1)S(1)} %get-tuple-element.11), kind=kOutput, calls=%fused_computation.12 | convolution fusion | flops 135528448 | bytes 4984832 | tf_op jit(solution)/shard_map/iajrs,oivjs->oajrv/dot_general | solution.py:69
  72.0 3.5 %copy.63 = bf16[2,32,16,8,16]{4,3,2,1,0:T(8,128)(2,1)S(1)} copy(bf16[2,32,16,8,16]{1,4,3,0,2:T(8,128)(2,1)S(1)} %fusion.6) | data formatting | bytes 524288 | tf_op jit(solution)/shard_map/convert_element_type | solution.py:79
  75.6 1.4 %reshape.527 = bf16[2,4,8,16,128]{4,3,2,1,0:T(8,128)(2,1)S(1)} reshape(bf16[2,32,16,8,16]{4,3,2,1,0:T(8,128)(2,1)S(1)} %copy.63) | data formatting | bytes 524288 | tf_op jit(solution)/shard_map/reshape | solution.py:83
  77.0 0.7 copy.64
  77.7 3.4 %all-to-all-start.1 = ((bf16[4,2,8,16,128]{4,3,2,1,0:T(8,128)(2,1)}), bf16[4,2,8,16,128]{4,3,2,1,0:T(8,128)(2,1)S(1)}, u32[]{:S(2)}, u32[]{:S(2)}) async-start(bf16[4,2,8,16,128]{4,3,2,1,0:T(8,128)(2,1)} %copy.64), calls=%async_computation.1 | async-start | bytes 524288 | tf_op jit(solution)/shard_map/all_to_all | solution.py:86
  81.1 1.4 %convolution_convert_fusion = bf16[2560,8]{0,1:T(8,128)(2,1)S(1)} fusion(bf16[160,8]{0,1:T(8,128)(2,1)S(1)} %reshape.524, s32[2560]{0:T(1024)S(1)} %get-tuple-element.15), kind=kOutput, calls=%fused_computation.9 | convolution fusion | flops 6983680 | bytes 53760 | tf_op jit(solution)/shard_map/dot_general | solution.py:29
  82.5 4.6 %all-to-all-done.1 = bf16[4,2,8,16,128]{4,3,2,1,0:T(8,128)(2,1)S(1)} async-done(((bf16[4,2,8,16,128]{4,3,2,1,0:T(8,128)(2,1)}), bf16[4,2,8,16,128]{4,3,2,1,0:T(8,128)(2,1)S(1)}, u32[]{:S(2)}, u32[]{:S(2)}) %all-to-all-start.1) | async-done | bytes 262176 | tf_op jit(solution)/shard_map/all_to_all | solution.py:86
  87.1 0.6 copy.84
  87.8 0.5 reshape.537
  88.3 0.1 neg.43
  88.4 0.6 copy.83
  89.0 0.5 reshape.536
  89.6 0.2 maximum_bitcast_fusion.2
  89.8 3.2 %fusion.16 = bf16[2,16,8,256]{3,1,0,2:T(8,128)(2,1)S(1)} fusion(bf16[2,8,64,8,256,1]{4,3,2,1,0,5:T(8,128)(2,1)} %bitcast.86, bf16[1,2,8,64,8,16]{3,5,4,1,0,2:T(8,128)(2,1)S(1)} %get-tuple-element.6, bf16[1,2,8,64,8,16]{3,5,4,1,0,2:T(8,128)(2,1)S(1)} %get-tuple-element.5), kind=kOutput, calls=%fused_computation.17 | convolution fusion | flops 134545408 | bytes 4849664 | tf_op jit(solution)/shard_map/imdlh,oimdlu->oumh/dot_general | solution.py:97
  93.0 0.1 copy.72
  93.1 0.1 convert_element_type.129
  93.2 15.6 %all_gather.3 = bf16[4,2,16,2048]{3,2,1,0:T(8,128)(2,1)S(1)} all-gather(bf16[1,2,16,2048]{3,2,1,0:T(8,128)(2,1)S(1)} %convert_element_type.129), channel_id=1, replica_groups=mesh['groups'=2,'freq'=4,'tile'=4] {'freq'}, dimensions={0}, use_global_device_ids=true | all-gather | bytes 655360 | tf_op jit(solution)/shard_map/all_gather | solution.py:106
  108.8 6.0 %multiply_convert_fusion = bf16[2560,2048]{1,0:T(8,128)(2,1)} fusion(bf16[128,2048]{1,0:T(8,128)(2,1)S(1)} %bitcast.76, bf16[2560,8]{0,1:T(8,128)(2,1)S(1)} %convolution_convert_fusion, s32[128]{0:T(128)S(1)} %get-tuple-element.18, s32[2560]{0:T(1024)S(1)} %get-tuple-element.16, s32[128]{0:T(128)S(1)} %get-tuple-element.17), kind=kOutput, calls=%fused_computation | convolution fusion | flops 1358889984 | bytes 11062272 | tf_op jit(solution)/shard_map/dot_general | solution.py:110
  (18 shorter events, 0.3 us)
Async XLA Ops:
  11.2 6.8 %copy-start = (s32[1,32,16]{1,2,0:T(8,128)S(1)}, s32[1,32,16]{1,2,0:T(8,128)}, u32[]{:S(2)}) copy-start(s32[1,32,16]{1,2,0:T(8,128)} %param.7) | copy-start | bytes 6148
  11.2 54.6 %all-to-all-start = ((f32[4,2,16,4096]{3,2,1,0:T(8,128)}), f32[4,2,16,4096]{3,2,1,0:T(8,128)S(1)}, u32[]{:S(2)}, u32[]{:S(2)}) async-start(f32[4,2,16,4096]{3,2,1,0:T(8,128)} %rev.4), calls=%async_computation | async-start | bytes 4194304 | tf_op jit(solution)/shard_map/all_to_all | solution.py:58
  77.7 9.4 %all-to-all-start.1 = ((bf16[4,2,8,16,128]{4,3,2,1,0:T(8,128)(2,1)}), bf16[4,2,8,16,128]{4,3,2,1,0:T(8,128)(2,1)S(1)}, u32[]{:S(2)}, u32[]{:S(2)}) async-start(bf16[4,2,8,16,128]{4,3,2,1,0:T(8,128)(2,1)} %copy.64), calls=%async_computation.1 | async-start | bytes 524288 | tf_op jit(solution)/shard_map/all_to_all | solution.py:86
